TPU v7x, 128 devices: a whole 4x4x4 slice. The times are simulated.
128 devices in a mesh: lon: 8 (over x, core), lat: 16 (over y, z).
Axes of the slice: x: 4, y: 4, z: 4, core: 2. Of those that a mesh axis runs over, the one named last changes fastest.
Arguments:
- tracers: float32 [2, 20, 1024, 3072], P(None, None, 'lat', 'lon'), may hold values from -6 to 6
- east_velocity: bfloat16 [20, 1024, 3072], P(None, 'lat', 'lon'), may hold values from -3 to 3
- north_velocity: bfloat16 [20, 1024, 3072], P(None, 'lat', 'lon'), may hold values from -3 to 3
- vertical_diffusivity: bfloat16 [20, 1024, 3072], P(None, 'lat', 'lon'), may hold values from 0.049804688 to 5
- depth_levels: int32 [1024, 3072], P('lat', 'lon'), may hold values from 0 to 20
- ocean_blocks: int32 [32, 16], P('lat', 'lon'), may hold values 0 or 1
- forcing: float32 [1024, 3072], P('lat', 'lon'), may hold values from -6 to 6
- surface_coupling: float32 [1024, 3072], P('lat', 'lon'), may hold values from 0.1 to 2
Outputs:
- new_tracers: float32 [2, 20, 1024, 3072], P(None, None, 'lat', 'lon')
- surface_solution: float32 [1024, 3072], P('lat', 'lon')
All inputs are finite; a program needn't handle non-finite values. No bound on the sum of `ocean_blocks` on one device may be relied on, other than what follows from the above.
Results may differ from a plain program's by a relative error of at most 0.0003.
Values sent between devices are 32-bit elements; how exact they have to be, the bound alone decides.
No kernel may reach another device: no remote copies, remote signals or barrier semaphores. Data moves between devices by JAX's collectives and lax.ppermute only.
A program may use at most 192 MiB of HBM per device.

v0:
```python
import jax
import jax.numpy as jnp
from jax import lax
from jax.sharding import PartitionSpec as P
from jax.experimental import pallas as pl
from jax.experimental.pallas import tpu as pltpu

ITERS = 3


advection_rate = 0.25
biharmonic_rate = 0.01
corner_weight = 0.5


def extended_2(block, sides, width, periodic):
    for axis, dim in sides:
        count = lax.axis_size(axis)
        forward = [(i, i + 1) for i in range(count - 1)]
        if periodic:
            forward.append((count - 1, 0))
        backward = [(target, source) for source, target in forward]
        low = lax.ppermute(
            lax.slice_in_dim(block, block.shape[dim] - width, None, axis=dim), axis, forward
        )
        high = lax.ppermute(lax.slice_in_dim(block, 0, width, axis=dim), axis, backward)
        block = jnp.concatenate([low, block, high], axis=dim)
    return block


def from_partner(block, axis, stride):
    count = lax.axis_size(axis)
    route = []
    for low in range(count):
        high = low | 1 << stride
        if high != low and high < count:
            route += [(low, high), (high, low)]
    return lax.ppermute(block, axis, route)


def passed_along(value, axis, steps):
    count = lax.axis_size(axis)
    pairs = [(source, (source + steps) % count) for source in range(count)]
    return lax.ppermute(value, axis, pairs)


def shifted(shard, axis, by):
    count = lax.axis_size(axis)
    pairs = [(i, i + by) for i in range(count) if 0 <= i + by < count]
    return lax.ppermute(shard, axis, pairs)


def window(array, shift_row, shift_col):
    inner_height = array.shape[-2] - 2
    inner_width = array.shape[-1] - 2
    return array[..., shift_row : shift_row + inner_height, shift_col : shift_col + inner_width]


def masked_laplacian(values, wet_mask):
    centre = window(values, 1, 1)
    running = jnp.zeros_like(centre)
    for shift_row, shift_col in ((0, 1), (2, 1), (1, 0), (1, 2)):
        running = running + window(wet_mask, shift_row, shift_col) * (
            window(values, shift_row, shift_col) - centre
        )
    return window(wet_mask, 1, 1) * running


def face_flux(speed_one, speed_two, tracer_one, tracer_two, wet_one, wet_two):
    return 0.5 * (speed_one + speed_two) * 0.5 * (tracer_one + tracer_two) * wet_one * wet_two


def baroclinic(padded):
    tracer = padded[0:2]
    wet_mask = padded[2]
    inner_tracer = tracer[..., 1:-1, 1:-1]
    inner_mask = wet_mask[..., 1:-1, 1:-1]
    east_speed = padded[3][..., 1:-1, 1:-1]
    north_speed = padded[4][..., 1:-1, 1:-1]
    lap_one = masked_laplacian(tracer, wet_mask)
    lap_two = masked_laplacian(lap_one, inner_mask)
    centre = window(inner_tracer, 1, 1)
    wet_centre = window(inner_mask, 1, 1)
    east_flux = face_flux(
        window(east_speed, 1, 1),
        window(east_speed, 1, 2),
        centre,
        window(inner_tracer, 1, 2),
        wet_centre,
        window(inner_mask, 1, 2),
    )
    west_flux = face_flux(
        window(east_speed, 1, 0),
        window(east_speed, 1, 1),
        window(inner_tracer, 1, 0),
        centre,
        window(inner_mask, 1, 0),
        wet_centre,
    )
    north_flux = face_flux(
        window(north_speed, 1, 1),
        window(north_speed, 2, 1),
        centre,
        window(inner_tracer, 2, 1),
        wet_centre,
        window(inner_mask, 2, 1),
    )
    south_flux = face_flux(
        window(north_speed, 0, 1),
        window(north_speed, 1, 1),
        window(inner_tracer, 0, 1),
        centre,
        window(inner_mask, 0, 1),
        wet_centre,
    )
    divergence = east_flux - west_flux + north_flux - south_flux
    return wet_centre * (centre - advection_rate * divergence - biharmonic_rate * lap_two)


def stencil_kernel(ext_ref, out_ref):
    height, width = ext_ref.shape[2], ext_ref.shape[3]
    row_count, col_count = out_ref.shape[2], out_ref.shape[3]

    def south(x):
        return pltpu.roll(x, 1, 0)

    def north(x):
        return pltpu.roll(x, height - 1, 0)

    def west(x):
        return pltpu.roll(x, 1, 1)

    def east(x):
        return pltpu.roll(x, width - 1, 1)

    shifts = (south, north, west, east)
    wet = ext_ref[2, 0]
    wet_near = [shift(wet) for shift in shifts]

    def laplacian(values):
        running = None
        for shift, wet_n in zip(shifts, wet_near):
            term = wet_n * (shift(values) - values)
            running = term if running is None else running + term
        return wet * running

    east_speed = ext_ref[3, 0]
    north_speed = ext_ref[4, 0]
    east_mean = 0.5 * (east_speed + east(east_speed))
    north_mean = 0.5 * (north_speed + north(north_speed))
    for t in range(out_ref.shape[0]):
        tracer = ext_ref[t, 0]
        lap_two = laplacian(laplacian(tracer))
        east_flux = east_mean * 0.5 * (tracer + east(tracer)) * wet * wet_near[3]
        north_flux = north_mean * 0.5 * (tracer + north(tracer)) * wet * wet_near[1]
        divergence = east_flux - west(east_flux) + north_flux - south(north_flux)
        result = wet * (tracer - advection_rate * divergence - biharmonic_rate * lap_two)
        out_ref[t, 0] = result[:row_count, :col_count]


def wrapped_layout(padded):
    rows = padded.shape[2] - 4
    cols = padded.shape[3] - 4
    height = -(-(rows + 4) // 8) * 8
    width = -(-(cols + 4) // 128) * 128
    lead = padded.shape[:2]
    by_rows = jnp.concatenate(
        [
            padded[:, :, 2 : rows + 4],
            jnp.zeros(lead + (height - rows - 4, padded.shape[3]), padded.dtype),
            padded[:, :, 0:2],
        ],
        axis=2,
    )
    return jnp.concatenate(
        [
            by_rows[..., 2 : cols + 4],
            jnp.zeros(lead + (height, width - cols - 4), padded.dtype),
            by_rows[..., 0:2],
        ],
        axis=3,
    )


def baroclinic_kernel(padded):
    tracer_count = 2
    level_count = padded.shape[1]
    rows = padded.shape[2] - 4
    cols = padded.shape[3] - 4
    ext = wrapped_layout(padded)
    height, width = ext.shape[2], ext.shape[3]
    return pl.pallas_call(
        stencil_kernel,
        grid=(level_count,),
        in_specs=[pl.BlockSpec((ext.shape[0], 1, height, width), lambda k: (0, k, 0, 0))],
        out_specs=pl.BlockSpec((tracer_count, 1, rows, cols), lambda k: (0, k, 0, 0)),
        out_shape=jax.ShapeDtypeStruct((tracer_count, level_count, rows, cols), jnp.float32),
    )(ext)


def mix_kernel(values_ref, wet_ref, diff_ref, out_ref, ratio_ref):
    level_count = wet_ref.shape[0]
    tracer_count = values_ref.shape[0]

    def coupling(k):
        return diff_ref[k].astype(jnp.float32) * wet_ref[k] * wet_ref[k - 1]

    below = coupling(1)
    upper = None
    reduced = [None] * tracer_count
    for k in range(level_count):
        above = below
        below = coupling(k + 1) if k + 1 < level_count else None
        if k == 0:
            diagonal = 1.0 + below
            divisor = diagonal
        elif below is None:
            diagonal = 1.0 + above
            divisor = diagonal + above * upper
        else:
            diagonal = 1.0 + above + below
            divisor = diagonal + above * upper
        if below is not None:
            upper = -below / divisor
            ratio_ref[k] = upper
        for t in range(tracer_count):
            if k == 0:
                source = values_ref[t, 0]
            else:
                source = values_ref[t, k] + above * reduced[t]
            reduced[t] = source / divisor
            out_ref[t, k] = reduced[t]
    result = reduced
    for k in range(level_count - 2, -1, -1):
        ratio = ratio_ref[k]
        for t in range(tracer_count):
            result[t] = out_ref[t, k] - ratio * result[t]
            out_ref[t, k] = result[t]


def vertical_mix(values, wet_mask, diffusivity):
    tracer_count, level_count, row_count, col_count = values.shape
    rows = 16 if row_count % 16 == 0 else row_count
    return pl.pallas_call(
        mix_kernel,
        grid=(row_count // rows,),
        in_specs=[
            pl.BlockSpec((tracer_count, level_count, rows, col_count), lambda i: (0, 0, i, 0)),
            pl.BlockSpec((level_count, rows, col_count), lambda i: (0, i, 0)),
            pl.BlockSpec((level_count, rows, col_count), lambda i: (0, i, 0)),
        ],
        out_specs=pl.BlockSpec((tracer_count, level_count, rows, col_count), lambda i: (0, 0, i, 0)),
        out_shape=jax.ShapeDtypeStruct(values.shape, jnp.float32),
        scratch_shapes=[pltpu.VMEM((level_count - 1, rows, col_count), jnp.float32)],
    )(values, wet_mask, diffusivity)


def nine_point(padded, wet_surface, centre_weight):
    centre = window(padded, 1, 1)
    edges = (
        window(padded, 0, 1) + window(padded, 2, 1) + window(padded, 1, 0) + window(padded, 1, 2)
    )
    corners = (
        window(padded, 0, 0) + window(padded, 0, 2) + window(padded, 2, 0) + window(padded, 2, 2)
    )
    return wet_surface * (centre_weight * centre - edges - corner_weight * corners)


def clinic_extend(stacked, fold_signs):
    row_count = stacked.shape[2]
    widened = extended_2(stacked, (("lon", 3),), 2, True)
    extended = extended_2(widened, (("lat", 2),), 2, False)
    top_rows = widened[:, :, row_count - 2 :, :]
    for bit in range(lax.axis_size("lon").bit_length() - 1):
        top_rows = from_partner(top_rows, "lon", bit)
    northern = jnp.flip(top_rows, axis=(2, 3)) * fold_signs
    at_top = lax.axis_index("lat") == lax.axis_size("lat") - 1
    ghost_rows = jnp.where(at_top, northern, extended[:, :, row_count + 2 :, :])
    return jnp.concatenate([extended[:, :, : row_count + 2, :], ghost_rows], axis=2)


def strip_pad(surface_field):
    lon_index = lax.axis_index("lon")
    lon_count = lax.axis_size("lon")
    first_row = surface_field[0:1, :]
    last_row = surface_field[-1:, :]
    following = passed_along(first_row, "lon", -1)
    following_far = shifted(following, "lat", -1)
    preceding = passed_along(last_row, "lon", 1)
    preceding_far = shifted(preceding, "lat", 1)
    above_row = jnp.where(lon_index == lon_count - 1, following_far, following)
    below_row = jnp.where(lon_index == 0, preceding_far, preceding)
    top_strip = jnp.logical_and(
        lon_index == lon_count - 1, lax.axis_index("lat") == lax.axis_size("lat") - 1
    )
    above_row = jnp.where(top_strip, jnp.flip(last_row, axis=1), above_row)
    extended = jnp.concatenate([below_row, surface_field, above_row], axis=0)
    return jnp.concatenate([extended[:, -1:], extended, extended[:, :1]], axis=1)


def butterfly_sum(value):
    for axis in ("lon", "lat"):
        count = lax.axis_size(axis)
        bit = 1
        while bit < count:
            value = value + lax.ppermute(value, axis, [(i, i ^ bit) for i in range(count)])
            bit <<= 1
    return value


def solve(surface_source, wet_surface, centre_weight, padder):

    def precondition(residual):
        return wet_surface * residual / centre_weight

    def apply_operator(field):
        return nine_point(padder(field), wet_surface, centre_weight)

    solution = jnp.zeros_like(surface_source)
    residual = surface_source
    precond = precondition(residual)
    direction = precond
    operator_image = apply_operator(direction)
    totals = butterfly_sum(
        jnp.stack([jnp.sum(residual * precond), jnp.sum(direction * operator_image)])
    )
    resid_dot, curvature = totals[0], totals[1]
    for iteration in range(ITERS):
        step_size = resid_dot / curvature
        solution = solution + step_size * direction
        if iteration + 1 < ITERS:
            residual = residual - step_size * operator_image
            precond = precondition(residual)
            precond_image = apply_operator(precond)
            totals = butterfly_sum(
                jnp.stack(
                    [
                        jnp.sum(residual * precond),
                        jnp.sum(precond * precond_image),
                        jnp.sum(precond * operator_image),
                    ]
                )
            )
            dot_next = totals[0]
            ratio = dot_next / resid_dot
            direction = precond + ratio * direction
            curvature = totals[1] + 2.0 * ratio * totals[2] + ratio * ratio * curvature
            operator_image = precond_image + ratio * operator_image
            resid_dot = dot_next
    return solution


def shards(
    tracers,
    east_velocity,
    north_velocity,
    vertical_diffusivity,
    depth_levels,
    ocean_blocks,
    forcing,
    surface_coupling,
):
    level_count = tracers.shape[1]
    row_count = tracers.shape[2]
    col_count = tracers.shape[3]
    ocean_cells = jnp.repeat(
        jnp.repeat(ocean_blocks, row_count // ocean_blocks.shape[0], axis=0),
        col_count // ocean_blocks.shape[1],
        axis=1,
    ).astype(jnp.float32)
    level_index = lax.broadcasted_iota(jnp.int32, (level_count, row_count, col_count), 0)
    wet_mask = jnp.where(
        level_index < depth_levels[None], ocean_cells[None], jnp.zeros_like(ocean_cells)[None]
    )
    east_float = east_velocity.astype(jnp.float32)
    north_float = north_velocity.astype(jnp.float32)
    stacked = jnp.concatenate(
        [tracers, wet_mask[None], east_float[None], north_float[None]], axis=0
    )
    fold_signs = jnp.array([1.0, 1.0, 1.0, -1.0, -1.0], jnp.float32).reshape(5, 1, 1, 1)
    padded = clinic_extend(stacked, fold_signs)
    provisional = baroclinic_kernel(padded)
    new_tracers = vertical_mix(provisional, wet_mask, vertical_diffusivity)
    wet_surface = wet_mask[0]
    surface_source = wet_surface * (forcing + jnp.mean(new_tracers[0] - new_tracers[1], axis=0))
    centre_weight = 6.0 + surface_coupling
    relaid = lax.all_to_all(
        jnp.stack([surface_source, wet_surface, centre_weight]),
        "lon",
        split_axis=1,
        concat_axis=2,
        tiled=True,
    )
    strip_solution = solve(relaid[0], relaid[1], relaid[2], strip_pad)
    solution = lax.all_to_all(strip_solution, "lon", split_axis=1, concat_axis=0, tiled=True)
    return (new_tracers, solution)


def solution(mesh):
    placed = (
        P(None, None, "lat", "lon"),
        P(None, "lat", "lon"),
        P(None, "lat", "lon"),
        P(None, "lat", "lon"),
        P("lat", "lon"),
        P("lat", "lon"),
        P("lat", "lon"),
        P("lat", "lon"),
    )
    return jax.shard_map(
        shards,
        mesh=mesh,
        in_specs=placed,
        out_specs=(P(None, None, "lat", "lon"), P("lat", "lon")),
        check_vma=False,
    )
```

profile of v0, /device:TPU:1, one launch (start us, length us, event | category | flops | bytes accessed | tf_op | source)
XLA Modules:
  0.0 311.4 jit_solution(8982341768870124897)
XLA Ops:
  4.3 3.9 %pad_maximum_fusion.5 = (f32[5,20,64,2]{3,2,1,0:T(8,128)}, f32[5,20,64,2]{3,2,1,0:T(8,128)}) fusion(f32[1,20,64,384]{3,2,1,0:T(8,128)S(1)} %get-tuple-element.43, f32[1,20,64,384]{3,2,1,0:T(8,128)S(1)} %get-tuple-element.44, f32[1,20,64,384]{3,2,1,0:T(8,128)S(1)} %fusion.1, f32[2,20,64,384]{3,2,1,0:T(8,128)S(1)} %copy-done), kind=kLoop, calls=%fused_computation.5 | loop fusion | flops 76800 | bytes 9932800 | tf_op jit(solution)/shard_map/slice | solution.py:24
  8.3 2.6 copy.22
  10.8 2.6 collective-permute-start
  13.4 2.6 copy.23
  16.0 2.4 copy.24
  20.1 2.3 copy.25
  22.4 4.1 %pad_maximum_fusion.6 = (f32[5,20,2,388]{3,2,1,0:T(2,128)}, f32[5,20,2,388]{3,2,1,0:T(2,128)}) fusion(f32[5,20,64,2]{3,2,1,0:T(8,128)} %copy.25, f32[5,20,64,2]{3,2,1,0:T(8,128)} %copy.24, f32[1,20,64,384]{3,2,1,0:T(8,128)S(1)} %get-tuple-element.43, f32[1,20,64,384]{3,2,1,0:T(8,128)} %copy-done.1, f32[1,20,64,384]{3,2,1,0:T(8,128)} %copy-done.2, ...), kind=kLoop, calls=%fused_computation.14 | loop fusion | flops 776000 | bytes 10553600 | tf_op jit(solution)/shard_map/concatenate | solution.py:27
  30.9 8.5 %collective-permute-done.3 = f32[5,20,2,388]{3,2,1,0:T(2,128)} collective-permute-done((f32[5,20,2,388]{3,2,1,0:T(2,128)S(1)}, f32[5,20,2,388]{3,2,1,0:T(2,128)}, u32[]{:S(2)}, u32[]{:S(2)}) %collective-permute-start.3) | collective-permute-done | bytes 310432 | tf_op jit(solution)/shard_map/ppermute | solution.py:38
  39.4 2.5 collective-permute-start.4
  43.3 3.7 %collective-permute-start.6 = (f32[5,20,2,388]{3,2,1,0:T(2,128)}, f32[5,20,2,388]{3,2,1,0:T(2,128)S(1)}, u32[]{:S(2)}, u32[]{:S(2)}) collective-permute-start(f32[5,20,2,388]{3,2,1,0:T(2,128)} %get-tuple-element.16), channel_id=1, source_target_pairs={{0,1},{1,2},{2,3},{3,4},{4,5},{5,6},{6,7},{7,8},{8,9},{9,10},{10,1... | collective-permute-start | bytes 931208 | tf_op jit(solution)/shard_map/ppermute | solution.py:23
  47.3 3.9 %collective-permute-done.4 = f32[5,20,2,388]{3,2,1,0:T(2,128)S(1)} collective-permute-done((f32[5,20,2,388]{3,2,1,0:T(2,128)}, f32[5,20,2,388]{3,2,1,0:T(2,128)S(1)}, u32[]{:S(2)}, u32[]{:S(2)}) %collective-permute-start.4) | collective-permute-done | bytes 310432 | tf_op jit(solution)/shard_map/ppermute | solution.py:38
  54.7 14.8 %pad_maximum_fusion = f32[5,20,72,388]{3,2,1,0:T(8,128)} fusion(f32[5,20,2,388]{3,2,1,0:T(2,128)S(1)} %collective-permute-done.6, f32[5,20,2,388]{3,2,1,0:T(2,128)S(1)} %multiply_select_fusion, f32[5,20,64,2]{3,2,1,0:T(8,128)} %copy.25, f32[1,20,64,384]{3,2,1,0:T(8,128)S(1)} %get-tuple-element.43, f32[1,20,64,384]{3,2,1,0:T(8,128)} %copy-done.1, ...), kind=kLoop, calls=%fused_computation | loop fusion | flops 22348800 | bytes 21728288 | tf_op jit(solution)/shard_map/concatenate | solution.py:167
  69.6 14.3 %slice.252 = f32[5,20,72,386]{3,2,1,0:T(8,128)} slice(f32[5,20,72,388]{3,2,1,0:T(8,128)} %pad_maximum_fusion), slice={[0:5], [0:20], [0:72], [2:388]} | slice | bytes 22233600 | tf_op jit(solution)/shard_map/slice | solution.py:177
  83.8 2.0 slice-done
  85.9 11.3 %pad_maximum_fusion.1.ext_ref = f32[5,20,72,512]{3,2,1,0:T(8,128)} fusion(f32[5,20,72,2]{3,2,1,0:T(8,128)S(1)} %slice-done, f32[5,20,72,386]{3,2,1,0:T(8,128)} %slice.252, f32[512]{0:T(512)S(1)} %pad.57.clone), kind=kLoop, calls=%fused_computation.1 | loop fusion | flops 7372800 | bytes 25922048 | tf_op jit(solution)/shard_map/concatenate | solution.py:175
  97.1 21.0 %shard_map.104.values_ref = f32[2,20,64,384]{3,2,1,0:T(8,128)} custom-call(f32[5,20,72,512]{3,2,1,0:T(8,128)} %pad_maximum_fusion.1.ext_ref), custom_call_target="tpu_custom_call" | custom-call | tf_op jit(solution)/shard_map/pallas_call | solution.py:192
  118.1 5.7 %shard_map.105 = f32[2,20,64,384]{3,2,1,0:T(8,128)} custom-call(f32[2,20,64,384]{3,2,1,0:T(8,128)} %shard_map.104.values_ref, f32[20,64,384]{2,1,0:T(8,128)} %fusion.2.wet_ref, bf16[20,64,384]{2,1,0:T(8,128)(2,1)} %diff_ref.1), custom_call_target="tpu_custom_call" | custom-call | tf_op jit(solution)/shard_map/pallas_call | solution.py:244
  123.8 2.5 fusion
  126.8 13.5 %all_to_all.34 = f32[3,64,384]{2,0,1:T(4,128)S(1)} all-to-all(f32[3,64,384]{2,0,1:T(4,128)S(1)} %copy.26), channel_id=1, replica_groups=mesh['lon'=8,'lat'=16] {'lon'}, dimensions={1} | all-to-all | bytes 589824 | tf_op jit(solution)/shard_map/all_to_all | solution.py:387
  143.1 3.6 %collective-permute-start.8 = (f32[1,3072]{1,0:T(1,128)S(1)}, f32[1,3072]{1,0:T(1,128)S(1)}, u32[]{:S(2)}, u32[]{:S(2)}) collective-permute-start(f32[1,3072]{1,0:T(1,128)S(1)} %collective-permute-done.7), channel_id=1, source_target_pairs={{0,1},{1,2},{2,3},{3,4},{4,5},{5,6},{6,7},{7,8},{8,9},{9,10},{10,1... | collective-permute-start | bytes 36872 | tf_op jit(solution)/shard_map/ppermute | solution.py:50
  146.8 2.1 rev.15
  150.2 3.3 %collective-permute-done.10 = f32[1,3072]{1,0:T(1,128)S(1)} collective-permute-done((f32[1,3072]{1,0:T(1,128)S(1)}, f32[1,3072]{1,0:T(1,128)S(1)}, u32[]{:S(2)}, u32[]{:S(2)}) %collective-permute-start.10) | collective-permute-done | bytes 12320 | tf_op jit(solution)/shard_map/ppermute | solution.py:50
  155.9 4.6 %collective-permute-start.11 = (f32[2]{0:T(128)S(1)}, f32[2]{0:T(128)S(1)}, u32[]{:S(2)}, u32[]{:S(2)}) collective-permute-start(f32[2]{0:T(128)S(1)} %pad_maximum_fusion.31), channel_id=1, source_target_pairs={{0,16},{16,0},{32,48},{48,32},{64,80},{80,64},{96,112},{112,96},{1... | collective-permute-start | bytes 32 | tf_op jit(solution)/shard_map/ppermute | solution.py:306
  162.7 2.4 collective-permute-done.12
  166.4 3.9 %collective-permute-done.13 = f32[2]{0:T(128)S(1)} collective-permute-done((f32[2]{0:T(128)S(1)}, f32[2]{0:T(128)S(1)}, u32[]{:S(2)}, u32[]{:S(2)}) %collective-permute-start.13) | collective-permute-done | bytes 40 | tf_op jit(solution)/shard_map/ppermute | solution.py:306
  173.0 5.4 %collective-permute-start.15 = (f32[2]{0:T(128)S(1)}, f32[2]{0:T(128)S(1)}, u32[]{:S(2)}, u32[]{:S(2)}) collective-permute-start(f32[2]{0:T(128)S(1)} %add.165), channel_id=1, source_target_pairs={{0,2},{1,3},{2,0},{3,1},{4,6},{5,7},{6,4},{7,5},{8,10},{9,11},{10,... | collective-permute-start | bytes 32 | tf_op jit(solution)/shard_map/ppermute | solution.py:306
  181.7 2.9 collective-permute-start.17
  187.6 6.3 %collective-permute-start.18 = (f32[1,3072]{1,0:T(1,128)S(1)}, f32[1,3072]{1,0:T(1,128)S(1)}, u32[]{:S(2)}, u32[]{:S(2)}) collective-permute-start(f32[1,3072]{1,0:T(1,128)S(1)} %get-tuple-element.32), channel_id=1, source_target_pairs={{0,16},{16,32},{32,48},{48,64},{64,80},{80,96},{96,112},{112,0},{1... | collective-permute-start | bytes 36872 | tf_op jit(solution)/shard_map/ppermute | solution.py:44
  195.0 3.0 collective-permute-start.19
  198.0 2.1 rev.16
  201.5 3.4 %collective-permute-done.21 = f32[1,3072]{1,0:T(1,128)S(1)} collective-permute-done((f32[1,3072]{1,0:T(1,128)S(1)}, f32[1,3072]{1,0:T(1,128)S(1)}, u32[]{:S(2)}, u32[]{:S(2)}) %collective-permute-start.21) | collective-permute-done | bytes 12320 | tf_op jit(solution)/shard_map/ppermute | solution.py:50
  207.8 4.8 %collective-permute-start.22 = (f32[3]{0:T(128)S(1)}, f32[3]{0:T(128)S(1)}, u32[]{:S(2)}, u32[]{:S(2)}) collective-permute-start(f32[3]{0:T(128)S(1)} %pad_maximum_fusion.32), channel_id=1, source_target_pairs={{0,16},{16,0},{32,48},{48,32},{64,80},{80,64},{96,112},{112,96},{1... | collective-permute-start | bytes 44 | tf_op jit(solution)/shard_map/ppermute | solution.py:306
  215.4 2.4 collective-permute-done.23
  219.7 3.9 %collective-permute-done.24 = f32[3]{0:T(128)S(1)} collective-permute-done((f32[3]{0:T(128)S(1)}, f32[3]{0:T(128)S(1)}, u32[]{:S(2)}, u32[]{:S(2)}) %collective-permute-start.24) | collective-permute-done | bytes 44 | tf_op jit(solution)/shard_map/ppermute | solution.py:306
  226.4 4.0 %collective-permute-start.26 = (f32[3]{0:T(128)S(1)}, f32[3]{0:T(128)S(1)}, u32[]{:S(2)}, u32[]{:S(2)}) collective-permute-start(f32[3]{0:T(128)S(1)} %add.178), channel_id=1, source_target_pairs={{0,2},{1,3},{2,0},{3,1},{4,6},{5,7},{6,4},{7,5},{8,10},{9,11},{10,... | collective-permute-start | bytes 44 | tf_op jit(solution)/shard_map/ppermute | solution.py:306
  233.8 2.8 collective-permute-start.28
  242.2 6.3 %collective-permute-start.29 = (f32[1,3072]{1,0:T(1,128)S(1)}, f32[1,3072]{1,0:T(1,128)S(1)}, u32[]{:S(2)}, u32[]{:S(2)}) collective-permute-start(f32[1,3072]{1,0:T(1,128)S(1)} %get-tuple-element.30), channel_id=1, source_target_pairs={{0,16},{16,32},{32,48},{48,64},{64,80},{80,96},{96,112},{112,0},{1... | collective-permute-start | bytes 36872 | tf_op jit(solution)/shard_map/ppermute | solution.py:44
  249.6 3.0 collective-permute-start.30
  252.6 2.1 rev.17
  256.1 3.4 %collective-permute-done.32 = f32[1,3072]{1,0:T(1,128)S(1)} collective-permute-done((f32[1,3072]{1,0:T(1,128)S(1)}, f32[1,3072]{1,0:T(1,128)S(1)}, u32[]{:S(2)}, u32[]{:S(2)}) %collective-permute-start.32) | collective-permute-done | bytes 12320 | tf_op jit(solution)/shard_map/ppermute | solution.py:50
  262.6 4.8 %collective-permute-start.33 = (f32[3]{0:T(128)S(1)}, f32[3]{0:T(128)S(1)}, u32[]{:S(2)}, u32[]{:S(2)}) collective-permute-start(f32[3]{0:T(128)S(1)} %pad_maximum_fusion.33), channel_id=1, source_target_pairs={{0,16},{16,0},{32,48},{48,32},{64,80},{80,64},{96,112},{112,96},{1... | collective-permute-start | bytes 44 | tf_op jit(solution)/shard_map/ppermute | solution.py:306
  268.2 2.0 fusion.35
  270.3 2.4 collective-permute-done.34
  272.7 2.0 fusion.38
  274.7 3.9 %collective-permute-done.35 = f32[3]{0:T(128)S(1)} collective-permute-done((f32[3]{0:T(128)S(1)}, f32[3]{0:T(128)S(1)}, u32[]{:S(2)}, u32[]{:S(2)}) %collective-permute-start.35) | collective-permute-done | bytes 44 | tf_op jit(solution)/shard_map/ppermute | solution.py:306
  281.4 4.0 %collective-permute-start.37 = (f32[3]{0:T(128)S(1)}, f32[3]{0:T(128)S(1)}, u32[]{:S(2)}, u32[]{:S(2)}) collective-permute-start(f32[3]{0:T(128)S(1)} %add.196), channel_id=1, source_target_pairs={{0,2},{1,3},{2,0},{3,1},{4,6},{5,7},{6,4},{7,5},{8,10},{9,11},{10,... | collective-permute-start | bytes 44 | tf_op jit(solution)/shard_map/ppermute | solution.py:306
  288.8 2.6 collective-permute-start.39
  296.7 14.0 %all_to_all.35 = f32[8,8,384]{2,0,1:T(8,128)S(1)} all-to-all(f32[8,8,384]{2,0,1:T(8,128)S(1)} %bitcast.70), channel_id=1, replica_groups=mesh['lon'=8,'lat'=16] {'lon'}, dimensions={1} | all-to-all | bytes 196608 | tf_op jit(solution)/shard_map/all_to_all | solution.py:395
  (138 shorter events, 66.0 us)
Async XLA Ops:
  0.6 3.0 copy-start.4
  3.6 4.6 %copy-start.1 = (f32[1,20,64,384]{3,2,1,0:T(8,128)}, f32[1,20,64,384]{3,2,1,0:T(8,128)S(1)}, u32[]{:S(2)}) copy-start(f32[1,20,64,384]{3,2,1,0:T(8,128)S(1)} %get-tuple-element.44) | copy-start | bytes 5898244
  3.8 4.4 %copy-start.2 = (f32[1,20,64,384]{3,2,1,0:T(8,128)}, f32[1,20,64,384]{3,2,1,0:T(8,128)S(1)}, u32[]{:S(2)}) copy-start(f32[1,20,64,384]{3,2,1,0:T(8,128)S(1)} %fusion.1) | copy-start | bytes 5898244
  10.8 5.2 %collective-permute-start = (f32[5,20,64,2]{2,3,1,0:T(2,128)S(1)}, f32[5,20,64,2]{2,3,1,0:T(2,128)S(1)}, u32[]{:S(2)}, u32[]{:S(2)}) collective-permute-start(f32[5,20,64,2]{2,3,1,0:T(2,128)S(1)} %copy.22), channel_id=1, source_target_pairs={{0,16},{16,32},{32,48},{48,64},{64,80},{80,96},{96,112},{112,0},{1... | collective-permute-start | bytes 153608 | tf_op jit(solution)/shard_map/ppermute | solution.py:23
  16.0 4.1 %collective-permute-start.1 = (f32[5,20,64,2]{2,3,1,0:T(2,128)S(1)}, f32[5,20,64,2]{2,3,1,0:T(2,128)S(1)}, u32[]{:S(2)}, u32[]{:S(2)}) collective-permute-start(f32[5,20,64,2]{2,3,1,0:T(2,128)S(1)} %copy.23), channel_id=1, source_target_pairs={{16,0},{32,16},{48,32},{64,48},{80,64},{96,80},{112,96},{0,112},{1... | collective-permute-start | bytes 153608 | tf_op jit(solution)/shard_map/ppermute | solution.py:26
  22.4 24.7 %copy-start.5 = (f32[64,384]{1,0:T(8,128)S(1)}, f32[64,384]{1,0:T(8,128)}, u32[]{:S(2)}) copy-start(f32[64,384]{1,0:T(8,128)} %param.16) | copy-start | bytes 294916
  26.5 26.4 %copy-start.7 = (f32[5]{0:T(128)S(1)}, f32[5]{0:T(128)}, u32[]{:S(2)}) copy-start(f32[5]{0:T(128)} %constant.31.clone) | copy-start | bytes 64
  26.5 2.0 collective-permute-start.2
  28.4 11.0 %collective-permute-start.3 = (f32[5,20,2,388]{3,2,1,0:T(2,128)S(1)}, f32[5,20,2,388]{3,2,1,0:T(2,128)}, u32[]{:S(2)}, u32[]{:S(2)}) collective-permute-start(f32[5,20,2,388]{3,2,1,0:T(2,128)S(1)} %collective-permute-done.2), channel_id=1, source_target_pairs={{0,32},{32,0},{16,48},{48,16},{64,96},{96,64},{80,112},{112,80},{1... | collective-permute-start | bytes 931208 | tf_op jit(solution)/shard_map/ppermute | solution.py:38
  29.6 23.3 %collective-permute-start.5 = (f32[5,20,2,388]{3,2,1,0:T(2,128)}, f32[5,20,2,388]{3,2,1,0:T(2,128)}, u32[]{:S(2)}, u32[]{:S(2)}) collective-permute-start(f32[5,20,2,388]{3,2,1,0:T(2,128)} %get-tuple-element.15), channel_id=1, source_target_pairs={{1,0},{2,1},{3,2},{4,3},{5,4},{6,5},{7,6},{8,7},{9,8},{10,9},{11,1... | collective-permute-start | bytes 931208 | tf_op jit(solution)/shard_map/ppermute | solution.py:26
  39.4 11.7 %collective-permute-start.4 = (f32[5,20,2,388]{3,2,1,0:T(2,128)}, f32[5,20,2,388]{3,2,1,0:T(2,128)S(1)}, u32[]{:S(2)}, u32[]{:S(2)}) collective-permute-start(f32[5,20,2,388]{3,2,1,0:T(2,128)} %collective-permute-done.3), channel_id=1, source_target_pairs={{0,64},{64,0},{16,80},{80,16},{32,96},{96,32},{48,112},{112,48},{1... | collective-permute-start | bytes 931208 | tf_op jit(solution)/shard_map/ppermute | solution.py:38
  43.3 11.4 %collective-permute-start.6 = (f32[5,20,2,388]{3,2,1,0:T(2,128)}, f32[5,20,2,388]{3,2,1,0:T(2,128)S(1)}, u32[]{:S(2)}, u32[]{:S(2)}) collective-permute-start(f32[5,20,2,388]{3,2,1,0:T(2,128)} %get-tuple-element.16), channel_id=1, source_target_pairs={{0,1},{1,2},{2,3},{3,4},{4,5},{5,6},{6,7},{7,8},{8,9},{9,10},{10,1... | collective-permute-start | bytes 931208 | tf_op jit(solution)/shard_map/ppermute | solution.py:23
  123.7 2.7 copy-start.3
  123.8 2.7 copy-start.6
  123.8 2.7 slice-start.1
  141.2 1.9 collective-permute-start.7
  142.3 6.6 %collective-permute-start.9 = (f32[1,3072]{1,0:T(1,128)S(1)}, f32[1,3072]{1,0:T(1,128)S(1)}, u32[]{:S(2)}, u32[]{:S(2)}) collective-permute-start(f32[1,3072]{1,0:T(1,128)S(1)} %get-tuple-element.33), channel_id=1, source_target_pairs={{0,112},{16,0},{32,16},{48,32},{64,48},{80,64},{96,80},{112,96},{1... | collective-permute-start | bytes 36872 | tf_op jit(solution)/shard_map/ppermute | solution.py:44
  143.1 7.1 %collective-permute-start.8 = (f32[1,3072]{1,0:T(1,128)S(1)}, f32[1,3072]{1,0:T(1,128)S(1)}, u32[]{:S(2)}, u32[]{:S(2)}) collective-permute-start(f32[1,3072]{1,0:T(1,128)S(1)} %collective-permute-done.7), channel_id=1, source_target_pairs={{0,1},{1,2},{2,3},{3,4},{4,5},{5,6},{6,7},{7,8},{8,9},{9,10},{10,1... | collective-permute-start | bytes 36872 | tf_op jit(solution)/shard_map/ppermute | solution.py:50
  148.9 4.6 %collective-permute-start.10 = (f32[1,3072]{1,0:T(1,128)S(1)}, f32[1,3072]{1,0:T(1,128)S(1)}, u32[]{:S(2)}, u32[]{:S(2)}) collective-permute-start(f32[1,3072]{1,0:T(1,128)S(1)} %collective-permute-done.9), channel_id=1, source_target_pairs={{1,0},{2,1},{3,2},{4,3},{5,4},{6,5},{7,6},{8,7},{9,8},{10,9},{11,1... | collective-permute-start | bytes 36872 | tf_op jit(solution)/shard_map/ppermute | solution.py:50
  155.9 5.4 %collective-permute-start.11 = (f32[2]{0:T(128)S(1)}, f32[2]{0:T(128)S(1)}, u32[]{:S(2)}, u32[]{:S(2)}) collective-permute-start(f32[2]{0:T(128)S(1)} %pad_maximum_fusion.31), channel_id=1, source_target_pairs={{0,16},{16,0},{32,48},{48,32},{64,80},{80,64},{96,112},{112,96},{1... | collective-permute-start | bytes 32 | tf_op jit(solution)/shard_map/ppermute | solution.py:306
  162.6 2.4 collective-permute-start.12
  166.4 3.9 %collective-permute-start.13 = (f32[2]{0:T(128)S(1)}, f32[2]{0:T(128)S(1)}, u32[]{:S(2)}, u32[]{:S(2)}) collective-permute-start(f32[2]{0:T(128)S(1)} %fusion.40), channel_id=1, source_target_pairs={{0,64},{16,80},{32,96},{48,112},{64,0},{80,16},{96,32},{112,48},{1... | collective-permute-start | bytes 32 | tf_op jit(solution)/shard_map/ppermute | solution.py:306
  170.4 2.6 collective-permute-start.14
  173.0 6.3 %collective-permute-start.15 = (f32[2]{0:T(128)S(1)}, f32[2]{0:T(128)S(1)}, u32[]{:S(2)}, u32[]{:S(2)}) collective-permute-start(f32[2]{0:T(128)S(1)} %add.165), channel_id=1, source_target_pairs={{0,2},{1,3},{2,0},{3,1},{4,6},{5,7},{6,4},{7,5},{8,10},{9,11},{10,... | collective-permute-start | bytes 32 | tf_op jit(solution)/shard_map/ppermute | solution.py:306
  179.3 2.4 collective-permute-start.16
  181.7 3.9 %collective-permute-start.17 = (f32[2]{0:T(128)S(1)}, f32[2]{0:T(128)S(1)}, u32[]{:S(2)}, u32[]{:S(2)}) collective-permute-start(f32[2]{0:T(128)S(1)} %add.167), channel_id=1, source_target_pairs={{0,8},{1,9},{2,10},{3,11},{4,12},{5,13},{6,14},{7,15},{8,0},{9,1},... | collective-permute-start | bytes 32 | tf_op jit(solution)/shard_map/ppermute | solution.py:306
  187.6 7.4 %collective-permute-start.18 = (f32[1,3072]{1,0:T(1,128)S(1)}, f32[1,3072]{1,0:T(1,128)S(1)}, u32[]{:S(2)}, u32[]{:S(2)}) collective-permute-start(f32[1,3072]{1,0:T(1,128)S(1)} %get-tuple-element.32), channel_id=1, source_target_pairs={{0,16},{16,32},{32,48},{48,64},{64,80},{80,96},{96,112},{112,0},{1... | collective-permute-start | bytes 36872 | tf_op jit(solution)/shard_map/ppermute | solution.py:44
  193.9 6.2 %collective-permute-start.20 = (f32[1,3072]{1,0:T(1,128)S(1)}, f32[1,3072]{1,0:T(1,128)S(1)}, u32[]{:S(2)}, u32[]{:S(2)}) collective-permute-start(f32[1,3072]{1,0:T(1,128)S(1)} %get-tuple-element.31), channel_id=1, source_target_pairs={{0,112},{16,0},{32,16},{48,32},{64,48},{80,64},{96,80},{112,96},{1... | collective-permute-start | bytes 36872 | tf_op jit(solution)/shard_map/ppermute | solution.py:44
  195.0 6.4 %collective-permute-start.19 = (f32[1,3072]{1,0:T(1,128)S(1)}, f32[1,3072]{1,0:T(1,128)S(1)}, u32[]{:S(2)}, u32[]{:S(2)}) collective-permute-start(f32[1,3072]{1,0:T(1,128)S(1)} %collective-permute-done.18), channel_id=1, source_target_pairs={{0,1},{1,2},{2,3},{3,4},{4,5},{5,6},{6,7},{7,8},{8,9},{9,10},{10,1... | collective-permute-start | bytes 36872 | tf_op jit(solution)/shard_map/ppermute | solution.py:50
  200.1 4.8 %collective-permute-start.21 = (f32[1,3072]{1,0:T(1,128)S(1)}, f32[1,3072]{1,0:T(1,128)S(1)}, u32[]{:S(2)}, u32[]{:S(2)}) collective-permute-start(f32[1,3072]{1,0:T(1,128)S(1)} %collective-permute-done.20), channel_id=1, source_target_pairs={{1,0},{2,1},{3,2},{4,3},{5,4},{6,5},{7,6},{8,7},{9,8},{10,9},{11,1... | collective-permute-start | bytes 36872 | tf_op jit(solution)/shard_map/ppermute | solution.py:50
  207.8 5.6 %collective-permute-start.22 = (f32[3]{0:T(128)S(1)}, f32[3]{0:T(128)S(1)}, u32[]{:S(2)}, u32[]{:S(2)}) collective-permute-start(f32[3]{0:T(128)S(1)} %pad_maximum_fusion.32), channel_id=1, source_target_pairs={{0,16},{16,0},{32,48},{48,32},{64,80},{80,64},{96,112},{112,96},{1... | collective-permute-start | bytes 44 | tf_op jit(solution)/shard_map/ppermute | solution.py:306
  215.4 2.4 collective-permute-start.23
  219.7 3.9 %collective-permute-start.24 = (f32[3]{0:T(128)S(1)}, f32[3]{0:T(128)S(1)}, u32[]{:S(2)}, u32[]{:S(2)}) collective-permute-start(f32[3]{0:T(128)S(1)} %fusion.39), channel_id=1, source_target_pairs={{0,64},{16,80},{32,96},{48,112},{64,0},{80,16},{96,32},{112,48},{1... | collective-permute-start | bytes 44 | tf_op jit(solution)/shard_map/ppermute | solution.py:306
  223.7 2.7 collective-permute-start.25
  226.4 5.0 %collective-permute-start.26 = (f32[3]{0:T(128)S(1)}, f32[3]{0:T(128)S(1)}, u32[]{:S(2)}, u32[]{:S(2)}) collective-permute-start(f32[3]{0:T(128)S(1)} %add.178), channel_id=1, source_target_pairs={{0,2},{1,3},{2,0},{3,1},{4,6},{5,7},{6,4},{7,5},{8,10},{9,11},{10,... | collective-permute-start | bytes 44 | tf_op jit(solution)/shard_map/ppermute | solution.py:306
  231.4 2.4 collective-permute-start.27
  233.8 3.9 %collective-permute-start.28 = (f32[3]{0:T(128)S(1)}, f32[3]{0:T(128)S(1)}, u32[]{:S(2)}, u32[]{:S(2)}) collective-permute-start(f32[3]{0:T(128)S(1)} %add.180), channel_id=1, source_target_pairs={{0,8},{1,9},{2,10},{3,11},{4,12},{5,13},{6,14},{7,15},{8,0},{9,1},... | collective-permute-start | bytes 44 | tf_op jit(solution)/shard_map/ppermute | solution.py:306
  242.2 7.4 %collective-permute-start.29 = (f32[1,3072]{1,0:T(1,128)S(1)}, f32[1,3072]{1,0:T(1,128)S(1)}, u32[]{:S(2)}, u32[]{:S(2)}) collective-permute-start(f32[1,3072]{1,0:T(1,128)S(1)} %get-tuple-element.30), channel_id=1, source_target_pairs={{0,16},{16,32},{32,48},{48,64},{64,80},{80,96},{96,112},{112,0},{1... | collective-permute-start | bytes 36872 | tf_op jit(solution)/shard_map/ppermute | solution.py:44
  248.5 6.2 %collective-permute-start.31 = (f32[1,3072]{1,0:T(1,128)S(1)}, f32[1,3072]{1,0:T(1,128)S(1)}, u32[]{:S(2)}, u32[]{:S(2)}) collective-permute-start(f32[1,3072]{1,0:T(1,128)S(1)} %get-tuple-element.29), channel_id=1, source_target_pairs={{0,112},{16,0},{32,16},{48,32},{64,48},{80,64},{96,80},{112,96},{1... | collective-permute-start | bytes 36872 | tf_op jit(solution)/shard_map/ppermute | solution.py:44
  249.6 6.4 %collective-permute-start.30 = (f32[1,3072]{1,0:T(1,128)S(1)}, f32[1,3072]{1,0:T(1,128)S(1)}, u32[]{:S(2)}, u32[]{:S(2)}) collective-permute-start(f32[1,3072]{1,0:T(1,128)S(1)} %collective-permute-done.29), channel_id=1, source_target_pairs={{0,1},{1,2},{2,3},{3,4},{4,5},{5,6},{6,7},{7,8},{8,9},{9,10},{10,1... | collective-permute-start | bytes 36872 | tf_op jit(solution)/shard_map/ppermute | solution.py:50
  254.7 4.8 %collective-permute-start.32 = (f32[1,3072]{1,0:T(1,128)S(1)}, f32[1,3072]{1,0:T(1,128)S(1)}, u32[]{:S(2)}, u32[]{:S(2)}) collective-permute-start(f32[1,3072]{1,0:T(1,128)S(1)} %collective-permute-done.31), channel_id=1, source_target_pairs={{1,0},{2,1},{3,2},{4,3},{5,4},{6,5},{7,6},{8,7},{9,8},{10,9},{11,1... | collective-permute-start | bytes 36872 | tf_op jit(solution)/shard_map/ppermute | solution.py:50
  262.6 5.6 %collective-permute-start.33 = (f32[3]{0:T(128)S(1)}, f32[3]{0:T(128)S(1)}, u32[]{:S(2)}, u32[]{:S(2)}) collective-permute-start(f32[3]{0:T(128)S(1)} %pad_maximum_fusion.33), channel_id=1, source_target_pairs={{0,16},{16,0},{32,48},{48,32},{64,80},{80,64},{96,112},{112,96},{1... | collective-permute-start | bytes 44 | tf_op jit(solution)/shard_map/ppermute | solution.py:306
  270.2 2.4 collective-permute-start.34
  274.7 3.9 %collective-permute-start.35 = (f32[3]{0:T(128)S(1)}, f32[3]{0:T(128)S(1)}, u32[]{:S(2)}, u32[]{:S(2)}) collective-permute-start(f32[3]{0:T(128)S(1)} %fusion.38), channel_id=1, source_target_pairs={{0,64},{16,80},{32,96},{48,112},{64,0},{80,16},{96,32},{112,48},{1... | collective-permute-start | bytes 44 | tf_op jit(solution)/shard_map/ppermute | solution.py:306
  278.7 2.7 collective-permute-start.36
  281.4 5.0 %collective-permute-start.37 = (f32[3]{0:T(128)S(1)}, f32[3]{0:T(128)S(1)}, u32[]{:S(2)}, u32[]{:S(2)}) collective-permute-start(f32[3]{0:T(128)S(1)} %add.196), channel_id=1, source_target_pairs={{0,2},{1,3},{2,0},{3,1},{4,6},{5,7},{6,4},{7,5},{8,10},{9,11},{10,... | collective-permute-start | bytes 44 | tf_op jit(solution)/shard_map/ppermute | solution.py:306
  286.4 2.4 collective-permute-start.38
  288.8 3.9 %collective-permute-start.39 = (f32[3]{0:T(128)S(1)}, f32[3]{0:T(128)S(1)}, u32[]{:S(2)}, u32[]{:S(2)}) collective-permute-start(f32[3]{0:T(128)S(1)} %add.198), channel_id=1, source_target_pairs={{0,8},{1,9},{2,10},{3,11},{4,12},{5,13},{6,14},{7,15},{8,0},{9,1},... | collective-permute-start | bytes 44 | tf_op jit(solution)/shard_map/ppermute | solution.py:306
  (2 other events, 4.7 us)
where the time goes:
time: 313 us; the launch traced here: 311 us
  starting transfers between devices  84.4 us (27%)
  waiting for transfers between devices  62.8 us (20%)
  other arithmetic  62.2 us (20%)
  local copies, waits for them, and re-layouts  38.3 us (12%)
  blocking collectives  27.6 us (9%)
  Pallas kernels  26.6 us (8%)
  between operations  9.54 us (3%)
    ppermute x21, starting transfers between devices, butterfly_sum(): lax.ppermute(value, axis, [(i, i ^ bit) for i in range(count)])  45 us
    ppermute x21, waiting for transfers between devices, butterfly_sum(): lax.ppermute(value, axis, [(i, i ^ bit) for i in range(count)])  34.1 us
    pallas_call x1, Pallas kernels, baroclinic_kernel(): pl.pallas_call(stencil_kernel, grid=(level_count,), in_specs=[pl.BlockSpe...  21 us
    concatenate x1, other arithmetic, wrapped_layout(): jnp.concatenate([padded[:, :, 2:rows + 4], jnp.zeros(lead + (height - row...  14.8 us
    ppermute x6, starting transfers between devices, passed_along(): return lax.ppermute(value, axis, pairs)  14.5 us
    ppermute x3, waiting for transfers between devices, from_partner(): return lax.ppermute(block, axis, route)  14.3 us
    slice x1, local copies, waits for them, and re-layouts, wrapped_layout(): by_rows[..., 2:cols + 4]  14.3 us
    all_to_all x1, blocking collectives, shards(): lax.all_to_all(strip_solution, 'lon', split_axis=1, concat_axis=0, tiled=...  14 us
  transfers between devices with their start and end apart: 40, of which 32 were waited for; matrix products, arithmetic and copies ran while one was open for 5% of the time, Pallas kernels for 0%

commit v1 on v0

--- a/solution.py
+++ b/solution.py
@@ -182,12 +182,9 @@
     )
 
 
-def baroclinic_kernel(padded):
+def stencil_call(ext, rows, cols):
     tracer_count = 2
-    level_count = padded.shape[1]
-    rows = padded.shape[2] - 4
-    cols = padded.shape[3] - 4
-    ext = wrapped_layout(padded)
+    level_count = ext.shape[1]
     height, width = ext.shape[2], ext.shape[3]
     return pl.pallas_call(
         stencil_kernel,
@@ -266,6 +263,39 @@
     return wet_surface * (centre_weight * centre - edges - corner_weight * corners)
 
 
+def wrapped_extend(stacked, fold_signs):
+    rows, cols = stacked.shape[2], stacked.shape[3]
+    height = -(-(rows + 4) // 8) * 8
+    width = -(-(cols + 4) // 128) * 128
+    lead = stacked.shape[:2]
+    lon_count = lax.axis_size("lon")
+    lat_count = lax.axis_size("lat")
+    east_halo = lax.ppermute(
+        stacked[..., :2], "lon", [(i, (i - 1) % lon_count) for i in range(lon_count)]
+    )
+    west_halo = lax.ppermute(
+        stacked[..., cols - 2 :], "lon", [(i, (i + 1) % lon_count) for i in range(lon_count)]
+    )
+    widened = jnp.concatenate(
+        [stacked, east_halo, jnp.zeros(lead + (rows, width - cols - 4), stacked.dtype), west_halo],
+        axis=3,
+    )
+    north_rows = lax.ppermute(widened[:, :, :2], "lat", [(j, j - 1) for j in range(1, lat_count)])
+    south_rows = lax.ppermute(
+        widened[:, :, rows - 2 :], "lat", [(j, j + 1) for j in range(lat_count - 1)]
+    )
+    mirrored = lax.ppermute(
+        widened[:, :, rows - 2 :], "lon", [(i, lon_count - 1 - i) for i in range(lon_count)]
+    )
+    folded = jnp.roll(jnp.flip(mirrored, axis=(2, 3)), cols - width, axis=3) * fold_signs
+    at_top = lax.axis_index("lat") == lat_count - 1
+    north = jnp.where(at_top, folded, north_rows)
+    return jnp.concatenate(
+        [widened, north, jnp.zeros(lead + (height - rows - 4, width), stacked.dtype), south_rows],
+        axis=2,
+    )
+
+
 def clinic_extend(stacked, fold_signs):
     row_count = stacked.shape[2]
     widened = extended_2(stacked, (("lon", 3),), 2, True)
@@ -378,8 +408,7 @@
         [tracers, wet_mask[None], east_float[None], north_float[None]], axis=0
     )
     fold_signs = jnp.array([1.0, 1.0, 1.0, -1.0, -1.0], jnp.float32).reshape(5, 1, 1, 1)
-    padded = clinic_extend(stacked, fold_signs)
-    provisional = baroclinic_kernel(padded)
+    provisional = stencil_call(wrapped_extend(stacked, fold_signs), row_count, col_count)
     new_tracers = vertical_mix(provisional, wet_mask, vertical_diffusivity)
     wet_surface = wet_mask[0]
     surface_source = wet_surface * (forcing + jnp.mean(new_tracers[0] - new_tracers[1], axis=0))

time: 313 us -> 276 us (0.88)
  other arithmetic: 62.2 us -> 46.7 us
  waiting for transfers between devices: 62.8 us -> 48.6 us
  local copies, waits for them, and re-layouts: 38.3 us -> 26.7 us
  starting transfers between devices: 84.4 us -> 90 us
    ppermute x7 -> x5, waiting for transfers between devices: 16.3 us -> 2.15 us  [the longest x1 1.09 us: wrapped_extend(): lax.ppermute(widened[:, :, rows - 2:], 'lat', [(j, j + 1) for j in range(...]
    concatenate x3 -> x2, other arithmetic: 30.2 us -> 16.4 us  [the longest x1 12.7 us: wrapped_extend(): jnp.concatenate([widened, north, jnp.zeros(lead + (height - rows - 4, wid...]
    slice x5 -> x6, local copies, waits for them, and re-layouts: 21.4 us -> 8.77 us  [the longest x4 3.66 us: wrapped_extend(): jnp.roll(jnp.flip(mirrored, axis=(2, 3)), cols - width, axis=3) * fold_signs]
    ppermute x21, starting transfers between devices: 45 us -> 49.1 us  [butterfly_sum(): lax.ppermute(value, axis, [(i, i ^ bit) for i in range(count)])]
    ppermute x7 -> x5, starting transfers between devices: 11.3 us -> 12.2 us  [the longest x1 4.94 us: wrapped_extend(): lax.ppermute(widened[:, :, rows - 2:], 'lat', [(j, j + 1) for j in range(...]
  transfers between devices with their start and end apart: 40 -> 38, of which waited for: 32 -> 30; matrix products, arithmetic and copies ran while one was open for 5% -> 6% of each run, Pallas kernels for 0% -> 0%
where the time goes in v1:
time: 276 us; the launch traced here: 274 us
  starting transfers between devices  90 us (33%)
  waiting for transfers between devices  48.6 us (18%)
  other arithmetic  46.7 us (17%)
  local copies, waits for them, and re-layouts  26.7 us (10%)
  Pallas kernels  26.6 us (10%)
  blocking collectives  26.2 us (9%)
  between operations  9.37 us (3%)
    ppermute x21, starting transfers between devices, butterfly_sum(): lax.ppermute(value, axis, [(i, i ^ bit) for i in range(count)])  49.1 us
    ppermute x21, waiting for transfers between devices, butterfly_sum(): lax.ppermute(value, axis, [(i, i ^ bit) for i in range(count)])  34.1 us
    pallas_call x1, Pallas kernels, stencil_call(): pl.pallas_call(stencil_kernel, grid=(level_count,), in_specs=[pl.BlockSpe...  21 us
    ppermute x6, starting transfers between devices, passed_along(): return lax.ppermute(value, axis, pairs)  14.5 us
    ppermute x6, starting transfers between devices, shifted(): return lax.ppermute(shard, axis, pairs)  14.3 us
    all_to_all x1, blocking collectives, shards(): lax.all_to_all(strip_solution, 'lon', split_axis=1, concat_axis=0, tiled=...  14 us
    concatenate x1, other arithmetic, wrapped_extend(): jnp.concatenate([widened, north, jnp.zeros(lead + (height - rows - 4, wid...  12.7 us
    all_to_all x1, blocking collectives, shards(): lax.all_to_all(jnp.stack([surface_source, wet_surface, centre_weight]), '...  12.2 us
  transfers between devices with their start and end apart: 38, of which 30 were waited for; matrix products, arithmetic and copies ran while one was open for 6% of the time, Pallas kernels for 0%

profile of v1, /device:TPU:1, one launch (start us, length us, event | category | flops | bytes accessed | tf_op | source)
XLA Modules:
  0.0 274.2 jit_solution(5462289795025894551)
XLA Ops:
  1.6 2.0 bitcast_convert_fusion
  4.3 3.9 %pad_maximum_fusion.4 = (f32[5,20,64,2]{3,2,1,0:T(8,128)}, f32[5,20,64,2]{3,2,1,0:T(8,128)}) fusion(f32[1,20,64,384]{3,2,1,0:T(8,128)S(1)} %get-tuple-element.43, f32[1,20,64,384]{3,2,1,0:T(8,128)S(1)} %get-tuple-element.44, f32[1,20,64,384]{3,2,1,0:T(8,128)S(1)} %fusion.1, f32[2,20,64,384]{3,2,1,0:T(8,128)S(1)} %copy-done), kind=kLoop, calls=%fused_computation.4 | loop fusion | flops 76800 | bytes 9932800 | tf_op jit(solution)/shard_map/slice | solution.py:274
  8.3 2.6 copy.22
  12.2 2.6 copy.23
  16.0 2.3 copy.24
  18.4 2.3 copy.25
  22.2 3.7 %pad_maximum_fusion.5 = (f32[5,20,2,512]{3,2,1,0:T(2,128)S(1)}, f32[5,20,2,512]{3,2,1,0:T(2,128)S(1)}) fusion(f32[5,20,64,2]{3,2,1,0:T(8,128)} %copy.25, f32[5,20,64,124]{3,2,1,0:T(8,128)S(1)} %broadcast_in_dim.55, f32[5,20,64,2]{3,2,1,0:T(8,128)} %copy.24, f32[1,20,64,384]{3,2,1,0:T(8,128)S(1)} %get-tuple-element.43, f32[1,20,64,384]{3,2,1,0:T(8,128)S(1)} %copy-done.2, ...), kind=kLoop, calls=%fused_computation.13 | loop fusion | flops 1228800 | bytes 13926400 | tf_op jit(solution)/shard_map/concatenate | solution.py:279
  26.0 3.3 %collective-permute-start.2 = (f32[5,20,2,512]{3,2,1,0:T(2,128)S(1)}, f32[5,20,2,512]{3,2,1,0:T(2,128)}, u32[]{:S(2)}, u32[]{:S(2)}) collective-permute-start(f32[5,20,2,512]{3,2,1,0:T(2,128)S(1)} %get-tuple-element.16), channel_id=1, source_target_pairs={{0,112},{16,96},{32,80},{48,64},{64,48},{80,32},{96,16},{112,0},{1... | collective-permute-start | bytes 1228808 | tf_op jit(solution)/shard_map/ppermute | solution.py:287
  32.2 4.9 %collective-permute-start.4 = (f32[5,20,2,512]{3,2,1,0:T(2,128)S(1)}, f32[5,20,2,512]{3,2,1,0:T(2,128)}, u32[]{:S(2)}, u32[]{:S(2)}) collective-permute-start(f32[5,20,2,512]{3,2,1,0:T(2,128)S(1)} %get-tuple-element.16), channel_id=1, source_target_pairs={{0,1},{1,2},{2,3},{3,4},{4,5},{5,6},{6,7},{7,8},{8,9},{9,10},{10,1... | collective-permute-start | bytes 1228808 | tf_op jit(solution)/shard_map/ppermute | solution.py:284
  44.3 12.7 %pad_maximum_fusion.ext_ref = f32[5,20,72,512]{3,2,1,0:T(8,128)} fusion(f32[5,20,2,512]{3,2,1,0:T(2,128)} %collective-permute-done.4, f32[5,20,2,512]{3,2,1,0:T(2,128)S(1)} %fusion.3, f32[5,20,64,2]{3,2,1,0:T(8,128)} %copy.25, f32[5,20,64,124]{3,2,1,0:T(8,128)} %copy-done.4, f32[5,20,64,2]{3,2,1,0:T(8,128)} %copy.24, ...), kind=kLoop, calls=%fused_computation | loop fusion | flops 33177600 | bytes 28672288 | tf_op jit(solution)/shard_map/concatenate | solution.py:293
  57.0 21.0 %shard_map.104.values_ref = f32[2,20,64,384]{3,2,1,0:T(8,128)} custom-call(f32[5,20,72,512]{3,2,1,0:T(8,128)} %pad_maximum_fusion.ext_ref), custom_call_target="tpu_custom_call" | custom-call | tf_op jit(solution)/shard_map/pallas_call | solution.py:189
  78.0 5.7 %shard_map.105 = f32[2,20,64,384]{3,2,1,0:T(8,128)} custom-call(f32[2,20,64,384]{3,2,1,0:T(8,128)} %shard_map.104.values_ref, f32[20,64,384]{2,1,0:T(8,128)} %copy-done.5, bf16[20,64,384]{2,1,0:T(8,128)(2,1)} %diff_ref.1), custom_call_target="tpu_custom_call" | custom-call | tf_op jit(solution)/shard_map/pallas_call | solution.py:241
  83.6 2.5 fusion
  86.6 12.2 %all_to_all.34 = f32[3,64,384]{2,0,1:T(4,128)S(1)} all-to-all(f32[3,64,384]{2,0,1:T(4,128)S(1)} %copy.26), channel_id=1, replica_groups=mesh['lon'=8,'lat'=16] {'lon'}, dimensions={1} | all-to-all | bytes 589824 | tf_op jit(solution)/shard_map/all_to_all | solution.py:416
  101.7 4.2 %collective-permute-start.6 = (f32[1,3072]{1,0:T(1,128)S(1)}, f32[1,3072]{1,0:T(1,128)S(1)}, u32[]{:S(2)}, u32[]{:S(2)}) collective-permute-start(f32[1,3072]{1,0:T(1,128)S(1)} %collective-permute-done.5), channel_id=1, source_target_pairs={{0,1},{1,2},{2,3},{3,4},{4,5},{5,6},{6,7},{7,8},{8,9},{9,10},{10,1... | collective-permute-start | bytes 36872 | tf_op jit(solution)/shard_map/ppermute | solution.py:50
  105.9 2.1 rev.12
  109.3 3.3 %collective-permute-done.8 = f32[1,3072]{1,0:T(1,128)S(1)} collective-permute-done((f32[1,3072]{1,0:T(1,128)S(1)}, f32[1,3072]{1,0:T(1,128)S(1)}, u32[]{:S(2)}, u32[]{:S(2)}) %collective-permute-start.8) | collective-permute-done | bytes 12320 | tf_op jit(solution)/shard_map/ppermute | solution.py:50
  114.9 4.6 %collective-permute-start.9 = (f32[2]{0:T(128)S(1)}, f32[2]{0:T(128)S(1)}, u32[]{:S(2)}, u32[]{:S(2)}) collective-permute-start(f32[2]{0:T(128)S(1)} %pad_maximum_fusion.31), channel_id=1, source_target_pairs={{0,16},{16,0},{32,48},{48,32},{64,80},{80,64},{96,112},{112,96},{1... | collective-permute-start | bytes 32 | tf_op jit(solution)/shard_map/ppermute | solution.py:336
  121.6 2.4 collective-permute-done.10
  125.3 3.9 %collective-permute-done.11 = f32[2]{0:T(128)S(1)} collective-permute-done((f32[2]{0:T(128)S(1)}, f32[2]{0:T(128)S(1)}, u32[]{:S(2)}, u32[]{:S(2)}) %collective-permute-start.11) | collective-permute-done | bytes 40 | tf_op jit(solution)/shard_map/ppermute | solution.py:336
  129.3 2.5 collective-permute-start.12
  132.7 8.6 %collective-permute-start.13 = (f32[2]{0:T(128)S(1)}, f32[2]{0:T(128)S(1)}, u32[]{:S(2)}, u32[]{:S(2)}) collective-permute-start(f32[2]{0:T(128)S(1)} %add.165), channel_id=1, source_target_pairs={{0,2},{1,3},{2,0},{3,1},{4,6},{5,7},{6,4},{7,5},{8,10},{9,11},{10,... | collective-permute-start | bytes 32 | tf_op jit(solution)/shard_map/ppermute | solution.py:336
  144.7 2.9 %collective-permute-start.15 = (f32[2]{0:T(128)S(1)}, f32[2]{0:T(128)S(1)}, u32[]{:S(2)}, u32[]{:S(2)}) collective-permute-start(f32[2]{0:T(128)S(1)} %add.167), channel_id=1, source_target_pairs={{0,8},{1,9},{2,10},{3,11},{4,12},{5,13},{6,14},{7,15},{8,0},{9,1},... | collective-permute-start | bytes 32 | tf_op jit(solution)/shard_map/ppermute | solution.py:336
  150.5 6.3 %collective-permute-start.16 = (f32[1,3072]{1,0:T(1,128)S(1)}, f32[1,3072]{1,0:T(1,128)S(1)}, u32[]{:S(2)}, u32[]{:S(2)}) collective-permute-start(f32[1,3072]{1,0:T(1,128)S(1)} %get-tuple-element.32), channel_id=1, source_target_pairs={{0,16},{16,32},{32,48},{48,64},{64,80},{80,96},{96,112},{112,0},{1... | collective-permute-start | bytes 36872 | tf_op jit(solution)/shard_map/ppermute | solution.py:44
  157.9 3.2 %collective-permute-start.17 = (f32[1,3072]{1,0:T(1,128)S(1)}, f32[1,3072]{1,0:T(1,128)S(1)}, u32[]{:S(2)}, u32[]{:S(2)}) collective-permute-start(f32[1,3072]{1,0:T(1,128)S(1)} %collective-permute-done.16), channel_id=1, source_target_pairs={{0,1},{1,2},{2,3},{3,4},{4,5},{5,6},{6,7},{7,8},{8,9},{9,10},{10,1... | collective-permute-start | bytes 36872 | tf_op jit(solution)/shard_map/ppermute | solution.py:50
  161.1 2.1 rev.13
  164.6 3.4 %collective-permute-done.19 = f32[1,3072]{1,0:T(1,128)S(1)} collective-permute-done((f32[1,3072]{1,0:T(1,128)S(1)}, f32[1,3072]{1,0:T(1,128)S(1)}, u32[]{:S(2)}, u32[]{:S(2)}) %collective-permute-start.19) | collective-permute-done | bytes 12320 | tf_op jit(solution)/shard_map/ppermute | solution.py:50
  169.0 2.0 pad_maximum_fusion.32
  171.0 4.8 %collective-permute-start.20 = (f32[3]{0:T(128)S(1)}, f32[3]{0:T(128)S(1)}, u32[]{:S(2)}, u32[]{:S(2)}) collective-permute-start(f32[3]{0:T(128)S(1)} %pad_maximum_fusion.32), channel_id=1, source_target_pairs={{0,16},{16,0},{32,48},{48,32},{64,80},{80,64},{96,112},{112,96},{1... | collective-permute-start | bytes 44 | tf_op jit(solution)/shard_map/ppermute | solution.py:336
  176.7 2.0 fusion.37
  178.7 2.4 collective-permute-done.21
  181.1 2.0 fusion.40
  183.1 3.9 %collective-permute-done.22 = f32[3]{0:T(128)S(1)} collective-permute-done((f32[3]{0:T(128)S(1)}, f32[3]{0:T(128)S(1)}, u32[]{:S(2)}, u32[]{:S(2)}) %collective-permute-start.22) | collective-permute-done | bytes 44 | tf_op jit(solution)/shard_map/ppermute | solution.py:336
  189.7 4.0 %collective-permute-start.24 = (f32[3]{0:T(128)S(1)}, f32[3]{0:T(128)S(1)}, u32[]{:S(2)}, u32[]{:S(2)}) collective-permute-start(f32[3]{0:T(128)S(1)} %add.178), channel_id=1, source_target_pairs={{0,2},{1,3},{2,0},{3,1},{4,6},{5,7},{6,4},{7,5},{8,10},{9,11},{10,... | collective-permute-start | bytes 44 | tf_op jit(solution)/shard_map/ppermute | solution.py:336
  197.2 2.8 %collective-permute-start.26 = (f32[3]{0:T(128)S(1)}, f32[3]{0:T(128)S(1)}, u32[]{:S(2)}, u32[]{:S(2)}) collective-permute-start(f32[3]{0:T(128)S(1)} %add.180), channel_id=1, source_target_pairs={{0,8},{1,9},{2,10},{3,11},{4,12},{5,13},{6,14},{7,15},{8,0},{9,1},... | collective-permute-start | bytes 44 | tf_op jit(solution)/shard_map/ppermute | solution.py:336
  205.6 6.3 %collective-permute-start.27 = (f32[1,3072]{1,0:T(1,128)S(1)}, f32[1,3072]{1,0:T(1,128)S(1)}, u32[]{:S(2)}, u32[]{:S(2)}) collective-permute-start(f32[1,3072]{1,0:T(1,128)S(1)} %get-tuple-element.30), channel_id=1, source_target_pairs={{0,16},{16,32},{32,48},{48,64},{64,80},{80,96},{96,112},{112,0},{1... | collective-permute-start | bytes 36872 | tf_op jit(solution)/shard_map/ppermute | solution.py:44
  213.0 3.0 %collective-permute-start.28 = (f32[1,3072]{1,0:T(1,128)S(1)}, f32[1,3072]{1,0:T(1,128)S(1)}, u32[]{:S(2)}, u32[]{:S(2)}) collective-permute-start(f32[1,3072]{1,0:T(1,128)S(1)} %collective-permute-done.27), channel_id=1, source_target_pairs={{0,1},{1,2},{2,3},{3,4},{4,5},{5,6},{6,7},{7,8},{8,9},{9,10},{10,1... | collective-permute-start | bytes 36872 | tf_op jit(solution)/shard_map/ppermute | solution.py:50
  216.0 2.1 rev.14
  219.5 3.4 %collective-permute-done.30 = f32[1,3072]{1,0:T(1,128)S(1)} collective-permute-done((f32[1,3072]{1,0:T(1,128)S(1)}, f32[1,3072]{1,0:T(1,128)S(1)}, u32[]{:S(2)}, u32[]{:S(2)}) %collective-permute-start.30) | collective-permute-done | bytes 12320 | tf_op jit(solution)/shard_map/ppermute | solution.py:50
  223.9 1.9 pad_maximum_fusion.33
  225.8 4.8 %collective-permute-start.31 = (f32[3]{0:T(128)S(1)}, f32[3]{0:T(128)S(1)}, u32[]{:S(2)}, u32[]{:S(2)}) collective-permute-start(f32[3]{0:T(128)S(1)} %pad_maximum_fusion.33), channel_id=1, source_target_pairs={{0,16},{16,0},{32,48},{48,32},{64,80},{80,64},{96,112},{112,96},{1... | collective-permute-start | bytes 44 | tf_op jit(solution)/shard_map/ppermute | solution.py:336
  231.5 1.9 fusion.36
  233.4 2.4 collective-permute-done.32
  235.8 1.9 fusion.39
  237.8 3.9 %collective-permute-done.33 = f32[3]{0:T(128)S(1)} collective-permute-done((f32[3]{0:T(128)S(1)}, f32[3]{0:T(128)S(1)}, u32[]{:S(2)}, u32[]{:S(2)}) %collective-permute-start.33) | collective-permute-done | bytes 44 | tf_op jit(solution)/shard_map/ppermute | solution.py:336
  244.4 4.0 %collective-permute-start.35 = (f32[3]{0:T(128)S(1)}, f32[3]{0:T(128)S(1)}, u32[]{:S(2)}, u32[]{:S(2)}) collective-permute-start(f32[3]{0:T(128)S(1)} %add.196), channel_id=1, source_target_pairs={{0,2},{1,3},{2,0},{3,1},{4,6},{5,7},{6,4},{7,5},{8,10},{9,11},{10,... | collective-permute-start | bytes 44 | tf_op jit(solution)/shard_map/ppermute | solution.py:336
  251.8 2.6 collective-permute-start.37
  259.5 14.0 %all_to_all.35 = f32[8,8,384]{2,0,1:T(8,128)S(1)} all-to-all(f32[8,8,384]{2,0,1:T(8,128)S(1)} %bitcast.68), channel_id=1, replica_groups=mesh['lon'=8,'lat'=16] {'lon'}, dimensions={1} | all-to-all | bytes 196608 | tf_op jit(solution)/shard_map/all_to_all | solution.py:424
  (138 shorter events, 57.2 us)
Async XLA Ops:
  0.6 3.0 %copy-start.7 = (s32[64,384]{1,0:T(8,128)S(1)}, s32[64,384]{1,0:T(8,128)}, u32[]{:S(2)}) copy-start(s32[64,384]{1,0:T(8,128)} %param.13) | copy-start | bytes 294916
  1.6 2.7 copy-start
  3.6 4.6 %copy-start.1 = (f32[1,20,64,384]{3,2,1,0:T(8,128)}, f32[1,20,64,384]{3,2,1,0:T(8,128)S(1)}, u32[]{:S(2)}) copy-start(f32[1,20,64,384]{3,2,1,0:T(8,128)S(1)} %get-tuple-element.44) | copy-start | bytes 5898244
  3.8 4.4 %copy-start.3 = (f32[1,20,64,384]{3,2,1,0:T(8,128)}, f32[1,20,64,384]{3,2,1,0:T(8,128)S(1)}, u32[]{:S(2)}) copy-start(f32[1,20,64,384]{3,2,1,0:T(8,128)S(1)} %fusion.1) | copy-start | bytes 5898244
  10.8 5.2 %collective-permute-start = (f32[5,20,64,2]{2,3,1,0:T(2,128)S(1)}, f32[5,20,64,2]{2,3,1,0:T(2,128)S(1)}, u32[]{:S(2)}, u32[]{:S(2)}) collective-permute-start(f32[5,20,64,2]{2,3,1,0:T(2,128)S(1)} %copy.22), channel_id=1, source_target_pairs={{0,112},{16,0},{32,16},{48,32},{64,48},{80,64},{96,80},{112,96},{1... | collective-permute-start | bytes 153608 | tf_op jit(solution)/shard_map/ppermute | solution.py:273
  14.8 3.6 %collective-permute-start.1 = (f32[5,20,64,2]{2,3,1,0:T(2,128)S(1)}, f32[5,20,64,2]{2,3,1,0:T(2,128)S(1)}, u32[]{:S(2)}, u32[]{:S(2)}) collective-permute-start(f32[5,20,64,2]{2,3,1,0:T(2,128)S(1)} %copy.23), channel_id=1, source_target_pairs={{0,16},{16,32},{32,48},{48,64},{64,80},{80,96},{96,112},{112,0},{1... | collective-permute-start | bytes 153608 | tf_op jit(solution)/shard_map/ppermute | solution.py:276
  22.2 3.7 %copy-start.4 = (f32[5,20,64,124]{3,2,1,0:T(8,128)}, f32[5,20,64,124]{3,2,1,0:T(8,128)S(1)}, u32[]{:S(2)}) copy-start(f32[5,20,64,124]{3,2,1,0:T(8,128)S(1)} %broadcast_in_dim.55) | copy-start | bytes 9523204
  22.2 14.9 %copy-start.8 = (f32[64,384]{1,0:T(8,128)S(1)}, f32[64,384]{1,0:T(8,128)}, u32[]{:S(2)}) copy-start(f32[64,384]{1,0:T(8,128)} %param.16) | copy-start | bytes 294916
  26.0 15.9 %copy-start.10 = (f32[5]{0:T(128)S(1)}, f32[5]{0:T(128)}, u32[]{:S(2)}) copy-start(f32[5]{0:T(128)} %constant.31.clone) | copy-start | bytes 64
  26.0 11.7 %collective-permute-start.2 = (f32[5,20,2,512]{3,2,1,0:T(2,128)S(1)}, f32[5,20,2,512]{3,2,1,0:T(2,128)}, u32[]{:S(2)}, u32[]{:S(2)}) collective-permute-start(f32[5,20,2,512]{3,2,1,0:T(2,128)S(1)} %get-tuple-element.16), channel_id=1, source_target_pairs={{0,112},{16,96},{32,80},{48,64},{64,48},{80,32},{96,16},{112,0},{1... | collective-permute-start | bytes 1228808 | tf_op jit(solution)/shard_map/ppermute | solution.py:287
  29.3 12.6 %collective-permute-start.3 = (f32[5,20,2,512]{3,2,1,0:T(2,128)S(1)}, f32[5,20,2,512]{3,2,1,0:T(2,128)}, u32[]{:S(2)}, u32[]{:S(2)}) collective-permute-start(f32[5,20,2,512]{3,2,1,0:T(2,128)S(1)} %get-tuple-element.15), channel_id=1, source_target_pairs={{1,0},{2,1},{3,2},{4,3},{5,4},{6,5},{7,6},{8,7},{9,8},{10,9},{11,1... | collective-permute-start | bytes 1228808 | tf_op jit(solution)/shard_map/ppermute | solution.py:283
  32.2 12.1 %collective-permute-start.4 = (f32[5,20,2,512]{3,2,1,0:T(2,128)S(1)}, f32[5,20,2,512]{3,2,1,0:T(2,128)}, u32[]{:S(2)}, u32[]{:S(2)}) collective-permute-start(f32[5,20,2,512]{3,2,1,0:T(2,128)S(1)} %get-tuple-element.16), channel_id=1, source_target_pairs={{0,1},{1,2},{2,3},{3,4},{4,5},{5,6},{6,7},{7,8},{8,9},{9,10},{10,1... | collective-permute-start | bytes 1228808 | tf_op jit(solution)/shard_map/ppermute | solution.py:284
  83.6 2.7 copy-start.6
  83.6 2.7 copy-start.9
  83.6 2.7 %slice-start = ((f32[20,64,384]{2,1,0:T(8,128)}), f32[1,64,384]{2,1,0:T(8,128)S(1)}, s32[]{:S(2)}) async-start(f32[20,64,384]{2,1,0:T(8,128)} %copy-done.5), calls=%async_computation.2 | async-start | bytes 196608 | tf_op jit(solution)/shard_map/slice | solution.py:413
  99.8 1.9 collective-permute-start.5
  100.8 7.2 %collective-permute-start.7 = (f32[1,3072]{1,0:T(1,128)S(1)}, f32[1,3072]{1,0:T(1,128)S(1)}, u32[]{:S(2)}, u32[]{:S(2)}) collective-permute-start(f32[1,3072]{1,0:T(1,128)S(1)} %get-tuple-element.33), channel_id=1, source_target_pairs={{0,112},{16,0},{32,16},{48,32},{64,48},{80,64},{96,80},{112,96},{1... | collective-permute-start | bytes 36872 | tf_op jit(solution)/shard_map/ppermute | solution.py:44
  101.7 7.6 %collective-permute-start.6 = (f32[1,3072]{1,0:T(1,128)S(1)}, f32[1,3072]{1,0:T(1,128)S(1)}, u32[]{:S(2)}, u32[]{:S(2)}) collective-permute-start(f32[1,3072]{1,0:T(1,128)S(1)} %collective-permute-done.5), channel_id=1, source_target_pairs={{0,1},{1,2},{2,3},{3,4},{4,5},{5,6},{6,7},{7,8},{8,9},{9,10},{10,1... | collective-permute-start | bytes 36872 | tf_op jit(solution)/shard_map/ppermute | solution.py:50
  108.0 4.6 %collective-permute-start.8 = (f32[1,3072]{1,0:T(1,128)S(1)}, f32[1,3072]{1,0:T(1,128)S(1)}, u32[]{:S(2)}, u32[]{:S(2)}) collective-permute-start(f32[1,3072]{1,0:T(1,128)S(1)} %collective-permute-done.7), channel_id=1, source_target_pairs={{1,0},{2,1},{3,2},{4,3},{5,4},{6,5},{7,6},{8,7},{9,8},{10,9},{11,1... | collective-permute-start | bytes 36872 | tf_op jit(solution)/shard_map/ppermute | solution.py:50
  114.9 5.4 %collective-permute-start.9 = (f32[2]{0:T(128)S(1)}, f32[2]{0:T(128)S(1)}, u32[]{:S(2)}, u32[]{:S(2)}) collective-permute-start(f32[2]{0:T(128)S(1)} %pad_maximum_fusion.31), channel_id=1, source_target_pairs={{0,16},{16,0},{32,48},{48,32},{64,80},{80,64},{96,112},{112,96},{1... | collective-permute-start | bytes 32 | tf_op jit(solution)/shard_map/ppermute | solution.py:336
  121.6 2.4 collective-permute-start.10
  125.3 3.9 %collective-permute-start.11 = (f32[2]{0:T(128)S(1)}, f32[2]{0:T(128)S(1)}, u32[]{:S(2)}, u32[]{:S(2)}) collective-permute-start(f32[2]{0:T(128)S(1)} %fusion.41), channel_id=1, source_target_pairs={{0,64},{16,80},{32,96},{48,112},{64,0},{80,16},{96,32},{112,48},{1... | collective-permute-start | bytes 32 | tf_op jit(solution)/shard_map/ppermute | solution.py:336
  129.3 3.5 %collective-permute-start.12 = (f32[2]{0:T(128)S(1)}, f32[2]{0:T(128)S(1)}, u32[]{:S(2)}, u32[]{:S(2)}) collective-permute-start(f32[2]{0:T(128)S(1)} %add.164), channel_id=1, source_target_pairs={{0,1},{1,0},{2,3},{3,2},{4,5},{5,4},{6,7},{7,6},{8,9},{9,8},{10,11... | collective-permute-start | bytes 32 | tf_op jit(solution)/shard_map/ppermute | solution.py:336
  132.7 9.5 %collective-permute-start.13 = (f32[2]{0:T(128)S(1)}, f32[2]{0:T(128)S(1)}, u32[]{:S(2)}, u32[]{:S(2)}) collective-permute-start(f32[2]{0:T(128)S(1)} %add.165), channel_id=1, source_target_pairs={{0,2},{1,3},{2,0},{3,1},{4,6},{5,7},{6,4},{7,5},{8,10},{9,11},{10,... | collective-permute-start | bytes 32 | tf_op jit(solution)/shard_map/ppermute | solution.py:336
  142.3 2.4 collective-permute-start.14
  144.7 3.9 %collective-permute-start.15 = (f32[2]{0:T(128)S(1)}, f32[2]{0:T(128)S(1)}, u32[]{:S(2)}, u32[]{:S(2)}) collective-permute-start(f32[2]{0:T(128)S(1)} %add.167), channel_id=1, source_target_pairs={{0,8},{1,9},{2,10},{3,11},{4,12},{5,13},{6,14},{7,15},{8,0},{9,1},... | collective-permute-start | bytes 32 | tf_op jit(solution)/shard_map/ppermute | solution.py:336
  150.5 7.4 %collective-permute-start.16 = (f32[1,3072]{1,0:T(1,128)S(1)}, f32[1,3072]{1,0:T(1,128)S(1)}, u32[]{:S(2)}, u32[]{:S(2)}) collective-permute-start(f32[1,3072]{1,0:T(1,128)S(1)} %get-tuple-element.32), channel_id=1, source_target_pairs={{0,16},{16,32},{32,48},{48,64},{64,80},{80,96},{96,112},{112,0},{1... | collective-permute-start | bytes 36872 | tf_op jit(solution)/shard_map/ppermute | solution.py:44
  156.8 6.4 %collective-permute-start.18 = (f32[1,3072]{1,0:T(1,128)S(1)}, f32[1,3072]{1,0:T(1,128)S(1)}, u32[]{:S(2)}, u32[]{:S(2)}) collective-permute-start(f32[1,3072]{1,0:T(1,128)S(1)} %get-tuple-element.31), channel_id=1, source_target_pairs={{0,112},{16,0},{32,16},{48,32},{64,48},{80,64},{96,80},{112,96},{1... | collective-permute-start | bytes 36872 | tf_op jit(solution)/shard_map/ppermute | solution.py:44
  157.9 6.6 %collective-permute-start.17 = (f32[1,3072]{1,0:T(1,128)S(1)}, f32[1,3072]{1,0:T(1,128)S(1)}, u32[]{:S(2)}, u32[]{:S(2)}) collective-permute-start(f32[1,3072]{1,0:T(1,128)S(1)} %collective-permute-done.16), channel_id=1, source_target_pairs={{0,1},{1,2},{2,3},{3,4},{4,5},{5,6},{6,7},{7,8},{8,9},{9,10},{10,1... | collective-permute-start | bytes 36872 | tf_op jit(solution)/shard_map/ppermute | solution.py:50
  163.2 4.8 %collective-permute-start.19 = (f32[1,3072]{1,0:T(1,128)S(1)}, f32[1,3072]{1,0:T(1,128)S(1)}, u32[]{:S(2)}, u32[]{:S(2)}) collective-permute-start(f32[1,3072]{1,0:T(1,128)S(1)} %collective-permute-done.18), channel_id=1, source_target_pairs={{1,0},{2,1},{3,2},{4,3},{5,4},{6,5},{7,6},{8,7},{9,8},{10,9},{11,1... | collective-permute-start | bytes 36872 | tf_op jit(solution)/shard_map/ppermute | solution.py:50
  171.0 5.6 %collective-permute-start.20 = (f32[3]{0:T(128)S(1)}, f32[3]{0:T(128)S(1)}, u32[]{:S(2)}, u32[]{:S(2)}) collective-permute-start(f32[3]{0:T(128)S(1)} %pad_maximum_fusion.32), channel_id=1, source_target_pairs={{0,16},{16,0},{32,48},{48,32},{64,80},{80,64},{96,112},{112,96},{1... | collective-permute-start | bytes 44 | tf_op jit(solution)/shard_map/ppermute | solution.py:336
  178.7 2.4 collective-permute-start.21
  183.1 3.9 %collective-permute-start.22 = (f32[3]{0:T(128)S(1)}, f32[3]{0:T(128)S(1)}, u32[]{:S(2)}, u32[]{:S(2)}) collective-permute-start(f32[3]{0:T(128)S(1)} %fusion.40), channel_id=1, source_target_pairs={{0,64},{16,80},{32,96},{48,112},{64,0},{80,16},{96,32},{112,48},{1... | collective-permute-start | bytes 44 | tf_op jit(solution)/shard_map/ppermute | solution.py:336
  187.0 2.7 collective-permute-start.23
  189.7 5.0 %collective-permute-start.24 = (f32[3]{0:T(128)S(1)}, f32[3]{0:T(128)S(1)}, u32[]{:S(2)}, u32[]{:S(2)}) collective-permute-start(f32[3]{0:T(128)S(1)} %add.178), channel_id=1, source_target_pairs={{0,2},{1,3},{2,0},{3,1},{4,6},{5,7},{6,4},{7,5},{8,10},{9,11},{10,... | collective-permute-start | bytes 44 | tf_op jit(solution)/shard_map/ppermute | solution.py:336
  194.8 2.4 collective-permute-start.25
  197.2 3.9 %collective-permute-start.26 = (f32[3]{0:T(128)S(1)}, f32[3]{0:T(128)S(1)}, u32[]{:S(2)}, u32[]{:S(2)}) collective-permute-start(f32[3]{0:T(128)S(1)} %add.180), channel_id=1, source_target_pairs={{0,8},{1,9},{2,10},{3,11},{4,12},{5,13},{6,14},{7,15},{8,0},{9,1},... | collective-permute-start | bytes 44 | tf_op jit(solution)/shard_map/ppermute | solution.py:336
  205.6 7.4 %collective-permute-start.27 = (f32[1,3072]{1,0:T(1,128)S(1)}, f32[1,3072]{1,0:T(1,128)S(1)}, u32[]{:S(2)}, u32[]{:S(2)}) collective-permute-start(f32[1,3072]{1,0:T(1,128)S(1)} %get-tuple-element.30), channel_id=1, source_target_pairs={{0,16},{16,32},{32,48},{48,64},{64,80},{80,96},{96,112},{112,0},{1... | collective-permute-start | bytes 36872 | tf_op jit(solution)/shard_map/ppermute | solution.py:44
  211.9 6.2 %collective-permute-start.29 = (f32[1,3072]{1,0:T(1,128)S(1)}, f32[1,3072]{1,0:T(1,128)S(1)}, u32[]{:S(2)}, u32[]{:S(2)}) collective-permute-start(f32[1,3072]{1,0:T(1,128)S(1)} %get-tuple-element.29), channel_id=1, source_target_pairs={{0,112},{16,0},{32,16},{48,32},{64,48},{80,64},{96,80},{112,96},{1... | collective-permute-start | bytes 36872 | tf_op jit(solution)/shard_map/ppermute | solution.py:44
  213.0 6.4 %collective-permute-start.28 = (f32[1,3072]{1,0:T(1,128)S(1)}, f32[1,3072]{1,0:T(1,128)S(1)}, u32[]{:S(2)}, u32[]{:S(2)}) collective-permute-start(f32[1,3072]{1,0:T(1,128)S(1)} %collective-permute-done.27), channel_id=1, source_target_pairs={{0,1},{1,2},{2,3},{3,4},{4,5},{5,6},{6,7},{7,8},{8,9},{9,10},{10,1... | collective-permute-start | bytes 36872 | tf_op jit(solution)/shard_map/ppermute | solution.py:50
  218.2 4.8 %collective-permute-start.30 = (f32[1,3072]{1,0:T(1,128)S(1)}, f32[1,3072]{1,0:T(1,128)S(1)}, u32[]{:S(2)}, u32[]{:S(2)}) collective-permute-start(f32[1,3072]{1,0:T(1,128)S(1)} %collective-permute-done.29), channel_id=1, source_target_pairs={{1,0},{2,1},{3,2},{4,3},{5,4},{6,5},{7,6},{8,7},{9,8},{10,9},{11,1... | collective-permute-start | bytes 36872 | tf_op jit(solution)/shard_map/ppermute | solution.py:50
  225.8 5.6 %collective-permute-start.31 = (f32[3]{0:T(128)S(1)}, f32[3]{0:T(128)S(1)}, u32[]{:S(2)}, u32[]{:S(2)}) collective-permute-start(f32[3]{0:T(128)S(1)} %pad_maximum_fusion.33), channel_id=1, source_target_pairs={{0,16},{16,0},{32,48},{48,32},{64,80},{80,64},{96,112},{112,96},{1... | collective-permute-start | bytes 44 | tf_op jit(solution)/shard_map/ppermute | solution.py:336
  233.4 2.4 collective-permute-start.32
  237.7 3.9 %collective-permute-start.33 = (f32[3]{0:T(128)S(1)}, f32[3]{0:T(128)S(1)}, u32[]{:S(2)}, u32[]{:S(2)}) collective-permute-start(f32[3]{0:T(128)S(1)} %fusion.39), channel_id=1, source_target_pairs={{0,64},{16,80},{32,96},{48,112},{64,0},{80,16},{96,32},{112,48},{1... | collective-permute-start | bytes 44 | tf_op jit(solution)/shard_map/ppermute | solution.py:336
  241.7 2.7 collective-permute-start.34
  244.4 5.0 %collective-permute-start.35 = (f32[3]{0:T(128)S(1)}, f32[3]{0:T(128)S(1)}, u32[]{:S(2)}, u32[]{:S(2)}) collective-permute-start(f32[3]{0:T(128)S(1)} %add.196), channel_id=1, source_target_pairs={{0,2},{1,3},{2,0},{3,1},{4,6},{5,7},{6,4},{7,5},{8,10},{9,11},{10,... | collective-permute-start | bytes 44 | tf_op jit(solution)/shard_map/ppermute | solution.py:336
  249.4 2.4 collective-permute-start.36
  251.8 3.9 %collective-permute-start.37 = (f32[3]{0:T(128)S(1)}, f32[3]{0:T(128)S(1)}, u32[]{:S(2)}, u32[]{:S(2)}) collective-permute-start(f32[3]{0:T(128)S(1)} %add.198), channel_id=1, source_target_pairs={{0,8},{1,9},{2,10},{3,11},{4,12},{5,13},{6,14},{7,15},{8,0},{9,1},... | collective-permute-start | bytes 44 | tf_op jit(solution)/shard_map/ppermute | solution.py:336
  (2 other events, 2.9 us)

commit v2 on v1

--- a/solution.py
+++ b/solution.py
@@ -328,6 +328,31 @@
     return jnp.concatenate([extended[:, -1:], extended, extended[:, :1]], axis=1)
 
 
+def strip_pad_joined(surface_field):
+    lon_count = lax.axis_size("lon")
+    lat_count = lax.axis_size("lat")
+    strip_count = lon_count * lat_count
+    axes = ("lon", "lat")
+
+    def device(strip):
+        return (strip % lon_count) * lat_count + strip // lon_count
+
+    first_row = surface_field[0:1, :]
+    last_row = surface_field[-1:, :]
+    above_row = lax.ppermute(
+        first_row, axes, [(device(s + 1), device(s)) for s in range(strip_count - 1)]
+    )
+    below_row = lax.ppermute(
+        last_row, axes, [(device(s - 1), device(s)) for s in range(1, strip_count)]
+    )
+    top_strip = jnp.logical_and(
+        lax.axis_index("lon") == lon_count - 1, lax.axis_index("lat") == lat_count - 1
+    )
+    above_row = jnp.where(top_strip, jnp.flip(last_row, axis=1), above_row)
+    extended = jnp.concatenate([below_row, surface_field, above_row], axis=0)
+    return jnp.concatenate([extended[:, -1:], extended, extended[:, :1]], axis=1)
+
+
 def butterfly_sum(value):
     for axis in ("lon", "lat"):
         count = lax.axis_size(axis)
@@ -420,7 +445,7 @@
         concat_axis=2,
         tiled=True,
     )
-    strip_solution = solve(relaid[0], relaid[1], relaid[2], strip_pad)
+    strip_solution = solve(relaid[0], relaid[1], relaid[2], strip_pad_joined)
     solution = lax.all_to_all(strip_solution, "lon", split_axis=1, concat_axis=0, tiled=True)
     return (new_tracers, solution)
 

time: 276 us -> 267 us (0.967)
  waiting for transfers between devices: 48.6 us -> 31.4 us
  starting transfers between devices: 90 us -> 97.6 us
    ppermute x12 -> x6, waiting for transfers between devices: 12.3 us -> 2.82 us  [the longest x3 2.81 us: strip_pad_joined(): lax.ppermute(last_row, axes, [(device(s - 1), device(s)) for s in range(1...]
    ppermute x21, starting transfers between devices: 49.1 us -> 58.2 us  [butterfly_sum(): lax.ppermute(value, axis, [(i, i ^ bit) for i in range(count)])]
    ppermute x21, waiting for transfers between devices: 34.1 us -> 26.4 us  [butterfly_sum(): lax.ppermute(value, axis, [(i, i ^ bit) for i in range(count)])]
    ppermute x12 -> x6, starting transfers between devices: 28.8 us -> 27.3 us  [the longest x3 20.5 us: strip_pad_joined(): lax.ppermute(first_row, axes, [(device(s + 1), device(s)) for s in range(...]
  transfers between devices with their start and end apart: 38 -> 32, of which waited for: 30 -> 27; matrix products, arithmetic and copies ran while one was open for 6% -> 6% of each run, Pallas kernels for 0% -> 0%
where the time goes in v2:
time: 267 us; the launch traced here: 265 us
  starting transfers between devices  97.6 us (37%)
  other arithmetic  47 us (18%)
  waiting for transfers between devices  31.4 us (12%)
  local copies, waits for them, and re-layouts  26.7 us (10%)
  Pallas kernels  26.6 us (10%)
  blocking collectives  26.5 us (10%)
  between operations  9.54 us (4%)
    ppermute x21, starting transfers between devices, butterfly_sum(): lax.ppermute(value, axis, [(i, i ^ bit) for i in range(count)])  58.2 us
    ppermute x21, waiting for transfers between devices, butterfly_sum(): lax.ppermute(value, axis, [(i, i ^ bit) for i in range(count)])  26.4 us
    pallas_call x1, Pallas kernels, stencil_call(): pl.pallas_call(stencil_kernel, grid=(level_count,), in_specs=[pl.BlockSpe...  21 us
    ppermute x3, starting transfers between devices, strip_pad_joined(): lax.ppermute(first_row, axes, [(device(s + 1), device(s)) for s in range(...  20.5 us
    all_to_all x1, blocking collectives, shards(): lax.all_to_all(strip_solution, 'lon', split_axis=1, concat_axis=0, tiled=...  14.3 us
    concatenate x1, other arithmetic, wrapped_extend(): jnp.concatenate([widened, north, jnp.zeros(lead + (height - rows - 4, wid...  12.7 us
    all_to_all x1, blocking collectives, shards(): lax.all_to_all(jnp.stack([surface_source, wet_surface, centre_weight]), '...  12.2 us
    add x21, other arithmetic, butterfly_sum(): value + lax.ppermute(value, axis, [(i, i ^ bit) for i in range(count)])  10.6 us
  transfers between devices with their start and end apart: 32, of which 27 were waited for; matrix products, arithmetic and copies ran while one was open for 6% of the time, Pallas kernels for 0%

profile of v2, /device:TPU:1, one launch (start us, length us, event | category | flops | bytes accessed | tf_op | source)
XLA Modules:
  0.0 265.4 jit_solution(15038592567159855991)
XLA Ops:
  1.6 2.0 bitcast_convert_fusion
  4.3 3.9 %pad_maximum_fusion.4 = (f32[5,20,64,2]{3,2,1,0:T(8,128)}, f32[5,20,64,2]{3,2,1,0:T(8,128)}) fusion(f32[1,20,64,384]{3,2,1,0:T(8,128)S(1)} %get-tuple-element.43, f32[1,20,64,384]{3,2,1,0:T(8,128)S(1)} %get-tuple-element.44, f32[1,20,64,384]{3,2,1,0:T(8,128)S(1)} %fusion.1, f32[2,20,64,384]{3,2,1,0:T(8,128)S(1)} %copy-done), kind=kLoop, calls=%fused_computation.4 | loop fusion | flops 76800 | bytes 9932800 | tf_op jit(solution)/shard_map/slice | solution.py:274
  8.3 2.6 copy.22
  12.2 2.6 copy.23
  16.1 2.3 copy.24
  18.4 2.3 copy.25
  22.3 3.7 %pad_maximum_fusion.5 = (f32[5,20,2,512]{3,2,1,0:T(2,128)S(1)}, f32[5,20,2,512]{3,2,1,0:T(2,128)S(1)}) fusion(f32[5,20,64,2]{3,2,1,0:T(8,128)} %copy.25, f32[5,20,64,124]{3,2,1,0:T(8,128)S(1)} %broadcast_in_dim.55, f32[5,20,64,2]{3,2,1,0:T(8,128)} %copy.24, f32[1,20,64,384]{3,2,1,0:T(8,128)S(1)} %get-tuple-element.43, f32[1,20,64,384]{3,2,1,0:T(8,128)S(1)} %copy-done.2, ...), kind=kLoop, calls=%fused_computation.13 | loop fusion | flops 1228800 | bytes 13926400 | tf_op jit(solution)/shard_map/concatenate | solution.py:279
  26.0 3.3 %collective-permute-start.2 = (f32[5,20,2,512]{3,2,1,0:T(2,128)S(1)}, f32[5,20,2,512]{3,2,1,0:T(2,128)}, u32[]{:S(2)}, u32[]{:S(2)}) collective-permute-start(f32[5,20,2,512]{3,2,1,0:T(2,128)S(1)} %get-tuple-element.16), channel_id=1, source_target_pairs={{0,112},{16,96},{32,80},{48,64},{64,48},{80,32},{96,16},{112,0},{1... | collective-permute-start | bytes 1228808 | tf_op jit(solution)/shard_map/ppermute | solution.py:287
  32.2 4.9 %collective-permute-start.4 = (f32[5,20,2,512]{3,2,1,0:T(2,128)S(1)}, f32[5,20,2,512]{3,2,1,0:T(2,128)}, u32[]{:S(2)}, u32[]{:S(2)}) collective-permute-start(f32[5,20,2,512]{3,2,1,0:T(2,128)S(1)} %get-tuple-element.16), channel_id=1, source_target_pairs={{0,1},{1,2},{2,3},{3,4},{4,5},{5,6},{6,7},{7,8},{8,9},{9,10},{10,1... | collective-permute-start | bytes 1228808 | tf_op jit(solution)/shard_map/ppermute | solution.py:284
  44.3 12.7 %pad_maximum_fusion.ext_ref = f32[5,20,72,512]{3,2,1,0:T(8,128)} fusion(f32[5,20,2,512]{3,2,1,0:T(2,128)} %collective-permute-done.4, f32[5,20,2,512]{3,2,1,0:T(2,128)S(1)} %fusion.3, f32[5,20,64,2]{3,2,1,0:T(8,128)} %copy.25, f32[5,20,64,124]{3,2,1,0:T(8,128)} %copy-done.4, f32[5,20,64,2]{3,2,1,0:T(8,128)} %copy.24, ...), kind=kLoop, calls=%fused_computation | loop fusion | flops 33177600 | bytes 28672288 | tf_op jit(solution)/shard_map/concatenate | solution.py:293
  57.0 21.0 %shard_map.104.values_ref = f32[2,20,64,384]{3,2,1,0:T(8,128)} custom-call(f32[5,20,72,512]{3,2,1,0:T(8,128)} %pad_maximum_fusion.ext_ref), custom_call_target="tpu_custom_call" | custom-call | tf_op jit(solution)/shard_map/pallas_call | solution.py:189
  78.0 5.7 %shard_map.105 = f32[2,20,64,384]{3,2,1,0:T(8,128)} custom-call(f32[2,20,64,384]{3,2,1,0:T(8,128)} %shard_map.104.values_ref, f32[20,64,384]{2,1,0:T(8,128)} %copy-done.5, bf16[20,64,384]{2,1,0:T(8,128)(2,1)} %diff_ref.1), custom_call_target="tpu_custom_call" | custom-call | tf_op jit(solution)/shard_map/pallas_call | solution.py:241
  83.7 2.5 fusion
  86.7 12.2 %all_to_all.34 = f32[3,64,384]{2,0,1:T(4,128)S(1)} all-to-all(f32[3,64,384]{2,0,1:T(4,128)S(1)} %copy.26), channel_id=1, replica_groups=mesh['lon'=8,'lat'=16] {'lon'}, dimensions={1} | all-to-all | bytes 589824 | tf_op jit(solution)/shard_map/all_to_all | solution.py:441
  99.8 2.8 %collective-permute-start.6 = (f32[1,3072]{1,0:T(1,128)S(1)}, f32[1,3072]{1,0:T(1,128)S(1)}, u32[]{:S(2)}, u32[]{:S(2)}) collective-permute-start(f32[1,3072]{1,0:T(1,128)S(1)} %get-tuple-element.33), channel_id=1, source_target_pairs={{16,0},{32,16},{48,32},{64,48},{80,64},{96,80},{112,96},{1,112},{1... | collective-permute-start | bytes 36872 | tf_op jit(solution)/shard_map/ppermute | solution.py:342
  102.6 2.1 rev.12
  104.7 2.8 %collective-permute-start.5 = (f32[1,3072]{1,0:T(1,128)S(1)}, f32[1,3072]{1,0:T(1,128)S(1)}, u32[]{:S(2)}, u32[]{:S(2)}) collective-permute-start(f32[1,3072]{1,0:T(1,128)S(1)} %get-tuple-element.34), channel_id=1, source_target_pairs={{0,16},{16,32},{32,48},{48,64},{64,80},{80,96},{96,112},{112,1},{1... | collective-permute-start | bytes 36872 | tf_op jit(solution)/shard_map/ppermute | solution.py:345
  113.3 2.1 collective-permute-start.8
  117.7 2.9 %collective-permute-start.9 = (f32[2]{0:T(128)S(1)}, f32[2]{0:T(128)S(1)}, u32[]{:S(2)}, u32[]{:S(2)}) collective-permute-start(f32[2]{0:T(128)S(1)} %fusion.41), channel_id=1, source_target_pairs={{0,64},{16,80},{32,96},{48,112},{64,0},{80,16},{96,32},{112,48},{1... | collective-permute-start | bytes 32 | tf_op jit(solution)/shard_map/ppermute | solution.py:361
  121.7 4.9 %collective-permute-start.10 = (f32[2]{0:T(128)S(1)}, f32[2]{0:T(128)S(1)}, u32[]{:S(2)}, u32[]{:S(2)}) collective-permute-start(f32[2]{0:T(128)S(1)} %add.164), channel_id=1, source_target_pairs={{0,1},{1,0},{2,3},{3,2},{4,5},{5,4},{6,7},{7,6},{8,9},{9,8},{10,11... | collective-permute-start | bytes 32 | tf_op jit(solution)/shard_map/ppermute | solution.py:361
  127.5 4.6 %collective-permute-start.11 = (f32[2]{0:T(128)S(1)}, f32[2]{0:T(128)S(1)}, u32[]{:S(2)}, u32[]{:S(2)}) collective-permute-start(f32[2]{0:T(128)S(1)} %add.165), channel_id=1, source_target_pairs={{0,2},{1,3},{2,0},{3,1},{4,6},{5,7},{6,4},{7,5},{8,10},{9,11},{10,... | collective-permute-start | bytes 32 | tf_op jit(solution)/shard_map/ppermute | solution.py:361
  133.0 7.4 %collective-permute-start.12 = (f32[2]{0:T(128)S(1)}, f32[2]{0:T(128)S(1)}, u32[]{:S(2)}, u32[]{:S(2)}) collective-permute-start(f32[2]{0:T(128)S(1)} %add.166), channel_id=1, source_target_pairs={{0,4},{1,5},{2,6},{3,7},{4,0},{5,1},{6,2},{7,3},{8,12},{9,13},{10,... | collective-permute-start | bytes 32 | tf_op jit(solution)/shard_map/ppermute | solution.py:361
  141.4 3.1 %collective-permute-start.13 = (f32[2]{0:T(128)S(1)}, f32[2]{0:T(128)S(1)}, u32[]{:S(2)}, u32[]{:S(2)}) collective-permute-start(f32[2]{0:T(128)S(1)} %add.167), channel_id=1, source_target_pairs={{0,8},{1,9},{2,10},{3,11},{4,12},{5,13},{6,14},{7,15},{8,0},{9,1},... | collective-permute-start | bytes 32 | tf_op jit(solution)/shard_map/ppermute | solution.py:361
  147.4 8.9 %collective-permute-start.15 = (f32[1,3072]{1,0:T(1,128)S(1)}, f32[1,3072]{1,0:T(1,128)S(1)}, u32[]{:S(2)}, u32[]{:S(2)}) collective-permute-start(f32[1,3072]{1,0:T(1,128)S(1)} %get-tuple-element.31), channel_id=1, source_target_pairs={{16,0},{32,16},{48,32},{64,48},{80,64},{96,80},{112,96},{1,112},{1... | collective-permute-start | bytes 36872 | tf_op jit(solution)/shard_map/ppermute | solution.py:342
  156.3 2.1 rev.13
  158.4 2.1 collective-permute-start.14
  162.4 1.9 pad_maximum_fusion.32
  165.6 1.9 fusion.37
  167.5 1.7 collective-permute-start.17
  170.2 1.9 fusion.40
  173.7 2.4 collective-permute-done.18
  176.1 3.2 %collective-permute-start.19 = (f32[3]{0:T(128)S(1)}, f32[3]{0:T(128)S(1)}, u32[]{:S(2)}, u32[]{:S(2)}) collective-permute-start(f32[3]{0:T(128)S(1)} %add.177), channel_id=1, source_target_pairs={{0,1},{1,0},{2,3},{3,2},{4,5},{5,4},{6,7},{7,6},{8,9},{9,8},{10,11... | collective-permute-start | bytes 44 | tf_op jit(solution)/shard_map/ppermute | solution.py:361
  181.7 2.5 collective-permute-done.20
  184.2 5.5 %collective-permute-start.21 = (f32[3]{0:T(128)S(1)}, f32[3]{0:T(128)S(1)}, u32[]{:S(2)}, u32[]{:S(2)}) collective-permute-start(f32[3]{0:T(128)S(1)} %add.179), channel_id=1, source_target_pairs={{0,4},{1,5},{2,6},{3,7},{4,0},{5,1},{6,2},{7,3},{8,12},{9,13},{10,... | collective-permute-start | bytes 44 | tf_op jit(solution)/shard_map/ppermute | solution.py:361
  190.6 3.1 %collective-permute-start.22 = (f32[3]{0:T(128)S(1)}, f32[3]{0:T(128)S(1)}, u32[]{:S(2)}, u32[]{:S(2)}) collective-permute-start(f32[3]{0:T(128)S(1)} %add.180), channel_id=1, source_target_pairs={{0,8},{1,9},{2,10},{3,11},{4,12},{5,13},{6,14},{7,15},{8,0},{9,1},... | collective-permute-start | bytes 44 | tf_op jit(solution)/shard_map/ppermute | solution.py:361
  199.3 8.9 %collective-permute-start.24 = (f32[1,3072]{1,0:T(1,128)S(1)}, f32[1,3072]{1,0:T(1,128)S(1)}, u32[]{:S(2)}, u32[]{:S(2)}) collective-permute-start(f32[1,3072]{1,0:T(1,128)S(1)} %get-tuple-element.29), channel_id=1, source_target_pairs={{16,0},{32,16},{48,32},{64,48},{80,64},{96,80},{112,96},{1,112},{1... | collective-permute-start | bytes 36872 | tf_op jit(solution)/shard_map/ppermute | solution.py:342
  208.2 2.1 rev.14
  210.3 1.9 collective-permute-start.23
  214.3 2.0 pad_maximum_fusion.33
  217.5 2.0 fusion.36
  219.4 1.7 collective-permute-start.26
  222.1 2.0 fusion.39
  225.6 2.4 collective-permute-done.27
  228.0 3.2 %collective-permute-start.28 = (f32[3]{0:T(128)S(1)}, f32[3]{0:T(128)S(1)}, u32[]{:S(2)}, u32[]{:S(2)}) collective-permute-start(f32[3]{0:T(128)S(1)} %add.195), channel_id=1, source_target_pairs={{0,1},{1,0},{2,3},{3,2},{4,5},{5,4},{6,7},{7,6},{8,9},{9,8},{10,11... | collective-permute-start | bytes 44 | tf_op jit(solution)/shard_map/ppermute | solution.py:361
  233.6 2.5 collective-permute-done.29
  236.1 5.5 %collective-permute-start.30 = (f32[3]{0:T(128)S(1)}, f32[3]{0:T(128)S(1)}, u32[]{:S(2)}, u32[]{:S(2)}) collective-permute-start(f32[3]{0:T(128)S(1)} %add.197), channel_id=1, source_target_pairs={{0,4},{1,5},{2,6},{3,7},{4,0},{5,1},{6,2},{7,3},{8,12},{9,13},{10,... | collective-permute-start | bytes 44 | tf_op jit(solution)/shard_map/ppermute | solution.py:361
  242.6 3.1 %collective-permute-start.31 = (f32[3]{0:T(128)S(1)}, f32[3]{0:T(128)S(1)}, u32[]{:S(2)}, u32[]{:S(2)}) collective-permute-start(f32[3]{0:T(128)S(1)} %add.198), channel_id=1, source_target_pairs={{0,8},{1,9},{2,10},{3,11},{4,12},{5,13},{6,14},{7,15},{8,0},{9,1},... | collective-permute-start | bytes 44 | tf_op jit(solution)/shard_map/ppermute | solution.py:361
  250.5 14.3 %all_to_all.35 = f32[8,8,384]{2,0,1:T(8,128)S(1)} all-to-all(f32[8,8,384]{2,0,1:T(8,128)S(1)} %bitcast.68), channel_id=1, replica_groups=mesh['lon'=8,'lat'=16] {'lon'}, dimensions={1} | all-to-all | bytes 196608 | tf_op jit(solution)/shard_map/all_to_all | solution.py:449
  (123 shorter events, 53.0 us)
Async XLA Ops:
  0.6 3.0 %copy-start.7 = (s32[64,384]{1,0:T(8,128)S(1)}, s32[64,384]{1,0:T(8,128)}, u32[]{:S(2)}) copy-start(s32[64,384]{1,0:T(8,128)} %param.13) | copy-start | bytes 294916
  1.6 2.7 %copy-start = (f32[2,20,64,384]{3,2,1,0:T(8,128)S(1)}, f32[2,20,64,384]{3,2,1,0:T(8,128)}, u32[]{:S(2)}) copy-start(f32[2,20,64,384]{3,2,1,0:T(8,128)} %param.9) | copy-start | bytes 11796484
  3.6 4.7 %copy-start.1 = (f32[1,20,64,384]{3,2,1,0:T(8,128)}, f32[1,20,64,384]{3,2,1,0:T(8,128)S(1)}, u32[]{:S(2)}) copy-start(f32[1,20,64,384]{3,2,1,0:T(8,128)S(1)} %get-tuple-element.44) | copy-start | bytes 5898244
  3.8 4.4 %copy-start.3 = (f32[1,20,64,384]{3,2,1,0:T(8,128)}, f32[1,20,64,384]{3,2,1,0:T(8,128)S(1)}, u32[]{:S(2)}) copy-start(f32[1,20,64,384]{3,2,1,0:T(8,128)S(1)} %fusion.1) | copy-start | bytes 5898244
  10.9 5.2 %collective-permute-start = (f32[5,20,64,2]{2,3,1,0:T(2,128)S(1)}, f32[5,20,64,2]{2,3,1,0:T(2,128)S(1)}, u32[]{:S(2)}, u32[]{:S(2)}) collective-permute-start(f32[5,20,64,2]{2,3,1,0:T(2,128)S(1)} %copy.22), channel_id=1, source_target_pairs={{0,112},{16,0},{32,16},{48,32},{64,48},{80,64},{96,80},{112,96},{1... | collective-permute-start | bytes 153608 | tf_op jit(solution)/shard_map/ppermute | solution.py:273
  14.8 3.6 %collective-permute-start.1 = (f32[5,20,64,2]{2,3,1,0:T(2,128)S(1)}, f32[5,20,64,2]{2,3,1,0:T(2,128)S(1)}, u32[]{:S(2)}, u32[]{:S(2)}) collective-permute-start(f32[5,20,64,2]{2,3,1,0:T(2,128)S(1)} %copy.23), channel_id=1, source_target_pairs={{0,16},{16,32},{32,48},{48,64},{64,80},{80,96},{96,112},{112,0},{1... | collective-permute-start | bytes 153608 | tf_op jit(solution)/shard_map/ppermute | solution.py:276
  20.7 1.5 copy-start.2
  22.3 3.7 %copy-start.4 = (f32[5,20,64,124]{3,2,1,0:T(8,128)}, f32[5,20,64,124]{3,2,1,0:T(8,128)S(1)}, u32[]{:S(2)}) copy-start(f32[5,20,64,124]{3,2,1,0:T(8,128)S(1)} %broadcast_in_dim.55) | copy-start | bytes 9523204
  22.3 14.9 %copy-start.8 = (f32[64,384]{1,0:T(8,128)S(1)}, f32[64,384]{1,0:T(8,128)}, u32[]{:S(2)}) copy-start(f32[64,384]{1,0:T(8,128)} %param.16) | copy-start | bytes 294916
  26.0 15.9 %copy-start.10 = (f32[5]{0:T(128)S(1)}, f32[5]{0:T(128)}, u32[]{:S(2)}) copy-start(f32[5]{0:T(128)} %constant.29.clone) | copy-start | bytes 64
  26.0 11.6 %collective-permute-start.2 = (f32[5,20,2,512]{3,2,1,0:T(2,128)S(1)}, f32[5,20,2,512]{3,2,1,0:T(2,128)}, u32[]{:S(2)}, u32[]{:S(2)}) collective-permute-start(f32[5,20,2,512]{3,2,1,0:T(2,128)S(1)} %get-tuple-element.16), channel_id=1, source_target_pairs={{0,112},{16,96},{32,80},{48,64},{64,48},{80,32},{96,16},{112,0},{1... | collective-permute-start | bytes 1228808 | tf_op jit(solution)/shard_map/ppermute | solution.py:287
  29.3 12.6 %collective-permute-start.3 = (f32[5,20,2,512]{3,2,1,0:T(2,128)S(1)}, f32[5,20,2,512]{3,2,1,0:T(2,128)}, u32[]{:S(2)}, u32[]{:S(2)}) collective-permute-start(f32[5,20,2,512]{3,2,1,0:T(2,128)S(1)} %get-tuple-element.15), channel_id=1, source_target_pairs={{1,0},{2,1},{3,2},{4,3},{5,4},{6,5},{7,6},{8,7},{9,8},{10,9},{11,1... | collective-permute-start | bytes 1228808 | tf_op jit(solution)/shard_map/ppermute | solution.py:283
  30.8 1.3 copy-start.5
  32.2 12.1 %collective-permute-start.4 = (f32[5,20,2,512]{3,2,1,0:T(2,128)S(1)}, f32[5,20,2,512]{3,2,1,0:T(2,128)}, u32[]{:S(2)}, u32[]{:S(2)}) collective-permute-start(f32[5,20,2,512]{3,2,1,0:T(2,128)S(1)} %get-tuple-element.16), channel_id=1, source_target_pairs={{0,1},{1,2},{2,3},{3,4},{4,5},{5,6},{6,7},{7,8},{8,9},{9,10},{10,1... | collective-permute-start | bytes 1228808 | tf_op jit(solution)/shard_map/ppermute | solution.py:284
  83.7 2.7 %copy-start.6 = (f32[20,64,384]{2,1,0:T(8,128)S(1)}, f32[20,64,384]{2,1,0:T(8,128)}, u32[]{:S(2)}) copy-start(f32[20,64,384]{2,1,0:T(8,128)} %copy-done.5) | copy-start | bytes 5898244
  83.7 2.7 %copy-start.9 = (f32[64,384]{1,0:T(8,128)S(1)}, f32[64,384]{1,0:T(8,128)}, u32[]{:S(2)}) copy-start(f32[64,384]{1,0:T(8,128)} %param.15) | copy-start | bytes 294916
  83.7 2.7 %slice-start = ((f32[20,64,384]{2,1,0:T(8,128)}), f32[1,64,384]{2,1,0:T(8,128)S(1)}, s32[]{:S(2)}) async-start(f32[20,64,384]{2,1,0:T(8,128)} %copy-done.5), calls=%async_computation.2 | async-start | bytes 196608 | tf_op jit(solution)/shard_map/slice | solution.py:438
  99.8 7.7 %collective-permute-start.6 = (f32[1,3072]{1,0:T(1,128)S(1)}, f32[1,3072]{1,0:T(1,128)S(1)}, u32[]{:S(2)}, u32[]{:S(2)}) collective-permute-start(f32[1,3072]{1,0:T(1,128)S(1)} %get-tuple-element.33), channel_id=1, source_target_pairs={{16,0},{32,16},{48,32},{64,48},{80,64},{96,80},{112,96},{1,112},{1... | collective-permute-start | bytes 36872 | tf_op jit(solution)/shard_map/ppermute | solution.py:342
  104.7 3.6 %collective-permute-start.5 = (f32[1,3072]{1,0:T(1,128)S(1)}, f32[1,3072]{1,0:T(1,128)S(1)}, u32[]{:S(2)}, u32[]{:S(2)}) collective-permute-start(f32[1,3072]{1,0:T(1,128)S(1)} %get-tuple-element.34), channel_id=1, source_target_pairs={{0,16},{16,32},{32,48},{48,64},{64,80},{80,96},{96,112},{112,1},{1... | collective-permute-start | bytes 36872 | tf_op jit(solution)/shard_map/ppermute | solution.py:345
  110.7 1.2 collective-permute-start.7
  113.3 3.0 %collective-permute-start.8 = (f32[2]{0:T(128)S(1)}, f32[2]{0:T(128)S(1)}, u32[]{:S(2)}, u32[]{:S(2)}) collective-permute-start(f32[2]{0:T(128)S(1)} %fusion.38), channel_id=1, source_target_pairs={{0,32},{16,48},{32,0},{48,16},{64,96},{80,112},{96,64},{112,80},{1... | collective-permute-start | bytes 32 | tf_op jit(solution)/shard_map/ppermute | solution.py:361
  117.7 3.9 %collective-permute-start.9 = (f32[2]{0:T(128)S(1)}, f32[2]{0:T(128)S(1)}, u32[]{:S(2)}, u32[]{:S(2)}) collective-permute-start(f32[2]{0:T(128)S(1)} %fusion.41), channel_id=1, source_target_pairs={{0,64},{16,80},{32,96},{48,112},{64,0},{80,16},{96,32},{112,48},{1... | collective-permute-start | bytes 32 | tf_op jit(solution)/shard_map/ppermute | solution.py:361
  121.7 5.8 %collective-permute-start.10 = (f32[2]{0:T(128)S(1)}, f32[2]{0:T(128)S(1)}, u32[]{:S(2)}, u32[]{:S(2)}) collective-permute-start(f32[2]{0:T(128)S(1)} %add.164), channel_id=1, source_target_pairs={{0,1},{1,0},{2,3},{3,2},{4,5},{5,4},{6,7},{7,6},{8,9},{9,8},{10,11... | collective-permute-start | bytes 32 | tf_op jit(solution)/shard_map/ppermute | solution.py:361
  127.5 5.5 %collective-permute-start.11 = (f32[2]{0:T(128)S(1)}, f32[2]{0:T(128)S(1)}, u32[]{:S(2)}, u32[]{:S(2)}) collective-permute-start(f32[2]{0:T(128)S(1)} %add.165), channel_id=1, source_target_pairs={{0,2},{1,3},{2,0},{3,1},{4,6},{5,7},{6,4},{7,5},{8,10},{9,11},{10,... | collective-permute-start | bytes 32 | tf_op jit(solution)/shard_map/ppermute | solution.py:361
  133.0 8.3 %collective-permute-start.12 = (f32[2]{0:T(128)S(1)}, f32[2]{0:T(128)S(1)}, u32[]{:S(2)}, u32[]{:S(2)}) collective-permute-start(f32[2]{0:T(128)S(1)} %add.166), channel_id=1, source_target_pairs={{0,4},{1,5},{2,6},{3,7},{4,0},{5,1},{6,2},{7,3},{8,12},{9,13},{10,... | collective-permute-start | bytes 32 | tf_op jit(solution)/shard_map/ppermute | solution.py:361
  141.4 4.0 %collective-permute-start.13 = (f32[2]{0:T(128)S(1)}, f32[2]{0:T(128)S(1)}, u32[]{:S(2)}, u32[]{:S(2)}) collective-permute-start(f32[2]{0:T(128)S(1)} %add.167), channel_id=1, source_target_pairs={{0,8},{1,9},{2,10},{3,11},{4,12},{5,13},{6,14},{7,15},{8,0},{9,1},... | collective-permute-start | bytes 32 | tf_op jit(solution)/shard_map/ppermute | solution.py:361
  147.4 13.1 %collective-permute-start.15 = (f32[1,3072]{1,0:T(1,128)S(1)}, f32[1,3072]{1,0:T(1,128)S(1)}, u32[]{:S(2)}, u32[]{:S(2)}) collective-permute-start(f32[1,3072]{1,0:T(1,128)S(1)} %get-tuple-element.31), channel_id=1, source_target_pairs={{16,0},{32,16},{48,32},{64,48},{80,64},{96,80},{112,96},{1,112},{1... | collective-permute-start | bytes 36872 | tf_op jit(solution)/shard_map/ppermute | solution.py:342
  158.4 3.1 %collective-permute-start.14 = (f32[1,3072]{1,0:T(1,128)S(1)}, f32[1,3072]{1,0:T(1,128)S(1)}, u32[]{:S(2)}, u32[]{:S(2)}) collective-permute-start(f32[1,3072]{1,0:T(1,128)S(1)} %get-tuple-element.32), channel_id=1, source_target_pairs={{0,16},{16,32},{32,48},{48,64},{64,80},{80,96},{96,112},{112,1},{1... | collective-permute-start | bytes 36872 | tf_op jit(solution)/shard_map/ppermute | solution.py:345
  164.4 1.2 collective-permute-start.16
  167.5 2.7 %collective-permute-start.17 = (f32[3]{0:T(128)S(1)}, f32[3]{0:T(128)S(1)}, u32[]{:S(2)}, u32[]{:S(2)}) collective-permute-start(f32[3]{0:T(128)S(1)} %fusion.37), channel_id=1, source_target_pairs={{0,32},{16,48},{32,0},{48,16},{64,96},{80,112},{96,64},{112,80},{1... | collective-permute-start | bytes 44 | tf_op jit(solution)/shard_map/ppermute | solution.py:361
  172.1 3.9 %collective-permute-start.18 = (f32[3]{0:T(128)S(1)}, f32[3]{0:T(128)S(1)}, u32[]{:S(2)}, u32[]{:S(2)}) collective-permute-start(f32[3]{0:T(128)S(1)} %fusion.40), channel_id=1, source_target_pairs={{0,64},{16,80},{32,96},{48,112},{64,0},{80,16},{96,32},{112,48},{1... | collective-permute-start | bytes 44 | tf_op jit(solution)/shard_map/ppermute | solution.py:361
  176.1 4.1 %collective-permute-start.19 = (f32[3]{0:T(128)S(1)}, f32[3]{0:T(128)S(1)}, u32[]{:S(2)}, u32[]{:S(2)}) collective-permute-start(f32[3]{0:T(128)S(1)} %add.177), channel_id=1, source_target_pairs={{0,1},{1,0},{2,3},{3,2},{4,5},{5,4},{6,7},{7,6},{8,9},{9,8},{10,11... | collective-permute-start | bytes 44 | tf_op jit(solution)/shard_map/ppermute | solution.py:361
  180.2 3.9 %collective-permute-start.20 = (f32[3]{0:T(128)S(1)}, f32[3]{0:T(128)S(1)}, u32[]{:S(2)}, u32[]{:S(2)}) collective-permute-start(f32[3]{0:T(128)S(1)} %add.178), channel_id=1, source_target_pairs={{0,2},{1,3},{2,0},{3,1},{4,6},{5,7},{6,4},{7,5},{8,10},{9,11},{10,... | collective-permute-start | bytes 44 | tf_op jit(solution)/shard_map/ppermute | solution.py:361
  184.2 6.4 %collective-permute-start.21 = (f32[3]{0:T(128)S(1)}, f32[3]{0:T(128)S(1)}, u32[]{:S(2)}, u32[]{:S(2)}) collective-permute-start(f32[3]{0:T(128)S(1)} %add.179), channel_id=1, source_target_pairs={{0,4},{1,5},{2,6},{3,7},{4,0},{5,1},{6,2},{7,3},{8,12},{9,13},{10,... | collective-permute-start | bytes 44 | tf_op jit(solution)/shard_map/ppermute | solution.py:361
  190.6 4.0 %collective-permute-start.22 = (f32[3]{0:T(128)S(1)}, f32[3]{0:T(128)S(1)}, u32[]{:S(2)}, u32[]{:S(2)}) collective-permute-start(f32[3]{0:T(128)S(1)} %add.180), channel_id=1, source_target_pairs={{0,8},{1,9},{2,10},{3,11},{4,12},{5,13},{6,14},{7,15},{8,0},{9,1},... | collective-permute-start | bytes 44 | tf_op jit(solution)/shard_map/ppermute | solution.py:361
  199.3 12.9 %collective-permute-start.24 = (f32[1,3072]{1,0:T(1,128)S(1)}, f32[1,3072]{1,0:T(1,128)S(1)}, u32[]{:S(2)}, u32[]{:S(2)}) collective-permute-start(f32[1,3072]{1,0:T(1,128)S(1)} %get-tuple-element.29), channel_id=1, source_target_pairs={{16,0},{32,16},{48,32},{64,48},{80,64},{96,80},{112,96},{1,112},{1... | collective-permute-start | bytes 36872 | tf_op jit(solution)/shard_map/ppermute | solution.py:342
  210.3 3.1 %collective-permute-start.23 = (f32[1,3072]{1,0:T(1,128)S(1)}, f32[1,3072]{1,0:T(1,128)S(1)}, u32[]{:S(2)}, u32[]{:S(2)}) collective-permute-start(f32[1,3072]{1,0:T(1,128)S(1)} %get-tuple-element.30), channel_id=1, source_target_pairs={{0,16},{16,32},{32,48},{48,64},{64,80},{80,96},{96,112},{112,1},{1... | collective-permute-start | bytes 36872 | tf_op jit(solution)/shard_map/ppermute | solution.py:345
  216.3 1.2 collective-permute-start.25
  219.4 2.7 %collective-permute-start.26 = (f32[3]{0:T(128)S(1)}, f32[3]{0:T(128)S(1)}, u32[]{:S(2)}, u32[]{:S(2)}) collective-permute-start(f32[3]{0:T(128)S(1)} %fusion.36), channel_id=1, source_target_pairs={{0,32},{16,48},{32,0},{48,16},{64,96},{80,112},{96,64},{112,80},{1... | collective-permute-start | bytes 44 | tf_op jit(solution)/shard_map/ppermute | solution.py:361
  224.1 3.9 %collective-permute-start.27 = (f32[3]{0:T(128)S(1)}, f32[3]{0:T(128)S(1)}, u32[]{:S(2)}, u32[]{:S(2)}) collective-permute-start(f32[3]{0:T(128)S(1)} %fusion.39), channel_id=1, source_target_pairs={{0,64},{16,80},{32,96},{48,112},{64,0},{80,16},{96,32},{112,48},{1... | collective-permute-start | bytes 44 | tf_op jit(solution)/shard_map/ppermute | solution.py:361
  228.0 4.1 %collective-permute-start.28 = (f32[3]{0:T(128)S(1)}, f32[3]{0:T(128)S(1)}, u32[]{:S(2)}, u32[]{:S(2)}) collective-permute-start(f32[3]{0:T(128)S(1)} %add.195), channel_id=1, source_target_pairs={{0,1},{1,0},{2,3},{3,2},{4,5},{5,4},{6,7},{7,6},{8,9},{9,8},{10,11... | collective-permute-start | bytes 44 | tf_op jit(solution)/shard_map/ppermute | solution.py:361
  232.2 3.9 %collective-permute-start.29 = (f32[3]{0:T(128)S(1)}, f32[3]{0:T(128)S(1)}, u32[]{:S(2)}, u32[]{:S(2)}) collective-permute-start(f32[3]{0:T(128)S(1)} %add.196), channel_id=1, source_target_pairs={{0,2},{1,3},{2,0},{3,1},{4,6},{5,7},{6,4},{7,5},{8,10},{9,11},{10,... | collective-permute-start | bytes 44 | tf_op jit(solution)/shard_map/ppermute | solution.py:361
  236.1 6.4 %collective-permute-start.30 = (f32[3]{0:T(128)S(1)}, f32[3]{0:T(128)S(1)}, u32[]{:S(2)}, u32[]{:S(2)}) collective-permute-start(f32[3]{0:T(128)S(1)} %add.197), channel_id=1, source_target_pairs={{0,4},{1,5},{2,6},{3,7},{4,0},{5,1},{6,2},{7,3},{8,12},{9,13},{10,... | collective-permute-start | bytes 44 | tf_op jit(solution)/shard_map/ppermute | solution.py:361
  242.6 4.0 %collective-permute-start.31 = (f32[3]{0:T(128)S(1)}, f32[3]{0:T(128)S(1)}, u32[]{:S(2)}, u32[]{:S(2)}) collective-permute-start(f32[3]{0:T(128)S(1)} %add.198), channel_id=1, source_target_pairs={{0,8},{1,9},{2,10},{3,11},{4,12},{5,13},{6,14},{7,15},{8,0},{9,1},... | collective-permute-start | bytes 44 | tf_op jit(solution)/shard_map/ppermute | solution.py:361

commit v3 on v2

--- a/solution.py
+++ b/solution.py
@@ -117,8 +117,8 @@
     return wet_centre * (centre - advection_rate * divergence - biharmonic_rate * lap_two)
 
 
-def stencil_kernel(ext_ref, out_ref):
-    height, width = ext_ref.shape[2], ext_ref.shape[3]
+def stencil_body(field, out_ref):
+    height, width = field(2).shape
     row_count, col_count = out_ref.shape[2], out_ref.shape[3]
 
     def south(x):
@@ -134,7 +134,7 @@
         return pltpu.roll(x, width - 1, 1)
 
     shifts = (south, north, west, east)
-    wet = ext_ref[2, 0]
+    wet = field(2)
     wet_near = [shift(wet) for shift in shifts]
 
     def laplacian(values):
@@ -144,18 +144,113 @@
             running = term if running is None else running + term
         return wet * running
 
-    east_speed = ext_ref[3, 0]
-    north_speed = ext_ref[4, 0]
+    east_speed = field(3)
+    north_speed = field(4)
     east_mean = 0.5 * (east_speed + east(east_speed))
     north_mean = 0.5 * (north_speed + north(north_speed))
     for t in range(out_ref.shape[0]):
-        tracer = ext_ref[t, 0]
+        tracer = field(t)
         lap_two = laplacian(laplacian(tracer))
         east_flux = east_mean * 0.5 * (tracer + east(tracer)) * wet * wet_near[3]
         north_flux = north_mean * 0.5 * (tracer + north(tracer)) * wet * wet_near[1]
         divergence = east_flux - west(east_flux) + north_flux - south(north_flux)
         result = wet * (tracer - advection_rate * divergence - biharmonic_rate * lap_two)
         out_ref[t, 0] = result[:row_count, :col_count]
+
+
+def stencil_kernel(ext_ref, out_ref):
+    stencil_body(lambda f: ext_ref[f, 0], out_ref)
+
+
+def assembling_kernel(tracer_ref, wet_ref, east_ref, north_ref, cols_ref, rows_ref, out_ref, ext_ref):
+    rows, cols = wet_ref.shape[1], wet_ref.shape[2]
+    interiors = (
+        tracer_ref[0, 0],
+        tracer_ref[1, 0],
+        wet_ref[0],
+        east_ref[0].astype(jnp.float32),
+        north_ref[0].astype(jnp.float32),
+    )
+    for f, interior in enumerate(interiors):
+        ext_ref[f, 0:rows, 0:cols] = interior
+        ext_ref[f, 0:rows, cols:] = cols_ref[f, 0]
+        ext_ref[f, rows:, :] = rows_ref[f, 0]
+    stencil_body(lambda f: ext_ref[f], out_ref)
+
+
+def halo_pieces(tracers, wet_mask, east_velocity, north_velocity, fold_signs):
+    rows, cols = wet_mask.shape[1], wet_mask.shape[2]
+    width = -(-(cols + 4) // 128) * 128
+    lead = wet_mask.shape[:1]
+    lon_count = lax.axis_size("lon")
+    lat_count = lax.axis_size("lat")
+
+    def fields(index):
+        return jnp.concatenate(
+            [
+                tracers[index],
+                wet_mask[None][index],
+                east_velocity[None][index].astype(jnp.float32),
+                north_velocity[None][index].astype(jnp.float32),
+            ],
+            axis=0,
+        )
+
+    every = slice(None)
+    east_halo = lax.ppermute(
+        fields((every, every, every, slice(0, 2))),
+        "lon",
+        [(i, (i - 1) % lon_count) for i in range(lon_count)],
+    )
+    west_halo = lax.ppermute(
+        fields((every, every, every, slice(cols - 2, cols))),
+        "lon",
+        [(i, (i + 1) % lon_count) for i in range(lon_count)],
+    )
+    halo_cols = jnp.concatenate(
+        [east_halo, jnp.zeros((5,) + lead + (rows, width - cols - 4), jnp.float32), west_halo],
+        axis=3,
+    )
+
+    def widened_rows(start):
+        band = (every, every, slice(start, start + 2))
+        return jnp.concatenate([fields(band), halo_cols[band]], axis=3)
+
+    bottom = widened_rows(0)
+    top = widened_rows(rows - 2)
+    north_rows = lax.ppermute(bottom, "lat", [(j, j - 1) for j in range(1, lat_count)])
+    south_rows = lax.ppermute(top, "lat", [(j, j + 1) for j in range(lat_count - 1)])
+    mirrored = lax.ppermute(top, "lon", [(i, lon_count - 1 - i) for i in range(lon_count)])
+    folded = jnp.roll(jnp.flip(mirrored, axis=(2, 3)), cols - width, axis=3) * fold_signs
+    at_top = lax.axis_index("lat") == lat_count - 1
+    north = jnp.where(at_top, folded, north_rows)
+    halo_rows = jnp.concatenate(
+        [north, jnp.zeros((5,) + lead + (4, width), jnp.float32), south_rows], axis=2
+    )
+    return halo_cols, halo_rows
+
+
+def assembling_call(tracers, wet_mask, east_velocity, north_velocity, fold_signs):
+    halo_cols, halo_rows = halo_pieces(tracers, wet_mask, east_velocity, north_velocity, fold_signs)
+    tracer_count, level_count, rows, cols = tracers.shape
+    width = cols + halo_cols.shape[3]
+    height = rows + halo_rows.shape[2]
+    level_block = pl.BlockSpec((1, rows, cols), lambda k: (k, 0, 0))
+    return pl.pallas_call(
+        assembling_kernel,
+        grid=(level_count,),
+        in_specs=[
+            pl.BlockSpec((tracer_count, 1, rows, cols), lambda k: (0, k, 0, 0)),
+            level_block,
+            level_block,
+            level_block,
+            pl.BlockSpec((5, 1, rows, halo_cols.shape[3]), lambda k: (0, k, 0, 0)),
+            pl.BlockSpec((5, 1, halo_rows.shape[2], width), lambda k: (0, k, 0, 0)),
+        ],
+        out_specs=pl.BlockSpec((tracer_count, 1, rows, cols), lambda k: (0, k, 0, 0)),
+        out_shape=jax.ShapeDtypeStruct(tracers.shape, jnp.float32),
+        scratch_shapes=[pltpu.VMEM((5, height, width), jnp.float32)],
+    )(tracers, wet_mask, east_velocity, north_velocity, halo_cols, halo_rows)
 
 
 def wrapped_layout(padded):
@@ -427,13 +522,8 @@
     wet_mask = jnp.where(
         level_index < depth_levels[None], ocean_cells[None], jnp.zeros_like(ocean_cells)[None]
     )
-    east_float = east_velocity.astype(jnp.float32)
-    north_float = north_velocity.astype(jnp.float32)
-    stacked = jnp.concatenate(
-        [tracers, wet_mask[None], east_float[None], north_float[None]], axis=0
-    )
     fold_signs = jnp.array([1.0, 1.0, 1.0, -1.0, -1.0], jnp.float32).reshape(5, 1, 1, 1)
-    provisional = stencil_call(wrapped_extend(stacked, fold_signs), row_count, col_count)
+    provisional = assembling_call(tracers, wet_mask, east_velocity, north_velocity, fold_signs)
     new_tracers = vertical_mix(provisional, wet_mask, vertical_diffusivity)
     wet_surface = wet_mask[0]
     surface_source = wet_surface * (forcing + jnp.mean(new_tracers[0] - new_tracers[1], axis=0))

time: 267 us -> 265 us (level)
  other arithmetic: 47 us -> 37.6 us
  local copies, waits for them, and re-layouts: 26.7 us -> 35.2 us
    concatenate x2 -> x6, other arithmetic: 16.5 us -> 7.06 us  [the longest x1 2.9 us: halo_pieces(): jnp.concatenate([east_halo, jnp.zeros((5,) + lead + (rows, width - cols -...]
    convert_element_type x0 -> x3, other arithmetic: none -> 5.24 us  [the longest x2 3.96 us: fields(): north_velocity[None][index].astype(jnp.float32)]
    slice x6 -> x11, local copies, waits for them, and re-layouts: 8.77 us -> 13.5 us  [the longest x2 5.17 us: fields(): tracers[index]]
    convert_element_type x0 -> x4, local copies, waits for them, and re-layouts: none -> 4.31 us  [the longest x2 2.7 us: fields(): east_velocity[None][index].astype(jnp.float32)]
    slice x1 -> x0, other arithmetic: 3.94 us -> none  [wrapped_extend(): stacked[..., :2]]
  transfers between devices with their start and end apart: 32 -> 32, of which waited for: 27 -> 25; matrix products, arithmetic and copies ran while one was open for 6% -> 9% of each run, Pallas kernels for 0% -> 0%
where the time goes in v3:
time: 265 us; the launch traced here: 263 us
  starting transfers between devices  95.1 us (36%)
  other arithmetic  37.6 us (14%)
  local copies, waits for them, and re-layouts  35.2 us (13%)
  waiting for transfers between devices  34 us (13%)
  Pallas kernels  26.4 us (10%)
  blocking collectives  25.6 us (10%)
  between operations  9.38 us (4%)
    ppermute x21, starting transfers between devices, butterfly_sum(): lax.ppermute(value, axis, [(i, i ^ bit) for i in range(count)])  57.9 us
    ppermute x21, waiting for transfers between devices, butterfly_sum(): lax.ppermute(value, axis, [(i, i ^ bit) for i in range(count)])  26.7 us
    pallas_call x1, Pallas kernels, assembling_call(): pl.pallas_call(assembling_kernel, grid=(level_count,), in_specs=[pl.Block...  20.7 us
    ppermute x3, starting transfers between devices, strip_pad_joined(): lax.ppermute(first_row, axes, [(device(s + 1), device(s)) for s in range(...  20.5 us
    all_to_all x1, blocking collectives, shards(): lax.all_to_all(strip_solution, 'lon', split_axis=1, concat_axis=0, tiled=...  14.3 us
    all_to_all x1, blocking collectives, shards(): lax.all_to_all(jnp.stack([surface_source, wet_surface, centre_weight]), '...  11.3 us
    add x21, other arithmetic, butterfly_sum(): value + lax.ppermute(value, axis, [(i, i ^ bit) for i in range(count)])  10.5 us
    ppermute x3, starting transfers between devices, strip_pad_joined(): lax.ppermute(last_row, axes, [(device(s - 1), device(s)) for s in range(1...  6.6 us
  transfers between devices with their start and end apart: 32, of which 25 were waited for; matrix products, arithmetic and copies ran while one was open for 9% of the time, Pallas kernels for 0%

profile of v3, /device:TPU:1, one launch (start us, length us, event | category | flops | bytes accessed | tf_op | source)
XLA Modules:
  0.0 263.3 jit_solution(1098232518740249425)
XLA Ops:
  7.9 2.1 slice_convert_fusion.2
  10.3 3.3 %fusion.31 = (f32[2,20,64,2]{3,2,1,0:T(8,128)}, f32[2,20,64,2]{3,2,1,0:T(8,128)S(1)}) fusion(f32[2,20,64,384]{3,2,1,0:T(8,128)} %tracer_ref.1), kind=kLoop, calls=%fused_computation.107 | loop fusion | bytes 81920 | tf_op jit(solution)/shard_map/slice | solution.py:191
  13.6 1.8 copy.55
  23.9 1.8 slice_convert_fusion.4
  25.7 1.9 fusion.30
  28.5 1.9 copy.50
  30.5 3.1 %copy.51 = f32[5,20,64,2]{3,2,1,0:T(8,128)} copy(f32[5,20,64,2]{2,3,1,0:T(2,128)} %collective-permute-done.1) | data formatting | bytes 102400 | tf_op jit(solution)/shard_map/ppermute | solution.py:205
  33.6 2.9 %pad_maximum_fusion.cols_ref = f32[5,20,64,128]{3,2,1,0:T(8,128)S(1)} fusion(f32[5,20,64,2]{3,2,1,0:T(8,128)} %copy.51, f32[5,20,64,2]{3,2,1,0:T(8,128)S(1)} %copy.50, f32[128]{0:T(128)S(1)} %pad.72.clone), kind=kLoop, calls=%fused_computation | loop fusion | flops 1638400 | bytes 3379712 | tf_op jit(solution)/shard_map/concatenate | solution.py:210
  36.9 1.9 collective-permute-start.2
  41.4 4.2 %collective-permute-start.4 = (f32[5,20,2,512]{3,2,1,0:T(2,128)S(1)}, f32[5,20,2,512]{3,2,1,0:T(2,128)S(1)}, u32[]{:S(2)}, u32[]{:S(2)}) collective-permute-start(f32[5,20,2,512]{3,2,1,0:T(2,128)S(1)} %pad_maximum_fusion.2), channel_id=1, source_target_pairs={{0,1},{1,2},{2,3},{3,4},{4,5},{5,6},{6,7},{7,8},{8,9},{9,10},{10,1... | collective-permute-start | bytes 1228808 | tf_op jit(solution)/shard_map/ppermute | solution.py:222
  45.6 4.3 %collective-permute-done.2 = f32[5,20,2,512]{3,2,1,0:T(2,128)} collective-permute-done((f32[5,20,2,512]{3,2,1,0:T(2,128)S(1)}, f32[5,20,2,512]{3,2,1,0:T(2,128)}, u32[]{:S(2)}, u32[]{:S(2)}) %collective-permute-start.2) | collective-permute-done | bytes 409632 | tf_op jit(solution)/shard_map/ppermute | solution.py:223
  56.5 20.7 %shard_map.104.values_ref = f32[2,20,64,384]{3,2,1,0:T(8,128)} custom-call(f32[2,20,64,384]{3,2,1,0:T(8,128)} %tracer_ref.1, f32[20,64,384]{2,1,0:T(8,128)} %copy-done, bf16[20,64,384]{2,1,0:T(8,128)(2,1)} %east_ref.1, bf16[20,64,384]{2,1,0:T(8,128)(2,1)} %north_ref.1, f32[5,20,64,128]{3,2,1,0:T(8,128)} %copy-done.2, ...), custom_call_target="tpu_custom_call" | custom-call | tf_op jit(solution)/shard_map/pallas_call | solution.py:239
  77.2 5.7 %shard_map.105 = f32[2,20,64,384]{3,2,1,0:T(8,128)} custom-call(f32[2,20,64,384]{3,2,1,0:T(8,128)} %shard_map.104.values_ref, f32[20,64,384]{2,1,0:T(8,128)} %copy-done, bf16[20,64,384]{2,1,0:T(8,128)(2,1)} %diff_ref.1), custom_call_target="tpu_custom_call" | custom-call | tf_op jit(solution)/shard_map/pallas_call | solution.py:336
  82.9 2.5 fusion
  85.9 11.3 %all_to_all.34 = f32[3,64,384]{2,0,1:T(4,128)S(1)} all-to-all(f32[3,64,384]{2,0,1:T(4,128)S(1)} %copy.52), channel_id=1, replica_groups=mesh['lon'=8,'lat'=16] {'lon'}, dimensions={1} | all-to-all | bytes 589824 | tf_op jit(solution)/shard_map/all_to_all | solution.py:531
  98.1 2.8 %collective-permute-start.6 = (f32[1,3072]{1,0:T(1,128)S(1)}, f32[1,3072]{1,0:T(1,128)S(1)}, u32[]{:S(2)}, u32[]{:S(2)}) collective-permute-start(f32[1,3072]{1,0:T(1,128)S(1)} %get-tuple-element.47), channel_id=1, source_target_pairs={{16,0},{32,16},{48,32},{64,48},{80,64},{96,80},{112,96},{1,112},{1... | collective-permute-start | bytes 36872 | tf_op jit(solution)/shard_map/ppermute | solution.py:437
  100.9 2.1 rev.12
  103.1 2.8 %collective-permute-start.5 = (f32[1,3072]{1,0:T(1,128)S(1)}, f32[1,3072]{1,0:T(1,128)S(1)}, u32[]{:S(2)}, u32[]{:S(2)}) collective-permute-start(f32[1,3072]{1,0:T(1,128)S(1)} %get-tuple-element.48), channel_id=1, source_target_pairs={{0,16},{16,32},{32,48},{48,64},{64,80},{80,96},{96,112},{112,1},{1... | collective-permute-start | bytes 36872 | tf_op jit(solution)/shard_map/ppermute | solution.py:440
  111.6 2.1 collective-permute-start.8
  116.0 2.5 collective-permute-start.9
  120.0 4.6 %collective-permute-start.10 = (f32[2]{0:T(128)S(1)}, f32[2]{0:T(128)S(1)}, u32[]{:S(2)}, u32[]{:S(2)}) collective-permute-start(f32[2]{0:T(128)S(1)} %add.164), channel_id=1, source_target_pairs={{0,1},{1,0},{2,3},{3,2},{4,5},{5,4},{6,7},{7,6},{8,9},{9,8},{10,11... | collective-permute-start | bytes 32 | tf_op jit(solution)/shard_map/ppermute | solution.py:456
  125.5 5.0 %collective-permute-start.11 = (f32[2]{0:T(128)S(1)}, f32[2]{0:T(128)S(1)}, u32[]{:S(2)}, u32[]{:S(2)}) collective-permute-start(f32[2]{0:T(128)S(1)} %add.165), channel_id=1, source_target_pairs={{0,2},{1,3},{2,0},{3,1},{4,6},{5,7},{6,4},{7,5},{8,10},{9,11},{10,... | collective-permute-start | bytes 32 | tf_op jit(solution)/shard_map/ppermute | solution.py:456
  131.5 7.2 %collective-permute-start.12 = (f32[2]{0:T(128)S(1)}, f32[2]{0:T(128)S(1)}, u32[]{:S(2)}, u32[]{:S(2)}) collective-permute-start(f32[2]{0:T(128)S(1)} %add.166), channel_id=1, source_target_pairs={{0,4},{1,5},{2,6},{3,7},{4,0},{5,1},{6,2},{7,3},{8,12},{9,13},{10,... | collective-permute-start | bytes 32 | tf_op jit(solution)/shard_map/ppermute | solution.py:456
  139.7 3.1 %collective-permute-start.13 = (f32[2]{0:T(128)S(1)}, f32[2]{0:T(128)S(1)}, u32[]{:S(2)}, u32[]{:S(2)}) collective-permute-start(f32[2]{0:T(128)S(1)} %add.167), channel_id=1, source_target_pairs={{0,8},{1,9},{2,10},{3,11},{4,12},{5,13},{6,14},{7,15},{8,0},{9,1},... | collective-permute-start | bytes 32 | tf_op jit(solution)/shard_map/ppermute | solution.py:456
  145.8 8.9 %collective-permute-start.15 = (f32[1,3072]{1,0:T(1,128)S(1)}, f32[1,3072]{1,0:T(1,128)S(1)}, u32[]{:S(2)}, u32[]{:S(2)}) collective-permute-start(f32[1,3072]{1,0:T(1,128)S(1)} %get-tuple-element.45), channel_id=1, source_target_pairs={{16,0},{32,16},{48,32},{64,48},{80,64},{96,80},{112,96},{1,112},{1... | collective-permute-start | bytes 36872 | tf_op jit(solution)/shard_map/ppermute | solution.py:437
  154.7 2.1 rev.13
  156.8 1.9 collective-permute-start.14
  160.8 1.8 pad_maximum_fusion.26
  163.8 1.8 fusion.42
  165.6 1.7 collective-permute-start.17
  168.3 1.8 fusion.45
  171.6 2.4 collective-permute-done.18
  174.0 3.2 %collective-permute-start.19 = (f32[3]{0:T(128)S(1)}, f32[3]{0:T(128)S(1)}, u32[]{:S(2)}, u32[]{:S(2)}) collective-permute-start(f32[3]{0:T(128)S(1)} %add.177), channel_id=1, source_target_pairs={{0,1},{1,0},{2,3},{3,2},{4,5},{5,4},{6,7},{7,6},{8,9},{9,8},{10,11... | collective-permute-start | bytes 44 | tf_op jit(solution)/shard_map/ppermute | solution.py:456
  179.6 2.5 collective-permute-done.20
  182.1 5.5 %collective-permute-start.21 = (f32[3]{0:T(128)S(1)}, f32[3]{0:T(128)S(1)}, u32[]{:S(2)}, u32[]{:S(2)}) collective-permute-start(f32[3]{0:T(128)S(1)} %add.179), channel_id=1, source_target_pairs={{0,4},{1,5},{2,6},{3,7},{4,0},{5,1},{6,2},{7,3},{8,12},{9,13},{10,... | collective-permute-start | bytes 44 | tf_op jit(solution)/shard_map/ppermute | solution.py:456
  188.5 3.1 %collective-permute-start.22 = (f32[3]{0:T(128)S(1)}, f32[3]{0:T(128)S(1)}, u32[]{:S(2)}, u32[]{:S(2)}) collective-permute-start(f32[3]{0:T(128)S(1)} %add.180), channel_id=1, source_target_pairs={{0,8},{1,9},{2,10},{3,11},{4,12},{5,13},{6,14},{7,15},{8,0},{9,1},... | collective-permute-start | bytes 44 | tf_op jit(solution)/shard_map/ppermute | solution.py:456
  196.9 8.9 %collective-permute-start.24 = (f32[1,3072]{1,0:T(1,128)S(1)}, f32[1,3072]{1,0:T(1,128)S(1)}, u32[]{:S(2)}, u32[]{:S(2)}) collective-permute-start(f32[1,3072]{1,0:T(1,128)S(1)} %get-tuple-element.43), channel_id=1, source_target_pairs={{16,0},{32,16},{48,32},{64,48},{80,64},{96,80},{112,96},{1,112},{1... | collective-permute-start | bytes 36872 | tf_op jit(solution)/shard_map/ppermute | solution.py:437
  205.8 2.1 rev.14
  207.9 1.9 collective-permute-start.23
  212.0 2.0 pad_maximum_fusion.27
  215.2 2.0 fusion.41
  219.9 2.0 fusion.44
  223.5 2.4 collective-permute-done.27
  225.9 3.2 %collective-permute-start.28 = (f32[3]{0:T(128)S(1)}, f32[3]{0:T(128)S(1)}, u32[]{:S(2)}, u32[]{:S(2)}) collective-permute-start(f32[3]{0:T(128)S(1)} %add.195), channel_id=1, source_target_pairs={{0,1},{1,0},{2,3},{3,2},{4,5},{5,4},{6,7},{7,6},{8,9},{9,8},{10,11... | collective-permute-start | bytes 44 | tf_op jit(solution)/shard_map/ppermute | solution.py:456
  231.5 2.5 collective-permute-done.29
  234.0 5.5 %collective-permute-start.30 = (f32[3]{0:T(128)S(1)}, f32[3]{0:T(128)S(1)}, u32[]{:S(2)}, u32[]{:S(2)}) collective-permute-start(f32[3]{0:T(128)S(1)} %add.197), channel_id=1, source_target_pairs={{0,4},{1,5},{2,6},{3,7},{4,0},{5,1},{6,2},{7,3},{8,12},{9,13},{10,... | collective-permute-start | bytes 44 | tf_op jit(solution)/shard_map/ppermute | solution.py:456
  240.4 3.1 %collective-permute-start.31 = (f32[3]{0:T(128)S(1)}, f32[3]{0:T(128)S(1)}, u32[]{:S(2)}, u32[]{:S(2)}) collective-permute-start(f32[3]{0:T(128)S(1)} %add.198), channel_id=1, source_target_pairs={{0,8},{1,9},{2,10},{3,11},{4,12},{5,13},{6,14},{7,15},{8,0},{9,1},... | collective-permute-start | bytes 44 | tf_op jit(solution)/shard_map/ppermute | solution.py:456
  248.3 14.3 %all_to_all.35 = f32[8,8,384]{2,0,1:T(8,128)S(1)} all-to-all(f32[8,8,384]{2,0,1:T(8,128)S(1)} %bitcast.68), channel_id=1, replica_groups=mesh['lon'=8,'lat'=16] {'lon'}, dimensions={1} | all-to-all | bytes 196608 | tf_op jit(solution)/shard_map/all_to_all | solution.py:539
  (148 shorter events, 65.8 us)
Async XLA Ops:
  2.7 2.6 copy-start.3
  16.1 12.4 %collective-permute-start = (f32[5,20,64,2]{2,3,1,0:T(2,128)}, f32[5,20,64,2]{2,3,1,0:T(2,128)}, u32[]{:S(2)}, u32[]{:S(2)}) collective-permute-start(f32[5,20,64,2]{2,3,1,0:T(2,128)} %pad_maximum_fusion.17), channel_id=1, source_target_pairs={{0,112},{16,0},{32,16},{48,32},{64,48},{80,64},{96,80},{112,96},{1... | collective-permute-start | bytes 153608 | tf_op jit(solution)/shard_map/ppermute | solution.py:200
  22.7 7.8 %collective-permute-start.1 = (f32[5,20,64,2]{2,3,1,0:T(2,128)}, f32[5,20,64,2]{2,3,1,0:T(2,128)}, u32[]{:S(2)}, u32[]{:S(2)}) collective-permute-start(f32[5,20,64,2]{2,3,1,0:T(2,128)} %pad_maximum_fusion.18), channel_id=1, source_target_pairs={{0,16},{16,32},{32,48},{48,64},{64,80},{80,96},{96,112},{112,0},{1... | collective-permute-start | bytes 153608 | tf_op jit(solution)/shard_map/ppermute | solution.py:205
  33.6 3.1 %copy-start.4 = (f32[2,20,2,384]{3,2,1,0:T(2,128)S(1)}, f32[2,20,2,384]{3,2,1,0:T(2,128)}, u32[]{:S(2)}) copy-start(f32[2,20,2,384]{3,2,1,0:T(2,128)} %get-tuple-element.16) | copy-start | bytes 368644
  33.6 3.1 %copy-start.8 = (f32[1,20,2,384]{3,2,1,0:T(2,128)S(1)}, f32[1,20,2,384]{3,2,1,0:T(2,128)}, u32[]{:S(2)}) copy-start(f32[1,20,2,384]{3,2,1,0:T(2,128)} %get-tuple-element.28) | copy-start | bytes 184324
  33.6 3.1 %copy-start.9 = (f32[1,20,2,384]{3,2,1,0:T(2,128)S(1)}, f32[1,20,2,384]{3,2,1,0:T(2,128)}, u32[]{:S(2)}) copy-start(f32[1,20,2,384]{3,2,1,0:T(2,128)} %get-tuple-element.57) | copy-start | bytes 184324
  33.6 3.1 %copy-start.11 = (f32[1,20,2,384]{3,2,1,0:T(2,128)S(1)}, f32[1,20,2,384]{3,2,1,0:T(2,128)}, u32[]{:S(2)}) copy-start(f32[1,20,2,384]{3,2,1,0:T(2,128)} %get-tuple-element.22) | copy-start | bytes 184324
  33.6 5.1 %copy-start.6 = (f32[1,20,2,384]{3,2,1,0:T(2,128)S(1)}, f32[1,20,2,384]{3,2,1,0:T(2,128)}, u32[]{:S(2)}) copy-start(f32[1,20,2,384]{3,2,1,0:T(2,128)} %get-tuple-element.27) | copy-start | bytes 184324
  33.6 5.1 %copy-start.7 = (f32[1,20,2,384]{3,2,1,0:T(2,128)S(1)}, f32[1,20,2,384]{3,2,1,0:T(2,128)}, u32[]{:S(2)}) copy-start(f32[1,20,2,384]{3,2,1,0:T(2,128)} %get-tuple-element.58) | copy-start | bytes 184324
  33.6 5.1 %copy-start.10 = (f32[1,20,2,384]{3,2,1,0:T(2,128)S(1)}, f32[1,20,2,384]{3,2,1,0:T(2,128)}, u32[]{:S(2)}) copy-start(f32[1,20,2,384]{3,2,1,0:T(2,128)} %get-tuple-element.21) | copy-start | bytes 184324
  36.5 4.8 %copy-start.2 = (f32[5,20,64,128]{3,2,1,0:T(8,128)}, f32[5,20,64,128]{3,2,1,0:T(8,128)S(1)}, u32[]{:S(2)}) copy-start(f32[5,20,64,128]{3,2,1,0:T(8,128)S(1)} %pad_maximum_fusion.cols_ref) | copy-start | bytes 9830404
  36.5 4.6 %copy-start.5 = (s32[64,384]{1,0:T(8,128)S(1)}, s32[64,384]{1,0:T(8,128)}, u32[]{:S(2)}) copy-start(s32[64,384]{1,0:T(8,128)} %param.13) | copy-start | bytes 294916
  36.7 8.9 %copy-start.12 = (f32[64,384]{1,0:T(8,128)S(1)}, f32[64,384]{1,0:T(8,128)}, u32[]{:S(2)}) copy-start(f32[64,384]{1,0:T(8,128)} %param.16) | copy-start | bytes 294916
  36.9 13.0 %collective-permute-start.2 = (f32[5,20,2,512]{3,2,1,0:T(2,128)S(1)}, f32[5,20,2,512]{3,2,1,0:T(2,128)}, u32[]{:S(2)}, u32[]{:S(2)}) collective-permute-start(f32[5,20,2,512]{3,2,1,0:T(2,128)S(1)} %pad_maximum_fusion.2), channel_id=1, source_target_pairs={{0,112},{16,96},{32,80},{48,64},{64,48},{80,32},{96,16},{112,0},{1... | collective-permute-start | bytes 1228808 | tf_op jit(solution)/shard_map/ppermute | solution.py:223
  39.7 13.9 %copy-start.14 = (f32[5]{0:T(128)S(1)}, f32[5]{0:T(128)}, u32[]{:S(2)}) copy-start(f32[5]{0:T(128)} %constant.29.clone) | copy-start | bytes 64
  39.7 13.9 %collective-permute-start.3 = (f32[5,20,2,512]{3,2,1,0:T(2,128)}, f32[5,20,2,512]{3,2,1,0:T(2,128)}, u32[]{:S(2)}, u32[]{:S(2)}) collective-permute-start(f32[5,20,2,512]{3,2,1,0:T(2,128)} %pad_maximum_fusion.3), channel_id=1, source_target_pairs={{1,0},{2,1},{3,2},{4,3},{5,4},{6,5},{7,6},{8,7},{9,8},{10,9},{11,1... | collective-permute-start | bytes 1228808 | tf_op jit(solution)/shard_map/ppermute | solution.py:221
  41.4 15.2 %copy-start = (f32[20,64,384]{2,1,0:T(8,128)}, f32[20,64,384]{2,1,0:T(8,128)S(1)}, u32[]{:S(2)}) copy-start(f32[20,64,384]{2,1,0:T(8,128)S(1)} %fusion.1.wet_ref) | copy-start | bytes 5898244
  41.4 13.6 %collective-permute-start.4 = (f32[5,20,2,512]{3,2,1,0:T(2,128)S(1)}, f32[5,20,2,512]{3,2,1,0:T(2,128)S(1)}, u32[]{:S(2)}, u32[]{:S(2)}) collective-permute-start(f32[5,20,2,512]{3,2,1,0:T(2,128)S(1)} %pad_maximum_fusion.2), channel_id=1, source_target_pairs={{0,1},{1,2},{2,3},{3,4},{4,5},{5,6},{6,7},{7,8},{8,9},{9,10},{10,1... | collective-permute-start | bytes 1228808 | tf_op jit(solution)/shard_map/ppermute | solution.py:222
  82.9 2.7 %copy-start.1 = (f32[20,64,384]{2,1,0:T(8,128)S(1)}, f32[20,64,384]{2,1,0:T(8,128)}, u32[]{:S(2)}) copy-start(f32[20,64,384]{2,1,0:T(8,128)} %copy-done) | copy-start | bytes 5898244
  82.9 2.7 %copy-start.13 = (f32[64,384]{1,0:T(8,128)S(1)}, f32[64,384]{1,0:T(8,128)}, u32[]{:S(2)}) copy-start(f32[64,384]{1,0:T(8,128)} %param.15) | copy-start | bytes 294916
  82.9 2.7 %slice-start = ((f32[20,64,384]{2,1,0:T(8,128)}), f32[1,64,384]{2,1,0:T(8,128)S(1)}, s32[]{:S(2)}) async-start(f32[20,64,384]{2,1,0:T(8,128)} %copy-done), calls=%async_computation.2 | async-start | bytes 196608 | tf_op jit(solution)/shard_map/slice | solution.py:528
  98.1 7.7 %collective-permute-start.6 = (f32[1,3072]{1,0:T(1,128)S(1)}, f32[1,3072]{1,0:T(1,128)S(1)}, u32[]{:S(2)}, u32[]{:S(2)}) collective-permute-start(f32[1,3072]{1,0:T(1,128)S(1)} %get-tuple-element.47), channel_id=1, source_target_pairs={{16,0},{32,16},{48,32},{64,48},{80,64},{96,80},{112,96},{1,112},{1... | collective-permute-start | bytes 36872 | tf_op jit(solution)/shard_map/ppermute | solution.py:437
  103.1 3.6 %collective-permute-start.5 = (f32[1,3072]{1,0:T(1,128)S(1)}, f32[1,3072]{1,0:T(1,128)S(1)}, u32[]{:S(2)}, u32[]{:S(2)}) collective-permute-start(f32[1,3072]{1,0:T(1,128)S(1)} %get-tuple-element.48), channel_id=1, source_target_pairs={{0,16},{16,32},{32,48},{48,64},{64,80},{80,96},{96,112},{112,1},{1... | collective-permute-start | bytes 36872 | tf_op jit(solution)/shard_map/ppermute | solution.py:440
  109.0 1.2 collective-permute-start.7
  111.6 3.0 %collective-permute-start.8 = (f32[2]{0:T(128)S(1)}, f32[2]{0:T(128)S(1)}, u32[]{:S(2)}, u32[]{:S(2)}) collective-permute-start(f32[2]{0:T(128)S(1)} %fusion.43), channel_id=1, source_target_pairs={{0,32},{16,48},{32,0},{48,16},{64,96},{80,112},{96,64},{112,80},{1... | collective-permute-start | bytes 32 | tf_op jit(solution)/shard_map/ppermute | solution.py:456
  116.0 3.9 %collective-permute-start.9 = (f32[2]{0:T(128)S(1)}, f32[2]{0:T(128)S(1)}, u32[]{:S(2)}, u32[]{:S(2)}) collective-permute-start(f32[2]{0:T(128)S(1)} %fusion.46), channel_id=1, source_target_pairs={{0,64},{16,80},{32,96},{48,112},{64,0},{80,16},{96,32},{112,48},{1... | collective-permute-start | bytes 32 | tf_op jit(solution)/shard_map/ppermute | solution.py:456
  120.0 5.5 %collective-permute-start.10 = (f32[2]{0:T(128)S(1)}, f32[2]{0:T(128)S(1)}, u32[]{:S(2)}, u32[]{:S(2)}) collective-permute-start(f32[2]{0:T(128)S(1)} %add.164), channel_id=1, source_target_pairs={{0,1},{1,0},{2,3},{3,2},{4,5},{5,4},{6,7},{7,6},{8,9},{9,8},{10,11... | collective-permute-start | bytes 32 | tf_op jit(solution)/shard_map/ppermute | solution.py:456
  125.5 6.0 %collective-permute-start.11 = (f32[2]{0:T(128)S(1)}, f32[2]{0:T(128)S(1)}, u32[]{:S(2)}, u32[]{:S(2)}) collective-permute-start(f32[2]{0:T(128)S(1)} %add.165), channel_id=1, source_target_pairs={{0,2},{1,3},{2,0},{3,1},{4,6},{5,7},{6,4},{7,5},{8,10},{9,11},{10,... | collective-permute-start | bytes 32 | tf_op jit(solution)/shard_map/ppermute | solution.py:456
  131.5 8.2 %collective-permute-start.12 = (f32[2]{0:T(128)S(1)}, f32[2]{0:T(128)S(1)}, u32[]{:S(2)}, u32[]{:S(2)}) collective-permute-start(f32[2]{0:T(128)S(1)} %add.166), channel_id=1, source_target_pairs={{0,4},{1,5},{2,6},{3,7},{4,0},{5,1},{6,2},{7,3},{8,12},{9,13},{10,... | collective-permute-start | bytes 32 | tf_op jit(solution)/shard_map/ppermute | solution.py:456
  139.7 4.0 %collective-permute-start.13 = (f32[2]{0:T(128)S(1)}, f32[2]{0:T(128)S(1)}, u32[]{:S(2)}, u32[]{:S(2)}) collective-permute-start(f32[2]{0:T(128)S(1)} %add.167), channel_id=1, source_target_pairs={{0,8},{1,9},{2,10},{3,11},{4,12},{5,13},{6,14},{7,15},{8,0},{9,1},... | collective-permute-start | bytes 32 | tf_op jit(solution)/shard_map/ppermute | solution.py:456
  145.8 12.9 %collective-permute-start.15 = (f32[1,3072]{1,0:T(1,128)S(1)}, f32[1,3072]{1,0:T(1,128)S(1)}, u32[]{:S(2)}, u32[]{:S(2)}) collective-permute-start(f32[1,3072]{1,0:T(1,128)S(1)} %get-tuple-element.45), channel_id=1, source_target_pairs={{16,0},{32,16},{48,32},{64,48},{80,64},{96,80},{112,96},{1,112},{1... | collective-permute-start | bytes 36872 | tf_op jit(solution)/shard_map/ppermute | solution.py:437
  156.8 3.1 %collective-permute-start.14 = (f32[1,3072]{1,0:T(1,128)S(1)}, f32[1,3072]{1,0:T(1,128)S(1)}, u32[]{:S(2)}, u32[]{:S(2)}) collective-permute-start(f32[1,3072]{1,0:T(1,128)S(1)} %get-tuple-element.46), channel_id=1, source_target_pairs={{0,16},{16,32},{32,48},{48,64},{64,80},{80,96},{96,112},{112,1},{1... | collective-permute-start | bytes 36872 | tf_op jit(solution)/shard_map/ppermute | solution.py:440
  162.6 1.2 collective-permute-start.16
  165.6 2.7 %collective-permute-start.17 = (f32[3]{0:T(128)S(1)}, f32[3]{0:T(128)S(1)}, u32[]{:S(2)}, u32[]{:S(2)}) collective-permute-start(f32[3]{0:T(128)S(1)} %fusion.42), channel_id=1, source_target_pairs={{0,32},{16,48},{32,0},{48,16},{64,96},{80,112},{96,64},{112,80},{1... | collective-permute-start | bytes 44 | tf_op jit(solution)/shard_map/ppermute | solution.py:456
  170.1 3.9 %collective-permute-start.18 = (f32[3]{0:T(128)S(1)}, f32[3]{0:T(128)S(1)}, u32[]{:S(2)}, u32[]{:S(2)}) collective-permute-start(f32[3]{0:T(128)S(1)} %fusion.45), channel_id=1, source_target_pairs={{0,64},{16,80},{32,96},{48,112},{64,0},{80,16},{96,32},{112,48},{1... | collective-permute-start | bytes 44 | tf_op jit(solution)/shard_map/ppermute | solution.py:456
  174.0 4.1 %collective-permute-start.19 = (f32[3]{0:T(128)S(1)}, f32[3]{0:T(128)S(1)}, u32[]{:S(2)}, u32[]{:S(2)}) collective-permute-start(f32[3]{0:T(128)S(1)} %add.177), channel_id=1, source_target_pairs={{0,1},{1,0},{2,3},{3,2},{4,5},{5,4},{6,7},{7,6},{8,9},{9,8},{10,11... | collective-permute-start | bytes 44 | tf_op jit(solution)/shard_map/ppermute | solution.py:456
  178.2 3.9 %collective-permute-start.20 = (f32[3]{0:T(128)S(1)}, f32[3]{0:T(128)S(1)}, u32[]{:S(2)}, u32[]{:S(2)}) collective-permute-start(f32[3]{0:T(128)S(1)} %add.178), channel_id=1, source_target_pairs={{0,2},{1,3},{2,0},{3,1},{4,6},{5,7},{6,4},{7,5},{8,10},{9,11},{10,... | collective-permute-start | bytes 44 | tf_op jit(solution)/shard_map/ppermute | solution.py:456
  182.1 6.4 %collective-permute-start.21 = (f32[3]{0:T(128)S(1)}, f32[3]{0:T(128)S(1)}, u32[]{:S(2)}, u32[]{:S(2)}) collective-permute-start(f32[3]{0:T(128)S(1)} %add.179), channel_id=1, source_target_pairs={{0,4},{1,5},{2,6},{3,7},{4,0},{5,1},{6,2},{7,3},{8,12},{9,13},{10,... | collective-permute-start | bytes 44 | tf_op jit(solution)/shard_map/ppermute | solution.py:456
  188.5 4.0 %collective-permute-start.22 = (f32[3]{0:T(128)S(1)}, f32[3]{0:T(128)S(1)}, u32[]{:S(2)}, u32[]{:S(2)}) collective-permute-start(f32[3]{0:T(128)S(1)} %add.180), channel_id=1, source_target_pairs={{0,8},{1,9},{2,10},{3,11},{4,12},{5,13},{6,14},{7,15},{8,0},{9,1},... | collective-permute-start | bytes 44 | tf_op jit(solution)/shard_map/ppermute | solution.py:456
  196.9 12.9 %collective-permute-start.24 = (f32[1,3072]{1,0:T(1,128)S(1)}, f32[1,3072]{1,0:T(1,128)S(1)}, u32[]{:S(2)}, u32[]{:S(2)}) collective-permute-start(f32[1,3072]{1,0:T(1,128)S(1)} %get-tuple-element.43), channel_id=1, source_target_pairs={{16,0},{32,16},{48,32},{64,48},{80,64},{96,80},{112,96},{1,112},{1... | collective-permute-start | bytes 36872 | tf_op jit(solution)/shard_map/ppermute | solution.py:437
  207.9 3.1 %collective-permute-start.23 = (f32[1,3072]{1,0:T(1,128)S(1)}, f32[1,3072]{1,0:T(1,128)S(1)}, u32[]{:S(2)}, u32[]{:S(2)}) collective-permute-start(f32[1,3072]{1,0:T(1,128)S(1)} %get-tuple-element.44), channel_id=1, source_target_pairs={{0,16},{16,32},{32,48},{48,64},{64,80},{80,96},{96,112},{112,1},{1... | collective-permute-start | bytes 36872 | tf_op jit(solution)/shard_map/ppermute | solution.py:440
  214.0 1.2 collective-permute-start.25
  217.2 2.7 %collective-permute-start.26 = (f32[3]{0:T(128)S(1)}, f32[3]{0:T(128)S(1)}, u32[]{:S(2)}, u32[]{:S(2)}) collective-permute-start(f32[3]{0:T(128)S(1)} %fusion.41), channel_id=1, source_target_pairs={{0,32},{16,48},{32,0},{48,16},{64,96},{80,112},{96,64},{112,80},{1... | collective-permute-start | bytes 44 | tf_op jit(solution)/shard_map/ppermute | solution.py:456
  222.0 3.9 %collective-permute-start.27 = (f32[3]{0:T(128)S(1)}, f32[3]{0:T(128)S(1)}, u32[]{:S(2)}, u32[]{:S(2)}) collective-permute-start(f32[3]{0:T(128)S(1)} %fusion.44), channel_id=1, source_target_pairs={{0,64},{16,80},{32,96},{48,112},{64,0},{80,16},{96,32},{112,48},{1... | collective-permute-start | bytes 44 | tf_op jit(solution)/shard_map/ppermute | solution.py:456
  225.9 4.1 %collective-permute-start.28 = (f32[3]{0:T(128)S(1)}, f32[3]{0:T(128)S(1)}, u32[]{:S(2)}, u32[]{:S(2)}) collective-permute-start(f32[3]{0:T(128)S(1)} %add.195), channel_id=1, source_target_pairs={{0,1},{1,0},{2,3},{3,2},{4,5},{5,4},{6,7},{7,6},{8,9},{9,8},{10,11... | collective-permute-start | bytes 44 | tf_op jit(solution)/shard_map/ppermute | solution.py:456
  230.0 3.9 %collective-permute-start.29 = (f32[3]{0:T(128)S(1)}, f32[3]{0:T(128)S(1)}, u32[]{:S(2)}, u32[]{:S(2)}) collective-permute-start(f32[3]{0:T(128)S(1)} %add.196), channel_id=1, source_target_pairs={{0,2},{1,3},{2,0},{3,1},{4,6},{5,7},{6,4},{7,5},{8,10},{9,11},{10,... | collective-permute-start | bytes 44 | tf_op jit(solution)/shard_map/ppermute | solution.py:456
  234.0 6.4 %collective-permute-start.30 = (f32[3]{0:T(128)S(1)}, f32[3]{0:T(128)S(1)}, u32[]{:S(2)}, u32[]{:S(2)}) collective-permute-start(f32[3]{0:T(128)S(1)} %add.197), channel_id=1, source_target_pairs={{0,4},{1,5},{2,6},{3,7},{4,0},{5,1},{6,2},{7,3},{8,12},{9,13},{10,... | collective-permute-start | bytes 44 | tf_op jit(solution)/shard_map/ppermute | solution.py:456
  240.4 4.0 %collective-permute-start.31 = (f32[3]{0:T(128)S(1)}, f32[3]{0:T(128)S(1)}, u32[]{:S(2)}, u32[]{:S(2)}) collective-permute-start(f32[3]{0:T(128)S(1)} %add.198), channel_id=1, source_target_pairs={{0,8},{1,9},{2,10},{3,11},{4,12},{5,13},{6,14},{7,15},{8,0},{9,1},... | collective-permute-start | bytes 44 | tf_op jit(solution)/shard_map/ppermute | solution.py:456

commit v4 on v3

--- a/solution.py
+++ b/solution.py
@@ -458,19 +458,57 @@
     return value
 
 
-def solve(surface_source, wet_surface, centre_weight, padder):
-
-    def precondition(residual):
-        return wet_surface * residual / centre_weight
-
-    def apply_operator(field):
-        return nine_point(padder(field), wet_surface, centre_weight)
-
+def neighbour_rows(values):
+    lon_count = lax.axis_size("lon")
+    lat_count = lax.axis_size("lat")
+    strip_count = lon_count * lat_count
+    axes = ("lon", "lat")
+
+    def device(strip):
+        return (strip % lon_count) * lat_count + strip // lon_count
+
+    above = lax.ppermute(
+        values[:, 0:1, :], axes, [(device(s + 1), device(s)) for s in range(strip_count - 1)]
+    )
+    below = lax.ppermute(
+        values[:, -1:, :], axes, [(device(s - 1), device(s)) for s in range(1, strip_count)]
+    )
+    return above, below
+
+
+def strip_assemble(surface_field, above_row, below_row):
+    top_strip = jnp.logical_and(
+        lax.axis_index("lon") == lax.axis_size("lon") - 1,
+        lax.axis_index("lat") == lax.axis_size("lat") - 1,
+    )
+    above_row = jnp.where(top_strip, jnp.flip(surface_field[-1:, :], axis=1), above_row)
+    extended = jnp.concatenate([below_row, surface_field, above_row], axis=0)
+    return jnp.concatenate([extended[:, -1:], extended, extended[:, :1]], axis=1)
+
+
+def solve(surface_source, wet_surface, centre_weight):
+
+    def precondition(residual, wet, weight):
+        return wet * residual / weight
+
+    def apply_operator(field, above, below):
+        return nine_point(strip_assemble(field, above, below), wet_surface, centre_weight)
+
+    rim_above, rim_below = neighbour_rows(jnp.stack([wet_surface, centre_weight, surface_source]))
     solution = jnp.zeros_like(surface_source)
     residual = surface_source
-    precond = precondition(residual)
+    resid_rims = [rim_above[2], rim_below[2]]
+    weight_rims = [
+        (rim[0], jnp.where(rim[1] == 0.0, 1.0, rim[1])) for rim in (rim_above, rim_below)
+    ]
+    precond = precondition(residual, wet_surface, centre_weight)
     direction = precond
-    operator_image = apply_operator(direction)
+    operator_image = apply_operator(
+        direction,
+        *[precondition(r, w, c) for r, (w, c) in zip(resid_rims, weight_rims)],
+    )
+    image_above, image_below = neighbour_rows(operator_image[None])
+    image_rims = [image_above[0], image_below[0]]
     totals = butterfly_sum(
         jnp.stack([jnp.sum(residual * precond), jnp.sum(direction * operator_image)])
     )
@@ -480,8 +518,15 @@
         solution = solution + step_size * direction
         if iteration + 1 < ITERS:
             residual = residual - step_size * operator_image
-            precond = precondition(residual)
-            precond_image = apply_operator(precond)
+            resid_rims = [r - step_size * a for r, a in zip(resid_rims, image_rims)]
+            precond = precondition(residual, wet_surface, centre_weight)
+            precond_image = apply_operator(
+                precond,
+                *[precondition(r, w, c) for r, (w, c) in zip(resid_rims, weight_rims)],
+            )
+            if iteration + 2 < ITERS:
+                fresh_above, fresh_below = neighbour_rows(precond_image[None])
+                fresh_rims = [fresh_above[0], fresh_below[0]]
             totals = butterfly_sum(
                 jnp.stack(
                     [
@@ -496,6 +541,8 @@
             direction = precond + ratio * direction
             curvature = totals[1] + 2.0 * ratio * totals[2] + ratio * ratio * curvature
             operator_image = precond_image + ratio * operator_image
+            if iteration + 2 < ITERS:
+                image_rims = [f + ratio * a for f, a in zip(fresh_rims, image_rims)]
             resid_dot = dot_next
     return solution
 
@@ -535,7 +582,7 @@
         concat_axis=2,
         tiled=True,
     )
-    strip_solution = solve(relaid[0], relaid[1], relaid[2], strip_pad_joined)
+    strip_solution = solve(relaid[0], relaid[1], relaid[2])
     solution = lax.all_to_all(strip_solution, "lon", split_axis=1, concat_axis=0, tiled=True)
     return (new_tracers, solution)
 

time: 265 us -> 260 us (0.981)
  blocking collectives: 25.6 us -> 14.3 us
  waiting for transfers between devices: 34 us -> 45.1 us
  starting transfers between devices: 95.1 us -> 88.8 us
    ppermute x6, starting transfers between devices: 27.1 us -> 14.9 us  [the longest x3 7.46 us: neighbour_rows(): lax.ppermute(values[:, -1:, :], axes, [(device(s - 1), device(s)) for s i...]
    all_to_all x1 -> x0, blocking collectives: 11.3 us -> none  [shards(): lax.all_to_all(jnp.stack([surface_source, wet_surface, centre_weight]), '...]
    all_to_all x0 -> x1, waiting for transfers between devices: none -> 7.72 us  [shards(): lax.all_to_all(jnp.stack([surface_source, wet_surface, centre_weight]), '...]
    ppermute x21, waiting for transfers between devices: 26.7 us -> 33 us  [butterfly_sum(): lax.ppermute(value, axis, [(i, i ^ bit) for i in range(count)])]
    all_to_all x0 -> x1, starting transfers between devices: none -> 4.16 us  [shards(): lax.all_to_all(jnp.stack([surface_source, wet_surface, centre_weight]), '...]
    ppermute x6, waiting for transfers between devices: 3 us -> 0.02 us  [the longest x3 0.01 us: neighbour_rows(): lax.ppermute(values[:, -1:, :], axes, [(device(s - 1), device(s)) for s i...]
  transfers between devices with their start and end apart: 32 -> 33, of which waited for: 25 -> 21; matrix products, arithmetic and copies ran while one was open for 9% -> 13% of each run, Pallas kernels for 0% -> 0%
where the time goes in v4:
time: 260 us; the launch traced here: 258 us
  starting transfers between devices  88.8 us (34%)
  waiting for transfers between devices  45.1 us (17%)
  other arithmetic  37.8 us (15%)
  local copies, waits for them, and re-layouts  36.1 us (14%)
  Pallas kernels  26.4 us (10%)
  blocking collectives  14.3 us (6%)
  between operations  9.43 us (4%)
    ppermute x21, starting transfers between devices, butterfly_sum(): lax.ppermute(value, axis, [(i, i ^ bit) for i in range(count)])  59.7 us
    ppermute x21, waiting for transfers between devices, butterfly_sum(): lax.ppermute(value, axis, [(i, i ^ bit) for i in range(count)])  33 us
    pallas_call x1, Pallas kernels, assembling_call(): pl.pallas_call(assembling_kernel, grid=(level_count,), in_specs=[pl.Block...  20.7 us
    all_to_all x1, blocking collectives, shards(): lax.all_to_all(strip_solution, 'lon', split_axis=1, concat_axis=0, tiled=...  14.3 us
    add x21, other arithmetic, butterfly_sum(): value + lax.ppermute(value, axis, [(i, i ^ bit) for i in range(count)])  10.5 us
    all_to_all x1, waiting for transfers between devices, shards(): lax.all_to_all(jnp.stack([surface_source, wet_surface, centre_weight]), '...  7.72 us
    ppermute x3, starting transfers between devices, neighbour_rows(): lax.ppermute(values[:, -1:, :], axes, [(device(s - 1), device(s)) for s i...  7.46 us
    ppermute x3, starting transfers between devices, neighbour_rows(): lax.ppermute(values[:, 0:1, :], axes, [(device(s + 1), device(s)) for s i...  7.45 us
  transfers between devices with their start and end apart: 33, of which 21 were waited for; matrix products, arithmetic and copies ran while one was open for 13% of the time, Pallas kernels for 0%

profile of v4, /device:TPU:1, one launch (start us, length us, event | category | flops | bytes accessed | tf_op | source)
XLA Modules:
  0.0 258.0 jit_solution(9628891453260321124)
XLA Ops:
  7.9 2.1 slice_convert_fusion.2
  10.3 3.3 %fusion.35 = (f32[2,20,64,2]{3,2,1,0:T(8,128)}, f32[2,20,64,2]{3,2,1,0:T(8,128)S(1)}) fusion(f32[2,20,64,384]{3,2,1,0:T(8,128)} %tracer_ref.1), kind=kLoop, calls=%fused_computation.128 | loop fusion | bytes 81920 | tf_op jit(solution)/shard_map/slice | solution.py:191
  23.9 1.8 slice_convert_fusion.4
  25.7 1.9 fusion.34
  28.5 1.9 copy.50
  30.5 3.1 %copy.51 = f32[5,20,64,2]{3,2,1,0:T(8,128)} copy(f32[5,20,64,2]{2,3,1,0:T(2,128)} %collective-permute-done.1) | data formatting | bytes 102400 | tf_op jit(solution)/shard_map/ppermute | solution.py:205
  33.6 2.9 %pad_maximum_fusion.cols_ref = f32[5,20,64,128]{3,2,1,0:T(8,128)S(1)} fusion(f32[5,20,64,2]{3,2,1,0:T(8,128)} %copy.51, f32[5,20,64,2]{3,2,1,0:T(8,128)S(1)} %copy.50, f32[128]{0:T(128)S(1)} %pad.72.clone), kind=kLoop, calls=%fused_computation | loop fusion | flops 1638400 | bytes 3379712 | tf_op jit(solution)/shard_map/concatenate | solution.py:210
  36.9 1.9 collective-permute-start.2
  41.4 4.2 %collective-permute-start.4 = (f32[5,20,2,512]{3,2,1,0:T(2,128)S(1)}, f32[5,20,2,512]{3,2,1,0:T(2,128)S(1)}, u32[]{:S(2)}, u32[]{:S(2)}) collective-permute-start(f32[5,20,2,512]{3,2,1,0:T(2,128)S(1)} %pad_maximum_fusion.2), channel_id=1, source_target_pairs={{0,1},{1,2},{2,3},{3,4},{4,5},{5,6},{6,7},{7,8},{8,9},{9,10},{10,1... | collective-permute-start | bytes 1228808 | tf_op jit(solution)/shard_map/ppermute | solution.py:222
  45.6 4.3 %collective-permute-done.2 = f32[5,20,2,512]{3,2,1,0:T(2,128)} collective-permute-done((f32[5,20,2,512]{3,2,1,0:T(2,128)S(1)}, f32[5,20,2,512]{3,2,1,0:T(2,128)}, u32[]{:S(2)}, u32[]{:S(2)}) %collective-permute-start.2) | collective-permute-done | bytes 409632 | tf_op jit(solution)/shard_map/ppermute | solution.py:223
  56.5 20.7 %shard_map.104.values_ref = f32[2,20,64,384]{3,2,1,0:T(8,128)} custom-call(f32[2,20,64,384]{3,2,1,0:T(8,128)} %tracer_ref.1, f32[20,64,384]{2,1,0:T(8,128)} %copy-done, bf16[20,64,384]{2,1,0:T(8,128)(2,1)} %east_ref.1, bf16[20,64,384]{2,1,0:T(8,128)(2,1)} %north_ref.1, f32[5,20,64,128]{3,2,1,0:T(8,128)} %copy-done.2, ...), custom_call_target="tpu_custom_call" | custom-call | tf_op jit(solution)/shard_map/pallas_call | solution.py:239
  77.2 5.7 %shard_map.105 = f32[2,20,64,384]{3,2,1,0:T(8,128)} custom-call(f32[2,20,64,384]{3,2,1,0:T(8,128)} %shard_map.104.values_ref, f32[20,64,384]{2,1,0:T(8,128)} %copy-done, bf16[20,64,384]{2,1,0:T(8,128)(2,1)} %diff_ref.1), custom_call_target="tpu_custom_call" | custom-call | tf_op jit(solution)/shard_map/pallas_call | solution.py:336
  82.9 2.5 fusion
  86.7 4.2 %all-to-all-start = ((f32[3,64,384]{2,0,1:T(4,128)}), f32[3,64,384]{2,0,1:T(4,128)S(1)}, u32[]{:S(2)}, u32[]{:S(2)}) async-start(f32[3,64,384]{2,0,1:T(4,128)} %copy.52), calls=%async_computation | async-start | bytes 786432 | tf_op jit(solution)/shard_map/all_to_all | solution.py:578
  90.8 7.7 %all-to-all-done = f32[3,64,384]{2,0,1:T(4,128)S(1)} async-done(((f32[3,64,384]{2,0,1:T(4,128)}), f32[3,64,384]{2,0,1:T(4,128)S(1)}, u32[]{:S(2)}, u32[]{:S(2)}) %all-to-all-start) | async-done | bytes 294944 | tf_op jit(solution)/shard_map/all_to_all | solution.py:578
  99.6 3.1 %collective-permute-start.6 = (f32[3,1,3072]{2,1,0:T(1,128)S(1)}, f32[3,1,3072]{2,1,0:T(1,128)S(1)}, u32[]{:S(2)}, u32[]{:S(2)}) collective-permute-start(f32[3,1,3072]{2,1,0:T(1,128)S(1)} %get-tuple-element.41), channel_id=1, source_target_pairs={{16,0},{32,16},{48,32},{64,48},{80,64},{96,80},{112,96},{1,112},{1... | collective-permute-start | bytes 110600 | tf_op jit(solution)/shard_map/ppermute | solution.py:470
  102.8 2.4 collective-permute-start.5
  105.3 2.1 rev.12
  109.9 3.1 %collective-permute-start.14 = (f32[1,1,3072]{2,1,0:T(1,128)S(1)}, f32[1,1,3072]{2,1,0:T(1,128)S(1)}, u32[]{:S(2)}, u32[]{:S(2)}) collective-permute-start(f32[1,1,3072]{2,1,0:T(1,128)S(1)} %get-tuple-element.50), channel_id=1, source_target_pairs={{0,16},{16,32},{32,48},{48,64},{64,80},{80,96},{96,112},{112,1},{1... | collective-permute-start | bytes 36872 | tf_op jit(solution)/shard_map/ppermute | solution.py:473
  113.0 1.9 collective-permute-start.15
  116.9 1.8 collective-permute-done.8
  120.1 5.3 %collective-permute-start.9 = (f32[2]{0:T(128)S(1)}, f32[2]{0:T(128)S(1)}, u32[]{:S(2)}, u32[]{:S(2)}) collective-permute-start(f32[2]{0:T(128)S(1)} %fusion.50), channel_id=1, source_target_pairs={{0,64},{16,80},{32,96},{48,112},{64,0},{80,16},{96,32},{112,48},{1... | collective-permute-start | bytes 32 | tf_op jit(solution)/shard_map/ppermute | solution.py:456
  128.9 9.4 %collective-permute-start.11 = (f32[2]{0:T(128)S(1)}, f32[2]{0:T(128)S(1)}, u32[]{:S(2)}, u32[]{:S(2)}) collective-permute-start(f32[2]{0:T(128)S(1)} %add.189), channel_id=1, source_target_pairs={{0,2},{1,3},{2,0},{3,1},{4,6},{5,7},{6,4},{7,5},{8,10},{9,11},{10,... | collective-permute-start | bytes 32 | tf_op jit(solution)/shard_map/ppermute | solution.py:456
  139.3 2.6 %collective-permute-start.12 = (f32[2]{0:T(128)S(1)}, f32[2]{0:T(128)S(1)}, u32[]{:S(2)}, u32[]{:S(2)}) collective-permute-start(f32[2]{0:T(128)S(1)} %add.190), channel_id=1, source_target_pairs={{0,4},{1,5},{2,6},{3,7},{4,0},{5,1},{6,2},{7,3},{8,12},{9,13},{10,... | collective-permute-start | bytes 32 | tf_op jit(solution)/shard_map/ppermute | solution.py:456
  142.9 3.1 %collective-permute-start.13 = (f32[2]{0:T(128)S(1)}, f32[2]{0:T(128)S(1)}, u32[]{:S(2)}, u32[]{:S(2)}) collective-permute-start(f32[2]{0:T(128)S(1)} %add.191), channel_id=1, source_target_pairs={{0,8},{1,9},{2,10},{3,11},{4,12},{5,13},{6,14},{7,15},{8,0},{9,1},... | collective-permute-start | bytes 32 | tf_op jit(solution)/shard_map/ppermute | solution.py:456
  148.9 2.1 rev.13
  152.1 1.9 pad_maximum_fusion.26
  154.0 11.8 %collective-permute-start.16 = (f32[3]{0:T(128)S(1)}, f32[3]{0:T(128)S(1)}, u32[]{:S(2)}, u32[]{:S(2)}) collective-permute-start(f32[3]{0:T(128)S(1)} %pad_maximum_fusion.26), channel_id=1, source_target_pairs={{0,16},{16,0},{32,48},{48,32},{64,80},{80,64},{96,112},{112,96},{1... | collective-permute-start | bytes 44 | tf_op jit(solution)/shard_map/ppermute | solution.py:456
  165.8 1.9 collective-permute-start.23
  167.8 2.4 collective-permute-start.24
  170.2 1.9 fusion.46
  172.1 2.4 collective-permute-done.17
  174.5 1.9 fusion.49
  177.7 2.7 %collective-permute-done.18 = f32[3]{0:T(128)S(1)} collective-permute-done((f32[3]{0:T(128)S(1)}, f32[3]{0:T(128)S(1)}, u32[]{:S(2)}, u32[]{:S(2)}) %collective-permute-start.18) | collective-permute-done | bytes 44 | tf_op jit(solution)/shard_map/ppermute | solution.py:456
  180.3 2.4 collective-permute-done.19
  182.8 2.3 collective-permute-start.20
  189.5 3.1 %collective-permute-start.22 = (f32[3]{0:T(128)S(1)}, f32[3]{0:T(128)S(1)}, u32[]{:S(2)}, u32[]{:S(2)}) collective-permute-start(f32[3]{0:T(128)S(1)} %add.204), channel_id=1, source_target_pairs={{0,8},{1,9},{2,10},{3,11},{4,12},{5,13},{6,14},{7,15},{8,0},{9,1},... | collective-permute-start | bytes 44 | tf_op jit(solution)/shard_map/ppermute | solution.py:456
  197.9 2.1 rev.14
  201.1 2.0 pad_maximum_fusion.27
  203.1 11.9 %collective-permute-start.25 = (f32[3]{0:T(128)S(1)}, f32[3]{0:T(128)S(1)}, u32[]{:S(2)}, u32[]{:S(2)}) collective-permute-start(f32[3]{0:T(128)S(1)} %pad_maximum_fusion.27), channel_id=1, source_target_pairs={{0,16},{16,0},{32,48},{48,32},{64,80},{80,64},{96,112},{112,96},{1... | collective-permute-start | bytes 44 | tf_op jit(solution)/shard_map/ppermute | solution.py:456
  215.9 2.0 fusion.45
  217.9 2.4 collective-permute-done.26
  220.3 2.0 fusion.48
  222.3 3.9 %collective-permute-done.27 = f32[3]{0:T(128)S(1)} collective-permute-done((f32[3]{0:T(128)S(1)}, f32[3]{0:T(128)S(1)}, u32[]{:S(2)}, u32[]{:S(2)}) %collective-permute-start.27) | collective-permute-done | bytes 44 | tf_op jit(solution)/shard_map/ppermute | solution.py:456
  226.2 2.4 collective-permute-done.28
  228.7 3.9 %collective-permute-done.29 = f32[3]{0:T(128)S(1)} collective-permute-done((f32[3]{0:T(128)S(1)}, f32[3]{0:T(128)S(1)}, u32[]{:S(2)}, u32[]{:S(2)}) %collective-permute-start.29) | collective-permute-done | bytes 44 | tf_op jit(solution)/shard_map/ppermute | solution.py:456
  235.2 3.1 %collective-permute-start.31 = (f32[3]{0:T(128)S(1)}, f32[3]{0:T(128)S(1)}, u32[]{:S(2)}, u32[]{:S(2)}) collective-permute-start(f32[3]{0:T(128)S(1)} %add.224), channel_id=1, source_target_pairs={{0,8},{1,9},{2,10},{3,11},{4,12},{5,13},{6,14},{7,15},{8,0},{9,1},... | collective-permute-start | bytes 44 | tf_op jit(solution)/shard_map/ppermute | solution.py:456
  243.1 14.3 %all_to_all.34 = f32[8,8,384]{2,0,1:T(8,128)S(1)} all-to-all(f32[8,8,384]{2,0,1:T(8,128)S(1)} %bitcast.160), channel_id=1, replica_groups=mesh['lon'=8,'lat'=16] {'lon'}, dimensions={1} | all-to-all | bytes 196608 | tf_op jit(solution)/shard_map/all_to_all | solution.py:586
  (161 shorter events, 58.6 us)
Async XLA Ops:
  16.1 12.4 %collective-permute-start = (f32[5,20,64,2]{2,3,1,0:T(2,128)}, f32[5,20,64,2]{2,3,1,0:T(2,128)}, u32[]{:S(2)}, u32[]{:S(2)}) collective-permute-start(f32[5,20,64,2]{2,3,1,0:T(2,128)} %pad_maximum_fusion.17), channel_id=1, source_target_pairs={{0,112},{16,0},{32,16},{48,32},{64,48},{80,64},{96,80},{112,96},{1... | collective-permute-start | bytes 153608 | tf_op jit(solution)/shard_map/ppermute | solution.py:200
  22.7 7.8 %collective-permute-start.1 = (f32[5,20,64,2]{2,3,1,0:T(2,128)}, f32[5,20,64,2]{2,3,1,0:T(2,128)}, u32[]{:S(2)}, u32[]{:S(2)}) collective-permute-start(f32[5,20,64,2]{2,3,1,0:T(2,128)} %pad_maximum_fusion.18), channel_id=1, source_target_pairs={{0,16},{16,32},{32,48},{48,64},{64,80},{80,96},{96,112},{112,0},{1... | collective-permute-start | bytes 153608 | tf_op jit(solution)/shard_map/ppermute | solution.py:205
  33.6 3.1 %copy-start.4 = (f32[2,20,2,384]{3,2,1,0:T(2,128)S(1)}, f32[2,20,2,384]{3,2,1,0:T(2,128)}, u32[]{:S(2)}) copy-start(f32[2,20,2,384]{3,2,1,0:T(2,128)} %get-tuple-element.16) | copy-start | bytes 368644
  33.6 3.1 %copy-start.8 = (f32[1,20,2,384]{3,2,1,0:T(2,128)S(1)}, f32[1,20,2,384]{3,2,1,0:T(2,128)}, u32[]{:S(2)}) copy-start(f32[1,20,2,384]{3,2,1,0:T(2,128)} %get-tuple-element.28) | copy-start | bytes 184324
  33.6 3.1 %copy-start.9 = (f32[1,20,2,384]{3,2,1,0:T(2,128)S(1)}, f32[1,20,2,384]{3,2,1,0:T(2,128)}, u32[]{:S(2)}) copy-start(f32[1,20,2,384]{3,2,1,0:T(2,128)} %get-tuple-element.60) | copy-start | bytes 184324
  33.6 3.1 %copy-start.11 = (f32[1,20,2,384]{3,2,1,0:T(2,128)S(1)}, f32[1,20,2,384]{3,2,1,0:T(2,128)}, u32[]{:S(2)}) copy-start(f32[1,20,2,384]{3,2,1,0:T(2,128)} %get-tuple-element.22) | copy-start | bytes 184324
  33.6 5.1 %copy-start.6 = (f32[1,20,2,384]{3,2,1,0:T(2,128)S(1)}, f32[1,20,2,384]{3,2,1,0:T(2,128)}, u32[]{:S(2)}) copy-start(f32[1,20,2,384]{3,2,1,0:T(2,128)} %get-tuple-element.27) | copy-start | bytes 184324
  33.6 5.1 %copy-start.7 = (f32[1,20,2,384]{3,2,1,0:T(2,128)S(1)}, f32[1,20,2,384]{3,2,1,0:T(2,128)}, u32[]{:S(2)}) copy-start(f32[1,20,2,384]{3,2,1,0:T(2,128)} %get-tuple-element.61) | copy-start | bytes 184324
  33.6 5.1 %copy-start.10 = (f32[1,20,2,384]{3,2,1,0:T(2,128)S(1)}, f32[1,20,2,384]{3,2,1,0:T(2,128)}, u32[]{:S(2)}) copy-start(f32[1,20,2,384]{3,2,1,0:T(2,128)} %get-tuple-element.21) | copy-start | bytes 184324
  36.5 4.8 %copy-start.2 = (f32[5,20,64,128]{3,2,1,0:T(8,128)}, f32[5,20,64,128]{3,2,1,0:T(8,128)S(1)}, u32[]{:S(2)}) copy-start(f32[5,20,64,128]{3,2,1,0:T(8,128)S(1)} %pad_maximum_fusion.cols_ref) | copy-start | bytes 9830404
  36.5 4.6 %copy-start.5 = (s32[64,384]{1,0:T(8,128)S(1)}, s32[64,384]{1,0:T(8,128)}, u32[]{:S(2)}) copy-start(s32[64,384]{1,0:T(8,128)} %param.13) | copy-start | bytes 294916
  36.7 8.9 %copy-start.12 = (f32[64,384]{1,0:T(8,128)S(1)}, f32[64,384]{1,0:T(8,128)}, u32[]{:S(2)}) copy-start(f32[64,384]{1,0:T(8,128)} %param.16) | copy-start | bytes 294916
  36.9 13.0 %collective-permute-start.2 = (f32[5,20,2,512]{3,2,1,0:T(2,128)S(1)}, f32[5,20,2,512]{3,2,1,0:T(2,128)}, u32[]{:S(2)}, u32[]{:S(2)}) collective-permute-start(f32[5,20,2,512]{3,2,1,0:T(2,128)S(1)} %pad_maximum_fusion.2), channel_id=1, source_target_pairs={{0,112},{16,96},{32,80},{48,64},{64,48},{80,32},{96,16},{112,0},{1... | collective-permute-start | bytes 1228808 | tf_op jit(solution)/shard_map/ppermute | solution.py:223
  39.7 13.9 %copy-start.14 = (f32[5]{0:T(128)S(1)}, f32[5]{0:T(128)}, u32[]{:S(2)}) copy-start(f32[5]{0:T(128)} %constant.32.clone) | copy-start | bytes 64
  39.7 13.9 %collective-permute-start.3 = (f32[5,20,2,512]{3,2,1,0:T(2,128)}, f32[5,20,2,512]{3,2,1,0:T(2,128)}, u32[]{:S(2)}, u32[]{:S(2)}) collective-permute-start(f32[5,20,2,512]{3,2,1,0:T(2,128)} %pad_maximum_fusion.3), channel_id=1, source_target_pairs={{1,0},{2,1},{3,2},{4,3},{5,4},{6,5},{7,6},{8,7},{9,8},{10,9},{11,1... | collective-permute-start | bytes 1228808 | tf_op jit(solution)/shard_map/ppermute | solution.py:221
  41.3 15.2 %copy-start = (f32[20,64,384]{2,1,0:T(8,128)}, f32[20,64,384]{2,1,0:T(8,128)S(1)}, u32[]{:S(2)}) copy-start(f32[20,64,384]{2,1,0:T(8,128)S(1)} %fusion.1.wet_ref) | copy-start | bytes 5898244
  41.4 13.6 %collective-permute-start.4 = (f32[5,20,2,512]{3,2,1,0:T(2,128)S(1)}, f32[5,20,2,512]{3,2,1,0:T(2,128)S(1)}, u32[]{:S(2)}, u32[]{:S(2)}) collective-permute-start(f32[5,20,2,512]{3,2,1,0:T(2,128)S(1)} %pad_maximum_fusion.2), channel_id=1, source_target_pairs={{0,1},{1,2},{2,3},{3,4},{4,5},{5,6},{6,7},{7,8},{8,9},{9,10},{10,1... | collective-permute-start | bytes 1228808 | tf_op jit(solution)/shard_map/ppermute | solution.py:222
  82.9 2.7 %copy-start.1 = (f32[20,64,384]{2,1,0:T(8,128)S(1)}, f32[20,64,384]{2,1,0:T(8,128)}, u32[]{:S(2)}) copy-start(f32[20,64,384]{2,1,0:T(8,128)} %copy-done) | copy-start | bytes 5898244
  82.9 2.7 %copy-start.13 = (f32[64,384]{1,0:T(8,128)S(1)}, f32[64,384]{1,0:T(8,128)}, u32[]{:S(2)}) copy-start(f32[64,384]{1,0:T(8,128)} %param.15) | copy-start | bytes 294916
  82.9 2.7 %slice-start = ((f32[20,64,384]{2,1,0:T(8,128)}), f32[1,64,384]{2,1,0:T(8,128)S(1)}, s32[]{:S(2)}) async-start(f32[20,64,384]{2,1,0:T(8,128)} %copy-done), calls=%async_computation.2 | async-start | bytes 196608 | tf_op jit(solution)/shard_map/slice | solution.py:575
  86.7 11.9 %all-to-all-start = ((f32[3,64,384]{2,0,1:T(4,128)}), f32[3,64,384]{2,0,1:T(4,128)S(1)}, u32[]{:S(2)}, u32[]{:S(2)}) async-start(f32[3,64,384]{2,0,1:T(4,128)} %copy.52), calls=%async_computation | async-start | bytes 786432 | tf_op jit(solution)/shard_map/all_to_all | solution.py:578
  99.6 7.9 %collective-permute-start.6 = (f32[3,1,3072]{2,1,0:T(1,128)S(1)}, f32[3,1,3072]{2,1,0:T(1,128)S(1)}, u32[]{:S(2)}, u32[]{:S(2)}) collective-permute-start(f32[3,1,3072]{2,1,0:T(1,128)S(1)} %get-tuple-element.41), channel_id=1, source_target_pairs={{16,0},{32,16},{48,32},{64,48},{80,64},{96,80},{112,96},{1,112},{1... | collective-permute-start | bytes 110600 | tf_op jit(solution)/shard_map/ppermute | solution.py:470
  102.8 4.6 %collective-permute-start.5 = (f32[3,1,3072]{2,1,0:T(1,128)S(1)}, f32[3,1,3072]{2,1,0:T(1,128)S(1)}, u32[]{:S(2)}, u32[]{:S(2)}) collective-permute-start(f32[3,1,3072]{2,1,0:T(1,128)S(1)} %get-tuple-element.40), channel_id=1, source_target_pairs={{0,16},{16,32},{32,48},{48,64},{64,80},{80,96},{96,112},{112,1},{1... | collective-permute-start | bytes 110600 | tf_op jit(solution)/shard_map/ppermute | solution.py:473
  109.8 5.1 %collective-permute-start.7 = (f32[2]{0:T(128)S(1)}, f32[2]{0:T(128)S(1)}, u32[]{:S(2)}, u32[]{:S(2)}) collective-permute-start(f32[2]{0:T(128)S(1)} %pad_maximum_fusion.25), channel_id=1, source_target_pairs={{0,16},{16,0},{32,48},{48,32},{64,80},{80,64},{96,112},{112,96},{1... | collective-permute-start | bytes 32 | tf_op jit(solution)/shard_map/ppermute | solution.py:456
  109.9 41.1 %collective-permute-start.14 = (f32[1,1,3072]{2,1,0:T(1,128)S(1)}, f32[1,1,3072]{2,1,0:T(1,128)S(1)}, u32[]{:S(2)}, u32[]{:S(2)}) collective-permute-start(f32[1,1,3072]{2,1,0:T(1,128)S(1)} %get-tuple-element.50), channel_id=1, source_target_pairs={{0,16},{16,32},{32,48},{48,64},{64,80},{80,96},{96,112},{112,1},{1... | collective-permute-start | bytes 36872 | tf_op jit(solution)/shard_map/ppermute | solution.py:473
  113.0 38.0 %collective-permute-start.15 = (f32[1,1,3072]{2,1,0:T(1,128)S(1)}, f32[1,1,3072]{2,1,0:T(1,128)S(1)}, u32[]{:S(2)}, u32[]{:S(2)}) collective-permute-start(f32[1,1,3072]{2,1,0:T(1,128)S(1)} %get-tuple-element.51), channel_id=1, source_target_pairs={{16,0},{32,16},{48,32},{64,48},{80,64},{96,80},{112,96},{1,112},{1... | collective-permute-start | bytes 36872 | tf_op jit(solution)/shard_map/ppermute | solution.py:470
  116.3 2.4 collective-permute-start.8
  120.1 6.2 %collective-permute-start.9 = (f32[2]{0:T(128)S(1)}, f32[2]{0:T(128)S(1)}, u32[]{:S(2)}, u32[]{:S(2)}) collective-permute-start(f32[2]{0:T(128)S(1)} %fusion.50), channel_id=1, source_target_pairs={{0,64},{16,80},{32,96},{48,112},{64,0},{80,16},{96,32},{112,48},{1... | collective-permute-start | bytes 32 | tf_op jit(solution)/shard_map/ppermute | solution.py:456
  126.3 2.6 %collective-permute-start.10 = (f32[2]{0:T(128)S(1)}, f32[2]{0:T(128)S(1)}, u32[]{:S(2)}, u32[]{:S(2)}) collective-permute-start(f32[2]{0:T(128)S(1)} %add.188), channel_id=1, source_target_pairs={{0,1},{1,0},{2,3},{3,2},{4,5},{5,4},{6,7},{7,6},{8,9},{9,8},{10,11... | collective-permute-start | bytes 32 | tf_op jit(solution)/shard_map/ppermute | solution.py:456
  128.9 10.4 %collective-permute-start.11 = (f32[2]{0:T(128)S(1)}, f32[2]{0:T(128)S(1)}, u32[]{:S(2)}, u32[]{:S(2)}) collective-permute-start(f32[2]{0:T(128)S(1)} %add.189), channel_id=1, source_target_pairs={{0,2},{1,3},{2,0},{3,1},{4,6},{5,7},{6,4},{7,5},{8,10},{9,11},{10,... | collective-permute-start | bytes 32 | tf_op jit(solution)/shard_map/ppermute | solution.py:456
  139.3 3.5 %collective-permute-start.12 = (f32[2]{0:T(128)S(1)}, f32[2]{0:T(128)S(1)}, u32[]{:S(2)}, u32[]{:S(2)}) collective-permute-start(f32[2]{0:T(128)S(1)} %add.190), channel_id=1, source_target_pairs={{0,4},{1,5},{2,6},{3,7},{4,0},{5,1},{6,2},{7,3},{8,12},{9,13},{10,... | collective-permute-start | bytes 32 | tf_op jit(solution)/shard_map/ppermute | solution.py:456
  142.9 4.0 %collective-permute-start.13 = (f32[2]{0:T(128)S(1)}, f32[2]{0:T(128)S(1)}, u32[]{:S(2)}, u32[]{:S(2)}) collective-permute-start(f32[2]{0:T(128)S(1)} %add.191), channel_id=1, source_target_pairs={{0,8},{1,9},{2,10},{3,11},{4,12},{5,13},{6,14},{7,15},{8,0},{9,1},... | collective-permute-start | bytes 32 | tf_op jit(solution)/shard_map/ppermute | solution.py:456
  154.0 16.2 %collective-permute-start.16 = (f32[3]{0:T(128)S(1)}, f32[3]{0:T(128)S(1)}, u32[]{:S(2)}, u32[]{:S(2)}) collective-permute-start(f32[3]{0:T(128)S(1)} %pad_maximum_fusion.26), channel_id=1, source_target_pairs={{0,16},{16,0},{32,48},{48,32},{64,80},{80,64},{96,112},{112,96},{1... | collective-permute-start | bytes 44 | tf_op jit(solution)/shard_map/ppermute | solution.py:456
  165.8 34.2 %collective-permute-start.23 = (f32[1,1,3072]{2,1,0:T(1,128)S(1)}, f32[1,1,3072]{2,1,0:T(1,128)S(1)}, u32[]{:S(2)}, u32[]{:S(2)}) collective-permute-start(f32[1,1,3072]{2,1,0:T(1,128)S(1)} %get-tuple-element.48), channel_id=1, source_target_pairs={{0,16},{16,32},{32,48},{48,64},{64,80},{80,96},{96,112},{112,1},{1... | collective-permute-start | bytes 36872 | tf_op jit(solution)/shard_map/ppermute | solution.py:473
  167.8 32.3 %collective-permute-start.24 = (f32[1,1,3072]{2,1,0:T(1,128)S(1)}, f32[1,1,3072]{2,1,0:T(1,128)S(1)}, u32[]{:S(2)}, u32[]{:S(2)}) collective-permute-start(f32[1,1,3072]{2,1,0:T(1,128)S(1)} %get-tuple-element.49), channel_id=1, source_target_pairs={{16,0},{32,16},{48,32},{64,48},{80,64},{96,80},{112,96},{1,112},{1... | collective-permute-start | bytes 36872 | tf_op jit(solution)/shard_map/ppermute | solution.py:470
  172.1 2.4 collective-permute-start.17
  176.4 3.9 %collective-permute-start.18 = (f32[3]{0:T(128)S(1)}, f32[3]{0:T(128)S(1)}, u32[]{:S(2)}, u32[]{:S(2)}) collective-permute-start(f32[3]{0:T(128)S(1)} %fusion.49), channel_id=1, source_target_pairs={{0,64},{16,80},{32,96},{48,112},{64,0},{80,16},{96,32},{112,48},{1... | collective-permute-start | bytes 44 | tf_op jit(solution)/shard_map/ppermute | solution.py:456
  180.3 2.4 collective-permute-start.19
  182.8 3.9 %collective-permute-start.20 = (f32[3]{0:T(128)S(1)}, f32[3]{0:T(128)S(1)}, u32[]{:S(2)}, u32[]{:S(2)}) collective-permute-start(f32[3]{0:T(128)S(1)} %add.202), channel_id=1, source_target_pairs={{0,2},{1,3},{2,0},{3,1},{4,6},{5,7},{6,4},{7,5},{8,10},{9,11},{10,... | collective-permute-start | bytes 44 | tf_op jit(solution)/shard_map/ppermute | solution.py:456
  186.7 2.8 %collective-permute-start.21 = (f32[3]{0:T(128)S(1)}, f32[3]{0:T(128)S(1)}, u32[]{:S(2)}, u32[]{:S(2)}) collective-permute-start(f32[3]{0:T(128)S(1)} %add.203), channel_id=1, source_target_pairs={{0,4},{1,5},{2,6},{3,7},{4,0},{5,1},{6,2},{7,3},{8,12},{9,13},{10,... | collective-permute-start | bytes 44 | tf_op jit(solution)/shard_map/ppermute | solution.py:456
  189.5 4.0 %collective-permute-start.22 = (f32[3]{0:T(128)S(1)}, f32[3]{0:T(128)S(1)}, u32[]{:S(2)}, u32[]{:S(2)}) collective-permute-start(f32[3]{0:T(128)S(1)} %add.204), channel_id=1, source_target_pairs={{0,8},{1,9},{2,10},{3,11},{4,12},{5,13},{6,14},{7,15},{8,0},{9,1},... | collective-permute-start | bytes 44 | tf_op jit(solution)/shard_map/ppermute | solution.py:456
  203.1 12.7 %collective-permute-start.25 = (f32[3]{0:T(128)S(1)}, f32[3]{0:T(128)S(1)}, u32[]{:S(2)}, u32[]{:S(2)}) collective-permute-start(f32[3]{0:T(128)S(1)} %pad_maximum_fusion.27), channel_id=1, source_target_pairs={{0,16},{16,0},{32,48},{48,32},{64,80},{80,64},{96,112},{112,96},{1... | collective-permute-start | bytes 44 | tf_op jit(solution)/shard_map/ppermute | solution.py:456
  217.9 2.4 collective-permute-start.26
  222.3 3.9 %collective-permute-start.27 = (f32[3]{0:T(128)S(1)}, f32[3]{0:T(128)S(1)}, u32[]{:S(2)}, u32[]{:S(2)}) collective-permute-start(f32[3]{0:T(128)S(1)} %fusion.48), channel_id=1, source_target_pairs={{0,64},{16,80},{32,96},{48,112},{64,0},{80,16},{96,32},{112,48},{1... | collective-permute-start | bytes 44 | tf_op jit(solution)/shard_map/ppermute | solution.py:456
  226.2 2.4 collective-permute-start.28
  228.7 3.9 %collective-permute-start.29 = (f32[3]{0:T(128)S(1)}, f32[3]{0:T(128)S(1)}, u32[]{:S(2)}, u32[]{:S(2)}) collective-permute-start(f32[3]{0:T(128)S(1)} %add.222), channel_id=1, source_target_pairs={{0,2},{1,3},{2,0},{3,1},{4,6},{5,7},{6,4},{7,5},{8,10},{9,11},{10,... | collective-permute-start | bytes 44 | tf_op jit(solution)/shard_map/ppermute | solution.py:456
  232.6 2.6 %collective-permute-start.30 = (f32[3]{0:T(128)S(1)}, f32[3]{0:T(128)S(1)}, u32[]{:S(2)}, u32[]{:S(2)}) collective-permute-start(f32[3]{0:T(128)S(1)} %add.223), channel_id=1, source_target_pairs={{0,4},{1,5},{2,6},{3,7},{4,0},{5,1},{6,2},{7,3},{8,12},{9,13},{10,... | collective-permute-start | bytes 44 | tf_op jit(solution)/shard_map/ppermute | solution.py:456
  235.2 4.0 %collective-permute-start.31 = (f32[3]{0:T(128)S(1)}, f32[3]{0:T(128)S(1)}, u32[]{:S(2)}, u32[]{:S(2)}) collective-permute-start(f32[3]{0:T(128)S(1)} %add.224), channel_id=1, source_target_pairs={{0,8},{1,9},{2,10},{3,11},{4,12},{5,13},{6,14},{7,15},{8,0},{9,1},... | collective-permute-start | bytes 44 | tf_op jit(solution)/shard_map/ppermute | solution.py:456
  (1 other events, 2.6 us)

commit v5 on v4

--- a/solution.py
+++ b/solution.py
@@ -290,7 +290,7 @@
     )(ext)
 
 
-def mix_kernel(values_ref, wet_ref, diff_ref, out_ref, ratio_ref):
+def mix_kernel(values_ref, wet_ref, diff_ref, forcing_ref, out_ref, source_ref, ratio_ref):
     level_count = wet_ref.shape[0]
     tracer_count = values_ref.shape[0]
 
@@ -323,14 +323,17 @@
             reduced[t] = source / divisor
             out_ref[t, k] = reduced[t]
     result = reduced
+    contrast = result[0] - result[1]
     for k in range(level_count - 2, -1, -1):
         ratio = ratio_ref[k]
         for t in range(tracer_count):
             result[t] = out_ref[t, k] - ratio * result[t]
             out_ref[t, k] = result[t]
-
-
-def vertical_mix(values, wet_mask, diffusivity):
+        contrast = contrast + (result[0] - result[1])
+    source_ref[...] = wet_ref[0] * (forcing_ref[...] + contrast / level_count)
+
+
+def vertical_mix(values, wet_mask, diffusivity, forcing):
     tracer_count, level_count, row_count, col_count = values.shape
     rows = 16 if row_count % 16 == 0 else row_count
     return pl.pallas_call(
@@ -340,11 +343,18 @@
             pl.BlockSpec((tracer_count, level_count, rows, col_count), lambda i: (0, 0, i, 0)),
             pl.BlockSpec((level_count, rows, col_count), lambda i: (0, i, 0)),
             pl.BlockSpec((level_count, rows, col_count), lambda i: (0, i, 0)),
+            pl.BlockSpec((rows, col_count), lambda i: (i, 0)),
         ],
-        out_specs=pl.BlockSpec((tracer_count, level_count, rows, col_count), lambda i: (0, 0, i, 0)),
-        out_shape=jax.ShapeDtypeStruct(values.shape, jnp.float32),
+        out_specs=[
+            pl.BlockSpec((tracer_count, level_count, rows, col_count), lambda i: (0, 0, i, 0)),
+            pl.BlockSpec((rows, col_count), lambda i: (i, 0)),
+        ],
+        out_shape=[
+            jax.ShapeDtypeStruct(values.shape, jnp.float32),
+            jax.ShapeDtypeStruct((row_count, col_count), jnp.float32),
+        ],
         scratch_shapes=[pltpu.VMEM((level_count - 1, rows, col_count), jnp.float32)],
-    )(values, wet_mask, diffusivity)
+    )(values, wet_mask, diffusivity, forcing)
 
 
 def nine_point(padded, wet_surface, centre_weight):
@@ -569,20 +579,22 @@
     wet_mask = jnp.where(
         level_index < depth_levels[None], ocean_cells[None], jnp.zeros_like(ocean_cells)[None]
     )
-    fold_signs = jnp.array([1.0, 1.0, 1.0, -1.0, -1.0], jnp.float32).reshape(5, 1, 1, 1)
-    provisional = assembling_call(tracers, wet_mask, east_velocity, north_velocity, fold_signs)
-    new_tracers = vertical_mix(provisional, wet_mask, vertical_diffusivity)
-    wet_surface = wet_mask[0]
-    surface_source = wet_surface * (forcing + jnp.mean(new_tracers[0] - new_tracers[1], axis=0))
-    centre_weight = 6.0 + surface_coupling
     relaid = lax.all_to_all(
-        jnp.stack([surface_source, wet_surface, centre_weight]),
+        jnp.stack([wet_mask[0], 6.0 + surface_coupling]),
         "lon",
         split_axis=1,
         concat_axis=2,
         tiled=True,
     )
-    strip_solution = solve(relaid[0], relaid[1], relaid[2])
+    fold_signs = jnp.array([1.0, 1.0, 1.0, -1.0, -1.0], jnp.float32).reshape(5, 1, 1, 1)
+    provisional = assembling_call(tracers, wet_mask, east_velocity, north_velocity, fold_signs)
+    new_tracers, surface_source = vertical_mix(
+        provisional, wet_mask, vertical_diffusivity, forcing
+    )
+    wet_surface = wet_mask[0]
+    centre_weight = 6.0 + surface_coupling
+    strip_source = lax.all_to_all(surface_source, "lon", split_axis=0, concat_axis=1, tiled=True)
+    strip_solution = solve(strip_source, relaid[0], relaid[1])
     solution = lax.all_to_all(strip_solution, "lon", split_axis=1, concat_axis=0, tiled=True)
     return (new_tracers, solution)
 

time: 260 us -> 253 us (0.973)
  local copies, waits for them, and re-layouts: 36.1 us -> 29.7 us
  starting transfers between devices: 88.8 us -> 95.1 us
  other arithmetic: 37.8 us -> 32.1 us
    all_to_all x1 -> x2, starting transfers between devices: 4.16 us -> 11 us  [the longest x1 5.57 us: shards(): lax.all_to_all(jnp.stack([wet_mask[0], 6.0 + surface_coupling]), 'lon', s...]
    ppermute x1, waiting for transfers between devices: 0.01 us -> 4.85 us  [halo_pieces(): lax.ppermute(top, 'lat', [(j, j + 1) for j in range(lat_count - 1)])]
    ppermute x1, waiting for transfers between devices: 4.32 us -> 0.01 us  [halo_pieces(): lax.ppermute(top, 'lon', [(i, lon_count - 1 - i) for i in range(lon_count)])]
    all_to_all x1 -> x2, waiting for transfers between devices: 7.72 us -> 6.47 us  [the longest x1 4.97 us: shards(): lax.all_to_all(surface_source, 'lon', split_axis=0, concat_axis=1, tiled=...]
  transfers between devices with their start and end apart: 33 -> 34, of which waited for: 21 -> 22; matrix products, arithmetic and copies ran while one was open for 13% -> 11% of each run, Pallas kernels for 0% -> 0%
where the time goes in v5:
time: 253 us; the launch traced here: 252 us
  starting transfers between devices  95.1 us (38%)
  waiting for transfers between devices  44.5 us (18%)
  other arithmetic  32.1 us (13%)
  local copies, waits for them, and re-layouts  29.7 us (12%)
  Pallas kernels  26.5 us (10%)
  blocking collectives  14.3 us (6%)
  between operations  9.33 us (4%)
    ppermute x21, starting transfers between devices, butterfly_sum(): lax.ppermute(value, axis, [(i, i ^ bit) for i in range(count)])  59.7 us
    ppermute x21, waiting for transfers between devices, butterfly_sum(): lax.ppermute(value, axis, [(i, i ^ bit) for i in range(count)])  33.2 us
    pallas_call x1, Pallas kernels, assembling_call(): pl.pallas_call(assembling_kernel, grid=(level_count,), in_specs=[pl.Block...  20.7 us
    all_to_all x1, blocking collectives, shards(): lax.all_to_all(strip_solution, 'lon', split_axis=1, concat_axis=0, tiled=...  14.3 us
    add x21, other arithmetic, butterfly_sum(): value + lax.ppermute(value, axis, [(i, i ^ bit) for i in range(count)])  10.5 us
    ppermute x3, starting transfers between devices, neighbour_rows(): lax.ppermute(values[:, -1:, :], axes, [(device(s - 1), device(s)) for s i...  7.32 us
    ppermute x3, starting transfers between devices, neighbour_rows(): lax.ppermute(values[:, 0:1, :], axes, [(device(s + 1), device(s)) for s i...  7.05 us
    rev x3, local copies, waits for them, and re-layouts, strip_assemble(): jnp.flip(surface_field[-1:, :], axis=1)  6.33 us
  transfers between devices with their start and end apart: 34, of which 22 were waited for; matrix products, arithmetic and copies ran while one was open for 11% of the time, Pallas kernels for 0%

profile of v5, /device:TPU:1, one launch (start us, length us, event | category | flops | bytes accessed | tf_op | source)
XLA Modules:
  0.0 251.6 jit_solution(3771493769744342971)
XLA Ops:
  9.0 2.2 fusion.35
  20.3 1.7 fusion.37
  22.1 3.1 %copy.51 = f32[5,20,64,2]{3,2,1,0:T(8,128)} copy(f32[5,20,64,2]{2,3,1,0:T(2,128)} %collective-permute-done) | data formatting | bytes 102400 | tf_op jit(solution)/shard_map/ppermute | solution.py:200
  25.2 2.3 copy.52
  27.6 3.8 %pad_maximum_fusion.cols_ref = f32[5,20,64,128]{3,2,1,0:T(8,128)S(1)} fusion(f32[5,20,64,2]{3,2,1,0:T(8,128)} %copy.52, f32[5,20,64,2]{3,2,1,0:T(8,128)} %copy.51, f32[128]{0:T(128)S(1)} %pad.74.clone), kind=kLoop, calls=%fused_computation | loop fusion | flops 1638400 | bytes 3379712 | tf_op jit(solution)/shard_map/concatenate | solution.py:210
  31.7 1.8 collective-permute-start.2
  36.0 5.6 %all-to-all-start.1 = ((f32[2,64,384]{2,0,1:T(2,128)}), f32[2,64,384]{2,0,1:T(2,128)S(1)}, u32[]{:S(2)}, u32[]{:S(2)}) async-start(f32[2,64,384]{2,0,1:T(2,128)} %copy.53), calls=%async_computation.1 | async-start | bytes 393216 | tf_op jit(solution)/shard_map/all_to_all | solution.py:582
  41.5 4.3 %collective-permute-start.4 = (f32[5,20,2,512]{3,2,1,0:T(2,128)S(1)}, f32[5,20,2,512]{3,2,1,0:T(2,128)S(1)}, u32[]{:S(2)}, u32[]{:S(2)}) collective-permute-start(f32[5,20,2,512]{3,2,1,0:T(2,128)S(1)} %pad_maximum_fusion.2), channel_id=1, source_target_pairs={{0,1},{1,2},{2,3},{3,4},{4,5},{5,6},{6,7},{7,8},{8,9},{9,10},{10,1... | collective-permute-start | bytes 1228808 | tf_op jit(solution)/shard_map/ppermute | solution.py:222
  49.6 4.8 %collective-permute-done.4 = f32[5,20,2,512]{3,2,1,0:T(2,128)S(1)} collective-permute-done((f32[5,20,2,512]{3,2,1,0:T(2,128)S(1)}, f32[5,20,2,512]{3,2,1,0:T(2,128)S(1)}, u32[]{:S(2)}, u32[]{:S(2)}) %collective-permute-start.4) | collective-permute-done | bytes 409632 | tf_op jit(solution)/shard_map/ppermute | solution.py:222
  56.0 20.7 %shard_map.104.values_ref = f32[2,20,64,384]{3,2,1,0:T(8,128)} custom-call(f32[2,20,64,384]{3,2,1,0:T(8,128)} %tracer_ref.1, f32[20,64,384]{2,1,0:T(8,128)} %copy-done, bf16[20,64,384]{2,1,0:T(8,128)(2,1)} %east_ref.1, bf16[20,64,384]{2,1,0:T(8,128)(2,1)} %north_ref.1, f32[5,20,64,128]{3,2,1,0:T(8,128)} %copy-done.1, ...), custom_call_target="tpu_custom_call" | custom-call | tf_op jit(solution)/shard_map/pallas_call | solution.py:239
  76.8 5.8 %shard_map.105 = (f32[2,20,64,384]{3,2,1,0:T(8,128)}, f32[64,384]{1,0:T(8,128)}) custom-call(f32[2,20,64,384]{3,2,1,0:T(8,128)} %shard_map.104.values_ref, f32[20,64,384]{2,1,0:T(8,128)} %copy-done, bf16[20,64,384]{2,1,0:T(8,128)(2,1)} %diff_ref.1, f32[64,384]{1,0:T(8,128)} %forcing_ref.1), custom_call_target="tpu_custom_call" | custom-call | tf_op jit(solution)/shard_map/pallas_call | solution.py:339
  82.6 5.4 %all-to-all-start = ((f32[8,8,384]{2,1,0:T(8,128)}), f32[8,8,384]{2,1,0:T(8,128)S(1)}, u32[]{:S(2)}, u32[]{:S(2)}) async-start(f32[8,8,384]{2,1,0:T(8,128)} %bitcast.167), calls=%async_computation | async-start | bytes 196608 | tf_op jit(solution)/shard_map/all_to_all | solution.py:596
  88.0 5.0 %all-to-all-done = f32[8,8,384]{2,1,0:T(8,128)S(1)} async-done(((f32[8,8,384]{2,1,0:T(8,128)}), f32[8,8,384]{2,1,0:T(8,128)S(1)}, u32[]{:S(2)}, u32[]{:S(2)}) %all-to-all-start) | async-done | bytes 98336 | tf_op jit(solution)/shard_map/all_to_all | solution.py:596
  93.0 2.7 %collective-permute-start.6 = (f32[3,1,3072]{2,1,0:T(1,128)S(1)}, f32[3,1,3072]{2,1,0:T(1,128)S(1)}, u32[]{:S(2)}, u32[]{:S(2)}) collective-permute-start(f32[3,1,3072]{2,1,0:T(1,128)S(1)} %get-tuple-element.38), channel_id=1, source_target_pairs={{16,0},{32,16},{48,32},{64,48},{80,64},{96,80},{112,96},{1,112},{1... | collective-permute-start | bytes 110600 | tf_op jit(solution)/shard_map/ppermute | solution.py:480
  95.7 2.8 %collective-permute-start.5 = (f32[3,1,3072]{2,1,0:T(1,128)S(1)}, f32[3,1,3072]{2,1,0:T(1,128)S(1)}, u32[]{:S(2)}, u32[]{:S(2)}) collective-permute-start(f32[3,1,3072]{2,1,0:T(1,128)S(1)} %get-tuple-element.37), channel_id=1, source_target_pairs={{0,16},{16,32},{32,48},{48,64},{64,80},{80,96},{96,112},{112,1},{1... | collective-permute-start | bytes 110600 | tf_op jit(solution)/shard_map/ppermute | solution.py:483
  99.3 2.1 rev.12
  103.9 2.6 %collective-permute-start.14 = (f32[1,1,3072]{2,1,0:T(1,128)S(1)}, f32[1,1,3072]{2,1,0:T(1,128)S(1)}, u32[]{:S(2)}, u32[]{:S(2)}) collective-permute-start(f32[1,1,3072]{2,1,0:T(1,128)S(1)} %get-tuple-element.49), channel_id=1, source_target_pairs={{0,16},{16,32},{32,48},{48,64},{64,80},{80,96},{96,112},{112,1},{1... | collective-permute-start | bytes 36872 | tf_op jit(solution)/shard_map/ppermute | solution.py:483
  106.5 1.9 collective-permute-start.15
  110.2 2.0 collective-permute-done.8
  113.5 5.3 %collective-permute-start.9 = (f32[2]{0:T(128)S(1)}, f32[2]{0:T(128)S(1)}, u32[]{:S(2)}, u32[]{:S(2)}) collective-permute-start(f32[2]{0:T(128)S(1)} %fusion.50), channel_id=1, source_target_pairs={{0,64},{16,80},{32,96},{48,112},{64,0},{80,16},{96,32},{112,48},{1... | collective-permute-start | bytes 32 | tf_op jit(solution)/shard_map/ppermute | solution.py:466
  119.8 1.6 collective-permute-start.10
  122.4 9.6 %collective-permute-start.11 = (f32[2]{0:T(128)S(1)}, f32[2]{0:T(128)S(1)}, u32[]{:S(2)}, u32[]{:S(2)}) collective-permute-start(f32[2]{0:T(128)S(1)} %add.185), channel_id=1, source_target_pairs={{0,2},{1,3},{2,0},{3,1},{4,6},{5,7},{6,4},{7,5},{8,10},{9,11},{10,... | collective-permute-start | bytes 32 | tf_op jit(solution)/shard_map/ppermute | solution.py:466
  133.0 2.6 %collective-permute-start.12 = (f32[2]{0:T(128)S(1)}, f32[2]{0:T(128)S(1)}, u32[]{:S(2)}, u32[]{:S(2)}) collective-permute-start(f32[2]{0:T(128)S(1)} %add.186), channel_id=1, source_target_pairs={{0,4},{1,5},{2,6},{3,7},{4,0},{5,1},{6,2},{7,3},{8,12},{9,13},{10,... | collective-permute-start | bytes 32 | tf_op jit(solution)/shard_map/ppermute | solution.py:466
  136.5 3.1 %collective-permute-start.13 = (f32[2]{0:T(128)S(1)}, f32[2]{0:T(128)S(1)}, u32[]{:S(2)}, u32[]{:S(2)}) collective-permute-start(f32[2]{0:T(128)S(1)} %add.187), channel_id=1, source_target_pairs={{0,8},{1,9},{2,10},{3,11},{4,12},{5,13},{6,14},{7,15},{8,0},{9,1},... | collective-permute-start | bytes 32 | tf_op jit(solution)/shard_map/ppermute | solution.py:466
  142.5 2.1 rev.13
  145.7 1.9 pad_maximum_fusion.29
  147.6 11.8 %collective-permute-start.16 = (f32[3]{0:T(128)S(1)}, f32[3]{0:T(128)S(1)}, u32[]{:S(2)}, u32[]{:S(2)}) collective-permute-start(f32[3]{0:T(128)S(1)} %pad_maximum_fusion.29), channel_id=1, source_target_pairs={{0,16},{16,0},{32,48},{48,32},{64,80},{80,64},{96,112},{112,96},{1... | collective-permute-start | bytes 44 | tf_op jit(solution)/shard_map/ppermute | solution.py:466
  159.4 1.9 collective-permute-start.23
  161.4 2.4 collective-permute-start.24
  163.8 1.9 fusion.46
  165.7 2.4 collective-permute-done.17
  168.1 1.9 fusion.49
  171.3 2.7 %collective-permute-done.18 = f32[3]{0:T(128)S(1)} collective-permute-done((f32[3]{0:T(128)S(1)}, f32[3]{0:T(128)S(1)}, u32[]{:S(2)}, u32[]{:S(2)}) %collective-permute-start.18) | collective-permute-done | bytes 44 | tf_op jit(solution)/shard_map/ppermute | solution.py:466
  173.9 2.4 collective-permute-done.19
  176.4 2.3 collective-permute-start.20
  180.3 1.8 collective-permute-start.21
  183.1 3.1 %collective-permute-start.22 = (f32[3]{0:T(128)S(1)}, f32[3]{0:T(128)S(1)}, u32[]{:S(2)}, u32[]{:S(2)}) collective-permute-start(f32[3]{0:T(128)S(1)} %add.200), channel_id=1, source_target_pairs={{0,8},{1,9},{2,10},{3,11},{4,12},{5,13},{6,14},{7,15},{8,0},{9,1},... | collective-permute-start | bytes 44 | tf_op jit(solution)/shard_map/ppermute | solution.py:466
  191.5 2.1 rev.14
  194.7 2.0 pad_maximum_fusion.30
  196.7 11.9 %collective-permute-start.25 = (f32[3]{0:T(128)S(1)}, f32[3]{0:T(128)S(1)}, u32[]{:S(2)}, u32[]{:S(2)}) collective-permute-start(f32[3]{0:T(128)S(1)} %pad_maximum_fusion.30), channel_id=1, source_target_pairs={{0,16},{16,0},{32,48},{48,32},{64,80},{80,64},{96,112},{112,96},{1... | collective-permute-start | bytes 44 | tf_op jit(solution)/shard_map/ppermute | solution.py:466
  209.5 2.0 fusion.45
  211.5 2.4 collective-permute-done.26
  213.9 2.0 fusion.48
  215.9 3.9 %collective-permute-done.27 = f32[3]{0:T(128)S(1)} collective-permute-done((f32[3]{0:T(128)S(1)}, f32[3]{0:T(128)S(1)}, u32[]{:S(2)}, u32[]{:S(2)}) %collective-permute-start.27) | collective-permute-done | bytes 44 | tf_op jit(solution)/shard_map/ppermute | solution.py:466
  219.8 2.4 collective-permute-done.28
  222.3 3.9 %collective-permute-done.29 = f32[3]{0:T(128)S(1)} collective-permute-done((f32[3]{0:T(128)S(1)}, f32[3]{0:T(128)S(1)}, u32[]{:S(2)}, u32[]{:S(2)}) %collective-permute-start.29) | collective-permute-done | bytes 44 | tf_op jit(solution)/shard_map/ppermute | solution.py:466
  228.8 3.1 %collective-permute-start.31 = (f32[3]{0:T(128)S(1)}, f32[3]{0:T(128)S(1)}, u32[]{:S(2)}, u32[]{:S(2)}) collective-permute-start(f32[3]{0:T(128)S(1)} %add.220), channel_id=1, source_target_pairs={{0,8},{1,9},{2,10},{3,11},{4,12},{5,13},{6,14},{7,15},{8,0},{9,1},... | collective-permute-start | bytes 44 | tf_op jit(solution)/shard_map/ppermute | solution.py:466
  236.7 14.3 %all_to_all.53 = f32[8,8,384]{2,0,1:T(8,128)S(1)} all-to-all(f32[8,8,384]{2,0,1:T(8,128)S(1)} %bitcast.165), channel_id=1, replica_groups=mesh['lon'=8,'lat'=16] {'lon'}, dimensions={1} | all-to-all | bytes 196608 | tf_op jit(solution)/shard_map/all_to_all | solution.py:598
  (141 shorter events, 50.7 us)
Async XLA Ops:
  2.7 1.3 copy-start.2
  4.0 1.2 copy-start.3
  4.2 2.9 %copy-start.4 = (bf16[20,64,384]{2,1,0:T(8,128)(2,1)S(1)}, bf16[20,64,384]{2,1,0:T(8,128)(2,1)}, u32[]{:S(2)}) copy-start(bf16[20,64,384]{2,1,0:T(8,128)(2,1)} %north_ref.1) | copy-start | bytes 2949124
  11.7 3.9 %copy-start.5 = (f32[1,20,64,2]{3,2,1,0:T(8,128)S(1)}, f32[1,20,64,2]{3,2,1,0:T(8,128)}, u32[]{:S(2)}) copy-start(f32[1,20,64,2]{3,2,1,0:T(8,128)} %get-tuple-element.36) | copy-start | bytes 30724
  12.6 9.5 %collective-permute-start = (f32[5,20,64,2]{2,3,1,0:T(2,128)S(1)}, f32[5,20,64,2]{2,3,1,0:T(2,128)}, u32[]{:S(2)}, u32[]{:S(2)}) collective-permute-start(f32[5,20,64,2]{2,3,1,0:T(2,128)S(1)} %pad_maximum_fusion.17), channel_id=1, source_target_pairs={{0,112},{16,0},{32,16},{48,32},{64,48},{80,64},{96,80},{112,96},{1... | collective-permute-start | bytes 153608 | tf_op jit(solution)/shard_map/ppermute | solution.py:200
  14.2 5.9 %copy-start.6 = (s32[64,384]{1,0:T(8,128)S(1)}, s32[64,384]{1,0:T(8,128)}, u32[]{:S(2)}) copy-start(s32[64,384]{1,0:T(8,128)} %param.13) | copy-start | bytes 294916
  16.4 8.8 %collective-permute-start.1 = (f32[5,20,64,2]{2,3,1,0:T(2,128)S(1)}, f32[5,20,64,2]{2,3,1,0:T(2,128)S(1)}, u32[]{:S(2)}, u32[]{:S(2)}) collective-permute-start(f32[5,20,64,2]{2,3,1,0:T(2,128)S(1)} %pad_maximum_fusion.18), channel_id=1, source_target_pairs={{0,16},{16,32},{32,48},{48,64},{64,80},{80,96},{96,112},{112,0},{1... | collective-permute-start | bytes 153608 | tf_op jit(solution)/shard_map/ppermute | solution.py:205
  20.3 7.3 %copy-start = (f32[20,64,384]{2,1,0:T(8,128)}, f32[20,64,384]{2,1,0:T(8,128)S(1)}, u32[]{:S(2)}) copy-start(f32[20,64,384]{2,1,0:T(8,128)S(1)} %fusion.wet_ref) | copy-start | bytes 5898244
  31.4 3.7 %copy-start.1 = (f32[5,20,64,128]{3,2,1,0:T(8,128)}, f32[5,20,64,128]{3,2,1,0:T(8,128)S(1)}, u32[]{:S(2)}) copy-start(f32[5,20,64,128]{3,2,1,0:T(8,128)S(1)} %pad_maximum_fusion.cols_ref) | copy-start | bytes 9830404
  31.4 3.6 %copy-start.7 = (f32[64,384]{1,0:T(8,128)S(1)}, f32[64,384]{1,0:T(8,128)}, u32[]{:S(2)}) copy-start(f32[64,384]{1,0:T(8,128)} %param.16) | copy-start | bytes 294916
  31.4 3.6 %slice-start = ((f32[20,64,384]{2,1,0:T(8,128)}), f32[1,64,384]{2,1,0:T(8,128)S(1)}, s32[]{:S(2)}) async-start(f32[20,64,384]{2,1,0:T(8,128)} %copy-done), calls=%async_computation.3 | async-start | bytes 196608 | tf_op jit(solution)/shard_map/slice | solution.py:583
  31.7 15.7 %collective-permute-start.2 = (f32[5,20,2,512]{3,2,1,0:T(2,128)S(1)}, f32[5,20,2,512]{3,2,1,0:T(2,128)S(1)}, u32[]{:S(2)}, u32[]{:S(2)}) collective-permute-start(f32[5,20,2,512]{3,2,1,0:T(2,128)S(1)} %pad_maximum_fusion.2), channel_id=1, source_target_pairs={{0,112},{16,96},{32,80},{48,64},{64,48},{80,32},{96,16},{112,0},{1... | collective-permute-start | bytes 1228808 | tf_op jit(solution)/shard_map/ppermute | solution.py:223
  33.6 15.7 %copy-start.8 = (f32[5]{0:T(128)S(1)}, f32[5]{0:T(128)}, u32[]{:S(2)}) copy-start(f32[5]{0:T(128)} %constant.10.clone) | copy-start | bytes 64
  33.8 15.5 %collective-permute-start.3 = (f32[5,20,2,512]{3,2,1,0:T(2,128)S(1)}, f32[5,20,2,512]{3,2,1,0:T(2,128)S(1)}, u32[]{:S(2)}, u32[]{:S(2)}) collective-permute-start(f32[5,20,2,512]{3,2,1,0:T(2,128)S(1)} %pad_maximum_fusion.3), channel_id=1, source_target_pairs={{1,0},{2,1},{3,2},{4,3},{5,4},{6,5},{7,6},{8,7},{9,8},{10,9},{11,1... | collective-permute-start | bytes 1228808 | tf_op jit(solution)/shard_map/ppermute | solution.py:221
  36.0 11.5 %all-to-all-start.1 = ((f32[2,64,384]{2,0,1:T(2,128)}), f32[2,64,384]{2,0,1:T(2,128)S(1)}, u32[]{:S(2)}, u32[]{:S(2)}) async-start(f32[2,64,384]{2,0,1:T(2,128)} %copy.53), calls=%async_computation.1 | async-start | bytes 393216 | tf_op jit(solution)/shard_map/all_to_all | solution.py:582
  41.5 12.9 %collective-permute-start.4 = (f32[5,20,2,512]{3,2,1,0:T(2,128)S(1)}, f32[5,20,2,512]{3,2,1,0:T(2,128)S(1)}, u32[]{:S(2)}, u32[]{:S(2)}) collective-permute-start(f32[5,20,2,512]{3,2,1,0:T(2,128)S(1)} %pad_maximum_fusion.2), channel_id=1, source_target_pairs={{0,1},{1,2},{2,3},{3,4},{4,5},{5,6},{6,7},{7,8},{8,9},{9,10},{10,1... | collective-permute-start | bytes 1228808 | tf_op jit(solution)/shard_map/ppermute | solution.py:222
  82.6 10.4 %all-to-all-start = ((f32[8,8,384]{2,1,0:T(8,128)}), f32[8,8,384]{2,1,0:T(8,128)S(1)}, u32[]{:S(2)}, u32[]{:S(2)}) async-start(f32[8,8,384]{2,1,0:T(8,128)} %bitcast.167), calls=%async_computation | async-start | bytes 196608 | tf_op jit(solution)/shard_map/all_to_all | solution.py:596
  93.0 8.5 %collective-permute-start.6 = (f32[3,1,3072]{2,1,0:T(1,128)S(1)}, f32[3,1,3072]{2,1,0:T(1,128)S(1)}, u32[]{:S(2)}, u32[]{:S(2)}) collective-permute-start(f32[3,1,3072]{2,1,0:T(1,128)S(1)} %get-tuple-element.38), channel_id=1, source_target_pairs={{16,0},{32,16},{48,32},{64,48},{80,64},{96,80},{112,96},{1,112},{1... | collective-permute-start | bytes 110600 | tf_op jit(solution)/shard_map/ppermute | solution.py:480
  95.7 5.7 %collective-permute-start.5 = (f32[3,1,3072]{2,1,0:T(1,128)S(1)}, f32[3,1,3072]{2,1,0:T(1,128)S(1)}, u32[]{:S(2)}, u32[]{:S(2)}) collective-permute-start(f32[3,1,3072]{2,1,0:T(1,128)S(1)} %get-tuple-element.37), channel_id=1, source_target_pairs={{0,16},{16,32},{32,48},{48,64},{64,80},{80,96},{96,112},{112,1},{1... | collective-permute-start | bytes 110600 | tf_op jit(solution)/shard_map/ppermute | solution.py:483
  103.8 4.6 %collective-permute-start.7 = (f32[2]{0:T(128)S(1)}, f32[2]{0:T(128)S(1)}, u32[]{:S(2)}, u32[]{:S(2)}) collective-permute-start(f32[2]{0:T(128)S(1)} %pad_maximum_fusion.28), channel_id=1, source_target_pairs={{0,16},{16,0},{32,48},{48,32},{64,80},{80,64},{96,112},{112,96},{1... | collective-permute-start | bytes 32 | tf_op jit(solution)/shard_map/ppermute | solution.py:466
  103.9 40.7 %collective-permute-start.14 = (f32[1,1,3072]{2,1,0:T(1,128)S(1)}, f32[1,1,3072]{2,1,0:T(1,128)S(1)}, u32[]{:S(2)}, u32[]{:S(2)}) collective-permute-start(f32[1,1,3072]{2,1,0:T(1,128)S(1)} %get-tuple-element.49), channel_id=1, source_target_pairs={{0,16},{16,32},{32,48},{48,64},{64,80},{80,96},{96,112},{112,1},{1... | collective-permute-start | bytes 36872 | tf_op jit(solution)/shard_map/ppermute | solution.py:483
  106.5 38.2 %collective-permute-start.15 = (f32[1,1,3072]{2,1,0:T(1,128)S(1)}, f32[1,1,3072]{2,1,0:T(1,128)S(1)}, u32[]{:S(2)}, u32[]{:S(2)}) collective-permute-start(f32[1,1,3072]{2,1,0:T(1,128)S(1)} %get-tuple-element.50), channel_id=1, source_target_pairs={{16,0},{32,16},{48,32},{64,48},{80,64},{96,80},{112,96},{1,112},{1... | collective-permute-start | bytes 36872 | tf_op jit(solution)/shard_map/ppermute | solution.py:480
  109.7 2.4 collective-permute-start.8
  113.5 6.2 %collective-permute-start.9 = (f32[2]{0:T(128)S(1)}, f32[2]{0:T(128)S(1)}, u32[]{:S(2)}, u32[]{:S(2)}) collective-permute-start(f32[2]{0:T(128)S(1)} %fusion.50), channel_id=1, source_target_pairs={{0,64},{16,80},{32,96},{48,112},{64,0},{80,16},{96,32},{112,48},{1... | collective-permute-start | bytes 32 | tf_op jit(solution)/shard_map/ppermute | solution.py:466
  119.8 2.6 %collective-permute-start.10 = (f32[2]{0:T(128)S(1)}, f32[2]{0:T(128)S(1)}, u32[]{:S(2)}, u32[]{:S(2)}) collective-permute-start(f32[2]{0:T(128)S(1)} %add.184), channel_id=1, source_target_pairs={{0,1},{1,0},{2,3},{3,2},{4,5},{5,4},{6,7},{7,6},{8,9},{9,8},{10,11... | collective-permute-start | bytes 32 | tf_op jit(solution)/shard_map/ppermute | solution.py:466
  122.4 10.6 %collective-permute-start.11 = (f32[2]{0:T(128)S(1)}, f32[2]{0:T(128)S(1)}, u32[]{:S(2)}, u32[]{:S(2)}) collective-permute-start(f32[2]{0:T(128)S(1)} %add.185), channel_id=1, source_target_pairs={{0,2},{1,3},{2,0},{3,1},{4,6},{5,7},{6,4},{7,5},{8,10},{9,11},{10,... | collective-permute-start | bytes 32 | tf_op jit(solution)/shard_map/ppermute | solution.py:466
  133.0 3.5 %collective-permute-start.12 = (f32[2]{0:T(128)S(1)}, f32[2]{0:T(128)S(1)}, u32[]{:S(2)}, u32[]{:S(2)}) collective-permute-start(f32[2]{0:T(128)S(1)} %add.186), channel_id=1, source_target_pairs={{0,4},{1,5},{2,6},{3,7},{4,0},{5,1},{6,2},{7,3},{8,12},{9,13},{10,... | collective-permute-start | bytes 32 | tf_op jit(solution)/shard_map/ppermute | solution.py:466
  136.5 4.0 %collective-permute-start.13 = (f32[2]{0:T(128)S(1)}, f32[2]{0:T(128)S(1)}, u32[]{:S(2)}, u32[]{:S(2)}) collective-permute-start(f32[2]{0:T(128)S(1)} %add.187), channel_id=1, source_target_pairs={{0,8},{1,9},{2,10},{3,11},{4,12},{5,13},{6,14},{7,15},{8,0},{9,1},... | collective-permute-start | bytes 32 | tf_op jit(solution)/shard_map/ppermute | solution.py:466
  147.6 16.2 %collective-permute-start.16 = (f32[3]{0:T(128)S(1)}, f32[3]{0:T(128)S(1)}, u32[]{:S(2)}, u32[]{:S(2)}) collective-permute-start(f32[3]{0:T(128)S(1)} %pad_maximum_fusion.29), channel_id=1, source_target_pairs={{0,16},{16,0},{32,48},{48,32},{64,80},{80,64},{96,112},{112,96},{1... | collective-permute-start | bytes 44 | tf_op jit(solution)/shard_map/ppermute | solution.py:466
  159.4 34.2 %collective-permute-start.23 = (f32[1,1,3072]{2,1,0:T(1,128)S(1)}, f32[1,1,3072]{2,1,0:T(1,128)S(1)}, u32[]{:S(2)}, u32[]{:S(2)}) collective-permute-start(f32[1,1,3072]{2,1,0:T(1,128)S(1)} %get-tuple-element.47), channel_id=1, source_target_pairs={{0,16},{16,32},{32,48},{48,64},{64,80},{80,96},{96,112},{112,1},{1... | collective-permute-start | bytes 36872 | tf_op jit(solution)/shard_map/ppermute | solution.py:483
  161.4 32.3 %collective-permute-start.24 = (f32[1,1,3072]{2,1,0:T(1,128)S(1)}, f32[1,1,3072]{2,1,0:T(1,128)S(1)}, u32[]{:S(2)}, u32[]{:S(2)}) collective-permute-start(f32[1,1,3072]{2,1,0:T(1,128)S(1)} %get-tuple-element.48), channel_id=1, source_target_pairs={{16,0},{32,16},{48,32},{64,48},{80,64},{96,80},{112,96},{1,112},{1... | collective-permute-start | bytes 36872 | tf_op jit(solution)/shard_map/ppermute | solution.py:480
  165.7 2.4 collective-permute-start.17
  170.0 3.9 %collective-permute-start.18 = (f32[3]{0:T(128)S(1)}, f32[3]{0:T(128)S(1)}, u32[]{:S(2)}, u32[]{:S(2)}) collective-permute-start(f32[3]{0:T(128)S(1)} %fusion.49), channel_id=1, source_target_pairs={{0,64},{16,80},{32,96},{48,112},{64,0},{80,16},{96,32},{112,48},{1... | collective-permute-start | bytes 44 | tf_op jit(solution)/shard_map/ppermute | solution.py:466
  173.9 2.4 collective-permute-start.19
  176.4 3.9 %collective-permute-start.20 = (f32[3]{0:T(128)S(1)}, f32[3]{0:T(128)S(1)}, u32[]{:S(2)}, u32[]{:S(2)}) collective-permute-start(f32[3]{0:T(128)S(1)} %add.198), channel_id=1, source_target_pairs={{0,2},{1,3},{2,0},{3,1},{4,6},{5,7},{6,4},{7,5},{8,10},{9,11},{10,... | collective-permute-start | bytes 44 | tf_op jit(solution)/shard_map/ppermute | solution.py:466
  180.3 2.8 %collective-permute-start.21 = (f32[3]{0:T(128)S(1)}, f32[3]{0:T(128)S(1)}, u32[]{:S(2)}, u32[]{:S(2)}) collective-permute-start(f32[3]{0:T(128)S(1)} %add.199), channel_id=1, source_target_pairs={{0,4},{1,5},{2,6},{3,7},{4,0},{5,1},{6,2},{7,3},{8,12},{9,13},{10,... | collective-permute-start | bytes 44 | tf_op jit(solution)/shard_map/ppermute | solution.py:466
  183.1 4.0 %collective-permute-start.22 = (f32[3]{0:T(128)S(1)}, f32[3]{0:T(128)S(1)}, u32[]{:S(2)}, u32[]{:S(2)}) collective-permute-start(f32[3]{0:T(128)S(1)} %add.200), channel_id=1, source_target_pairs={{0,8},{1,9},{2,10},{3,11},{4,12},{5,13},{6,14},{7,15},{8,0},{9,1},... | collective-permute-start | bytes 44 | tf_op jit(solution)/shard_map/ppermute | solution.py:466
  196.7 12.7 %collective-permute-start.25 = (f32[3]{0:T(128)S(1)}, f32[3]{0:T(128)S(1)}, u32[]{:S(2)}, u32[]{:S(2)}) collective-permute-start(f32[3]{0:T(128)S(1)} %pad_maximum_fusion.30), channel_id=1, source_target_pairs={{0,16},{16,0},{32,48},{48,32},{64,80},{80,64},{96,112},{112,96},{1... | collective-permute-start | bytes 44 | tf_op jit(solution)/shard_map/ppermute | solution.py:466
  211.5 2.4 collective-permute-start.26
  215.9 3.9 %collective-permute-start.27 = (f32[3]{0:T(128)S(1)}, f32[3]{0:T(128)S(1)}, u32[]{:S(2)}, u32[]{:S(2)}) collective-permute-start(f32[3]{0:T(128)S(1)} %fusion.48), channel_id=1, source_target_pairs={{0,64},{16,80},{32,96},{48,112},{64,0},{80,16},{96,32},{112,48},{1... | collective-permute-start | bytes 44 | tf_op jit(solution)/shard_map/ppermute | solution.py:466
  219.8 2.4 collective-permute-start.28
  222.3 3.9 %collective-permute-start.29 = (f32[3]{0:T(128)S(1)}, f32[3]{0:T(128)S(1)}, u32[]{:S(2)}, u32[]{:S(2)}) collective-permute-start(f32[3]{0:T(128)S(1)} %add.218), channel_id=1, source_target_pairs={{0,2},{1,3},{2,0},{3,1},{4,6},{5,7},{6,4},{7,5},{8,10},{9,11},{10,... | collective-permute-start | bytes 44 | tf_op jit(solution)/shard_map/ppermute | solution.py:466
  226.2 2.6 %collective-permute-start.30 = (f32[3]{0:T(128)S(1)}, f32[3]{0:T(128)S(1)}, u32[]{:S(2)}, u32[]{:S(2)}) collective-permute-start(f32[3]{0:T(128)S(1)} %add.219), channel_id=1, source_target_pairs={{0,4},{1,5},{2,6},{3,7},{4,0},{5,1},{6,2},{7,3},{8,12},{9,13},{10,... | collective-permute-start | bytes 44 | tf_op jit(solution)/shard_map/ppermute | solution.py:466
  228.8 4.0 %collective-permute-start.31 = (f32[3]{0:T(128)S(1)}, f32[3]{0:T(128)S(1)}, u32[]{:S(2)}, u32[]{:S(2)}) collective-permute-start(f32[3]{0:T(128)S(1)} %add.220), channel_id=1, source_target_pairs={{0,8},{1,9},{2,10},{3,11},{4,12},{5,13},{6,14},{7,15},{8,0},{9,1},... | collective-permute-start | bytes 44 | tf_op jit(solution)/shard_map/ppermute | solution.py:466

commit v6 on v5

--- a/solution.py
+++ b/solution.py
@@ -486,12 +486,16 @@
     return above, below
 
 
-def strip_assemble(surface_field, above_row, below_row):
+def last_flipped(surface_field):
+    return jnp.flip(surface_field[-1:, :], axis=1)
+
+
+def strip_assemble(surface_field, above_row, below_row, folded_row):
     top_strip = jnp.logical_and(
         lax.axis_index("lon") == lax.axis_size("lon") - 1,
         lax.axis_index("lat") == lax.axis_size("lat") - 1,
     )
-    above_row = jnp.where(top_strip, jnp.flip(surface_field[-1:, :], axis=1), above_row)
+    above_row = jnp.where(top_strip, folded_row, above_row)
     extended = jnp.concatenate([below_row, surface_field, above_row], axis=0)
     return jnp.concatenate([extended[:, -1:], extended, extended[:, :1]], axis=1)
 
@@ -501,8 +505,12 @@
     def precondition(residual, wet, weight):
         return wet * residual / weight
 
-    def apply_operator(field, above, below):
-        return nine_point(strip_assemble(field, above, below), wet_surface, centre_weight)
+    def apply_operator(field, above, below, folded):
+        return nine_point(strip_assemble(field, above, below, folded), wet_surface, centre_weight)
+
+    fold_wet = last_flipped(wet_surface)
+    fold_weight = last_flipped(centre_weight)
+    fold_resid = last_flipped(surface_source)
 
     rim_above, rim_below = neighbour_rows(jnp.stack([wet_surface, centre_weight, surface_source]))
     solution = jnp.zeros_like(surface_source)
@@ -516,7 +524,9 @@
     operator_image = apply_operator(
         direction,
         *[precondition(r, w, c) for r, (w, c) in zip(resid_rims, weight_rims)],
-    )
+        precondition(fold_resid, fold_wet, fold_weight),
+    )
+    fold_image = last_flipped(operator_image)
     image_above, image_below = neighbour_rows(operator_image[None])
     image_rims = [image_above[0], image_below[0]]
     totals = butterfly_sum(
@@ -529,14 +539,17 @@
         if iteration + 1 < ITERS:
             residual = residual - step_size * operator_image
             resid_rims = [r - step_size * a for r, a in zip(resid_rims, image_rims)]
+            fold_resid = fold_resid - step_size * fold_image
             precond = precondition(residual, wet_surface, centre_weight)
             precond_image = apply_operator(
                 precond,
                 *[precondition(r, w, c) for r, (w, c) in zip(resid_rims, weight_rims)],
+                precondition(fold_resid, fold_wet, fold_weight),
             )
             if iteration + 2 < ITERS:
                 fresh_above, fresh_below = neighbour_rows(precond_image[None])
                 fresh_rims = [fresh_above[0], fresh_below[0]]
+                fresh_fold = last_flipped(precond_image)
             totals = butterfly_sum(
                 jnp.stack(
                     [
@@ -553,6 +566,7 @@
             operator_image = precond_image + ratio * operator_image
             if iteration + 2 < ITERS:
                 image_rims = [f + ratio * a for f, a in zip(fresh_rims, image_rims)]
+                fold_image = fresh_fold + ratio * fold_image
             resid_dot = dot_next
     return solution
 

time: 253 us -> 259 us (1.024)
  local copies, waits for them, and re-layouts: 29.7 us -> 37.6 us
  waiting for transfers between devices: 44.5 us -> 39.6 us
    all_to_all x1, waiting for transfers between devices: 4.97 us -> 0.75 us  [shards(): lax.all_to_all(surface_source, 'lon', split_axis=0, concat_axis=1, tiled=...]
    rev x3 -> x5, local copies, waits for them, and re-layouts: 6.33 us -> 10.5 us  [last_flipped(): return jnp.flip(surface_field[-1:, :], axis=1)]
  transfers between devices with their start and end apart: 34 -> 34, of which waited for: 22 -> 22; matrix products, arithmetic and copies ran while one was open for 11% -> 13% of each run, Pallas kernels for 0% -> 0%
where the time goes in v6:
time: 259 us; the launch traced here: 258 us
  starting transfers between devices  96.2 us (37%)
  waiting for transfers between devices  39.6 us (15%)
  local copies, waits for them, and re-layouts  37.6 us (15%)
  other arithmetic  34 us (13%)
  Pallas kernels  26.5 us (10%)
  blocking collectives  14.3 us (6%)
  between operations  9.36 us (4%)
    ppermute x21, starting transfers between devices, butterfly_sum(): lax.ppermute(value, axis, [(i, i ^ bit) for i in range(count)])  60.5 us
    ppermute x21, waiting for transfers between devices, butterfly_sum(): lax.ppermute(value, axis, [(i, i ^ bit) for i in range(count)])  32.4 us
    pallas_call x1, Pallas kernels, assembling_call(): pl.pallas_call(assembling_kernel, grid=(level_count,), in_specs=[pl.Block...  20.7 us
    all_to_all x1, blocking collectives, shards(): lax.all_to_all(strip_solution, 'lon', split_axis=1, concat_axis=0, tiled=...  14.3 us
    rev x5, local copies, waits for them, and re-layouts, last_flipped(): return jnp.flip(surface_field[-1:, :], axis=1)  10.5 us
    add x21, other arithmetic, butterfly_sum(): value + lax.ppermute(value, axis, [(i, i ^ bit) for i in range(count)])  10.5 us
    ppermute x3, starting transfers between devices, neighbour_rows(): lax.ppermute(values[:, -1:, :], axes, [(device(s - 1), device(s)) for s i...  7.64 us
    ppermute x3, starting transfers between devices, neighbour_rows(): lax.ppermute(values[:, 0:1, :], axes, [(device(s + 1), device(s)) for s i...  7.05 us
  transfers between devices with their start and end apart: 34, of which 22 were waited for; matrix products, arithmetic and copies ran while one was open for 13% of the time, Pallas kernels for 0%

profile of v6, /device:TPU:1, one launch (start us, length us, event | category | flops | bytes accessed | tf_op | source)
XLA Modules:
  0.0 257.5 jit_solution(11330776558184771636)
XLA Ops:
  7.9 2.1 slice_convert_fusion.2
  10.3 3.3 %fusion.35 = (f32[2,20,64,2]{3,2,1,0:T(8,128)}, f32[2,20,64,2]{3,2,1,0:T(8,128)S(1)}) fusion(f32[2,20,64,384]{3,2,1,0:T(8,128)} %tracer_ref.1), kind=kLoop, calls=%fused_computation.125 | loop fusion | bytes 81920 | tf_op jit(solution)/shard_map/slice | solution.py:191
  20.2 2.0 copy.36
  27.5 3.2 %copy.37 = f32[5,20,64,2]{3,2,1,0:T(8,128)} copy(f32[5,20,64,2]{2,3,1,0:T(2,128)} %collective-permute-done) | data formatting | bytes 102400 | tf_op jit(solution)/shard_map/ppermute | solution.py:200
  30.7 2.3 copy.38
  33.0 3.8 %pad_maximum_fusion.cols_ref = f32[5,20,64,128]{3,2,1,0:T(8,128)S(1)} fusion(f32[5,20,64,2]{3,2,1,0:T(8,128)} %copy.38, f32[5,20,64,2]{3,2,1,0:T(8,128)} %copy.37, f32[128]{0:T(128)S(1)} %pad.74.clone), kind=kLoop, calls=%fused_computation | loop fusion | flops 1638400 | bytes 3379712 | tf_op jit(solution)/shard_map/concatenate | solution.py:210
  37.2 1.9 collective-permute-start.2
  41.4 5.6 %all-to-all-start.1 = ((f32[2,64,384]{2,0,1:T(2,128)}), f32[2,64,384]{2,0,1:T(2,128)S(1)}, u32[]{:S(2)}, u32[]{:S(2)}) async-start(f32[2,64,384]{2,0,1:T(2,128)} %copy.39), calls=%async_computation.1 | async-start | bytes 393216 | tf_op jit(solution)/shard_map/all_to_all | solution.py:596
  47.0 4.3 %collective-permute-start.4 = (f32[5,20,2,512]{3,2,1,0:T(2,128)S(1)}, f32[5,20,2,512]{3,2,1,0:T(2,128)S(1)}, u32[]{:S(2)}, u32[]{:S(2)}) collective-permute-start(f32[5,20,2,512]{3,2,1,0:T(2,128)S(1)} %pad_maximum_fusion.2), channel_id=1, source_target_pairs={{0,1},{1,2},{2,3},{3,4},{4,5},{5,6},{6,7},{7,8},{8,9},{9,10},{10,1... | collective-permute-start | bytes 1228808 | tf_op jit(solution)/shard_map/ppermute | solution.py:222
  55.1 4.9 %collective-permute-done.4 = f32[5,20,2,512]{3,2,1,0:T(2,128)S(1)} collective-permute-done((f32[5,20,2,512]{3,2,1,0:T(2,128)S(1)}, f32[5,20,2,512]{3,2,1,0:T(2,128)S(1)}, u32[]{:S(2)}, u32[]{:S(2)}) %collective-permute-start.4) | collective-permute-done | bytes 409632 | tf_op jit(solution)/shard_map/ppermute | solution.py:222
  61.6 20.7 %shard_map.104.values_ref = f32[2,20,64,384]{3,2,1,0:T(8,128)} custom-call(f32[2,20,64,384]{3,2,1,0:T(8,128)} %tracer_ref.1, f32[20,64,384]{2,1,0:T(8,128)} %copy-done, bf16[20,64,384]{2,1,0:T(8,128)(2,1)} %east_ref.1, bf16[20,64,384]{2,1,0:T(8,128)(2,1)} %north_ref.1, f32[5,20,64,128]{3,2,1,0:T(8,128)} %copy-done.1, ...), custom_call_target="tpu_custom_call" | custom-call | tf_op jit(solution)/shard_map/pallas_call | solution.py:239
  82.3 5.8 %shard_map.105 = (f32[2,20,64,384]{3,2,1,0:T(8,128)}, f32[64,384]{1,0:T(8,128)}) custom-call(f32[2,20,64,384]{3,2,1,0:T(8,128)} %shard_map.104.values_ref, f32[20,64,384]{2,1,0:T(8,128)} %copy-done, bf16[20,64,384]{2,1,0:T(8,128)(2,1)} %diff_ref.1, f32[64,384]{1,0:T(8,128)} %forcing_ref.1), custom_call_target="tpu_custom_call" | custom-call | tf_op jit(solution)/shard_map/pallas_call | solution.py:339
  88.1 5.4 %all-to-all-start = ((f32[8,8,384]{2,1,0:T(8,128)}), f32[8,8,384]{2,1,0:T(8,128)S(1)}, u32[]{:S(2)}, u32[]{:S(2)}) async-start(f32[8,8,384]{2,1,0:T(8,128)} %bitcast.170), calls=%async_computation | async-start | bytes 196608 | tf_op jit(solution)/shard_map/all_to_all | solution.py:610
  93.5 2.1 rev.18
  95.6 2.1 rev.20
  98.5 2.7 %collective-permute-start.6 = (f32[3,1,3072]{2,1,0:T(1,128)S(1)}, f32[3,1,3072]{2,1,0:T(1,128)S(1)}, u32[]{:S(2)}, u32[]{:S(2)}) collective-permute-start(f32[3,1,3072]{2,1,0:T(1,128)S(1)} %get-tuple-element.38), channel_id=1, source_target_pairs={{16,0},{32,16},{48,32},{64,48},{80,64},{96,80},{112,96},{1,112},{1... | collective-permute-start | bytes 110600 | tf_op jit(solution)/shard_map/ppermute | solution.py:480
  101.2 2.8 %collective-permute-start.5 = (f32[3,1,3072]{2,1,0:T(1,128)S(1)}, f32[3,1,3072]{2,1,0:T(1,128)S(1)}, u32[]{:S(2)}, u32[]{:S(2)}) collective-permute-start(f32[3,1,3072]{2,1,0:T(1,128)S(1)} %get-tuple-element.37), channel_id=1, source_target_pairs={{0,16},{16,32},{32,48},{48,64},{64,80},{80,96},{96,112},{112,1},{1... | collective-permute-start | bytes 110600 | tf_op jit(solution)/shard_map/ppermute | solution.py:483
  104.8 2.1 rev.19
  109.5 2.9 %collective-permute-start.14 = (f32[1,1,3072]{2,1,0:T(1,128)S(1)}, f32[1,1,3072]{2,1,0:T(1,128)S(1)}, u32[]{:S(2)}, u32[]{:S(2)}) collective-permute-start(f32[1,1,3072]{2,1,0:T(1,128)S(1)} %get-tuple-element.51), channel_id=1, source_target_pairs={{0,16},{16,32},{32,48},{48,64},{64,80},{80,96},{96,112},{112,1},{1... | collective-permute-start | bytes 36872 | tf_op jit(solution)/shard_map/ppermute | solution.py:483
  112.3 1.9 collective-permute-start.15
  114.3 2.1 rev.21
  121.6 5.3 %collective-permute-start.9 = (f32[2]{0:T(128)S(1)}, f32[2]{0:T(128)S(1)}, u32[]{:S(2)}, u32[]{:S(2)}) collective-permute-start(f32[2]{0:T(128)S(1)} %fusion.51), channel_id=1, source_target_pairs={{0,64},{16,80},{32,96},{48,112},{64,0},{80,16},{96,32},{112,48},{1... | collective-permute-start | bytes 32 | tf_op jit(solution)/shard_map/ppermute | solution.py:466
  127.9 2.2 collective-permute-start.10
  131.0 9.1 %collective-permute-start.11 = (f32[2]{0:T(128)S(1)}, f32[2]{0:T(128)S(1)}, u32[]{:S(2)}, u32[]{:S(2)}) collective-permute-start(f32[2]{0:T(128)S(1)} %add.188), channel_id=1, source_target_pairs={{0,2},{1,3},{2,0},{3,1},{4,6},{5,7},{6,4},{7,5},{8,10},{9,11},{10,... | collective-permute-start | bytes 32 | tf_op jit(solution)/shard_map/ppermute | solution.py:466
  141.1 2.3 collective-permute-start.12
  144.3 3.1 %collective-permute-start.13 = (f32[2]{0:T(128)S(1)}, f32[2]{0:T(128)S(1)}, u32[]{:S(2)}, u32[]{:S(2)}) collective-permute-start(f32[2]{0:T(128)S(1)} %add.190), channel_id=1, source_target_pairs={{0,8},{1,9},{2,10},{3,11},{4,12},{5,13},{6,14},{7,15},{8,0},{9,1},... | collective-permute-start | bytes 32 | tf_op jit(solution)/shard_map/ppermute | solution.py:466
  151.4 1.8 pad_maximum_fusion.29
  153.2 12.1 %collective-permute-start.16 = (f32[3]{0:T(128)S(1)}, f32[3]{0:T(128)S(1)}, u32[]{:S(2)}, u32[]{:S(2)}) collective-permute-start(f32[3]{0:T(128)S(1)} %pad_maximum_fusion.29), channel_id=1, source_target_pairs={{0,16},{16,0},{32,48},{48,32},{64,80},{80,64},{96,112},{112,96},{1... | collective-permute-start | bytes 44 | tf_op jit(solution)/shard_map/ppermute | solution.py:466
  165.4 1.9 collective-permute-start.23
  167.3 2.4 collective-permute-start.24
  169.7 2.1 rev.22
  171.8 1.8 fusion.47
  173.7 2.4 collective-permute-done.17
  176.1 1.8 fusion.50
  179.2 2.7 %collective-permute-done.18 = f32[3]{0:T(128)S(1)} collective-permute-done((f32[3]{0:T(128)S(1)}, f32[3]{0:T(128)S(1)}, u32[]{:S(2)}, u32[]{:S(2)}) %collective-permute-start.18) | collective-permute-done | bytes 44 | tf_op jit(solution)/shard_map/ppermute | solution.py:466
  181.8 2.4 collective-permute-done.19
  184.3 2.3 collective-permute-start.20
  190.8 3.1 %collective-permute-start.22 = (f32[3]{0:T(128)S(1)}, f32[3]{0:T(128)S(1)}, u32[]{:S(2)}, u32[]{:S(2)}) collective-permute-start(f32[3]{0:T(128)S(1)} %add.203), channel_id=1, source_target_pairs={{0,8},{1,9},{2,10},{3,11},{4,12},{5,13},{6,14},{7,15},{8,0},{9,1},... | collective-permute-start | bytes 44 | tf_op jit(solution)/shard_map/ppermute | solution.py:466
  200.3 2.0 pad_maximum_fusion.30
  202.4 12.1 %collective-permute-start.25 = (f32[3]{0:T(128)S(1)}, f32[3]{0:T(128)S(1)}, u32[]{:S(2)}, u32[]{:S(2)}) collective-permute-start(f32[3]{0:T(128)S(1)} %pad_maximum_fusion.30), channel_id=1, source_target_pairs={{0,16},{16,0},{32,48},{48,32},{64,80},{80,64},{96,112},{112,96},{1... | collective-permute-start | bytes 44 | tf_op jit(solution)/shard_map/ppermute | solution.py:466
  215.3 2.0 fusion.46
  217.3 2.4 collective-permute-done.26
  219.8 2.0 fusion.49
  221.8 3.9 %collective-permute-done.27 = f32[3]{0:T(128)S(1)} collective-permute-done((f32[3]{0:T(128)S(1)}, f32[3]{0:T(128)S(1)}, u32[]{:S(2)}, u32[]{:S(2)}) %collective-permute-start.27) | collective-permute-done | bytes 44 | tf_op jit(solution)/shard_map/ppermute | solution.py:466
  225.7 2.4 collective-permute-done.28
  228.2 3.9 %collective-permute-done.29 = f32[3]{0:T(128)S(1)} collective-permute-done((f32[3]{0:T(128)S(1)}, f32[3]{0:T(128)S(1)}, u32[]{:S(2)}, u32[]{:S(2)}) %collective-permute-start.29) | collective-permute-done | bytes 44 | tf_op jit(solution)/shard_map/ppermute | solution.py:466
  234.7 3.1 %collective-permute-start.31 = (f32[3]{0:T(128)S(1)}, f32[3]{0:T(128)S(1)}, u32[]{:S(2)}, u32[]{:S(2)}) collective-permute-start(f32[3]{0:T(128)S(1)} %add.224), channel_id=1, source_target_pairs={{0,8},{1,9},{2,10},{3,11},{4,12},{5,13},{6,14},{7,15},{8,0},{9,1},... | collective-permute-start | bytes 44 | tf_op jit(solution)/shard_map/ppermute | solution.py:466
  242.6 14.3 %all_to_all.53 = f32[8,8,384]{2,0,1:T(8,128)S(1)} all-to-all(f32[8,8,384]{2,0,1:T(8,128)S(1)} %bitcast.168), channel_id=1, replica_groups=mesh['lon'=8,'lat'=16] {'lon'}, dimensions={1} | all-to-all | bytes 196608 | tf_op jit(solution)/shard_map/all_to_all | solution.py:612
  (138 shorter events, 57.2 us)
Async XLA Ops:
  2.7 2.6 %copy-start.2 = (bf16[20,64,384]{2,1,0:T(8,128)(2,1)S(1)}, bf16[20,64,384]{2,1,0:T(8,128)(2,1)}, u32[]{:S(2)}) copy-start(bf16[20,64,384]{2,1,0:T(8,128)(2,1)} %east_ref.1) | copy-start | bytes 2949124
  16.1 11.4 %collective-permute-start = (f32[5,20,64,2]{2,3,1,0:T(2,128)}, f32[5,20,64,2]{2,3,1,0:T(2,128)}, u32[]{:S(2)}, u32[]{:S(2)}) collective-permute-start(f32[5,20,64,2]{2,3,1,0:T(2,128)} %pad_maximum_fusion.17), channel_id=1, source_target_pairs={{0,112},{16,0},{32,16},{48,32},{64,48},{80,64},{96,80},{112,96},{1... | collective-permute-start | bytes 153608 | tf_op jit(solution)/shard_map/ppermute | solution.py:200
  18.8 8.4 %copy-start.3 = (s32[64,384]{1,0:T(8,128)S(1)}, s32[64,384]{1,0:T(8,128)}, u32[]{:S(2)}) copy-start(s32[64,384]{1,0:T(8,128)} %param.13) | copy-start | bytes 294916
  22.6 4.8 %copy-start.4 = (f32[64,384]{1,0:T(8,128)S(1)}, f32[64,384]{1,0:T(8,128)}, u32[]{:S(2)}) copy-start(f32[64,384]{1,0:T(8,128)} %param.16) | copy-start | bytes 294916
  23.4 7.3 %collective-permute-start.1 = (f32[5,20,64,2]{2,3,1,0:T(2,128)S(1)}, f32[5,20,64,2]{2,3,1,0:T(2,128)S(1)}, u32[]{:S(2)}, u32[]{:S(2)}) collective-permute-start(f32[5,20,64,2]{2,3,1,0:T(2,128)S(1)} %pad_maximum_fusion.18), channel_id=1, source_target_pairs={{0,16},{16,32},{32,48},{48,64},{64,80},{80,96},{96,112},{112,0},{1... | collective-permute-start | bytes 153608 | tf_op jit(solution)/shard_map/ppermute | solution.py:205
  27.4 5.6 %copy-start = (f32[20,64,384]{2,1,0:T(8,128)}, f32[20,64,384]{2,1,0:T(8,128)S(1)}, u32[]{:S(2)}) copy-start(f32[20,64,384]{2,1,0:T(8,128)S(1)} %fusion.wet_ref) | copy-start | bytes 5898244
  36.9 3.7 %copy-start.1 = (f32[5,20,64,128]{3,2,1,0:T(8,128)}, f32[5,20,64,128]{3,2,1,0:T(8,128)S(1)}, u32[]{:S(2)}) copy-start(f32[5,20,64,128]{3,2,1,0:T(8,128)S(1)} %pad_maximum_fusion.cols_ref) | copy-start | bytes 9830404
  36.9 3.6 %slice-start = ((f32[20,64,384]{2,1,0:T(8,128)}), f32[1,64,384]{2,1,0:T(8,128)S(1)}, s32[]{:S(2)}) async-start(f32[20,64,384]{2,1,0:T(8,128)} %copy-done), calls=%async_computation.3 | async-start | bytes 196608 | tf_op jit(solution)/shard_map/slice | solution.py:597
  37.2 15.7 %collective-permute-start.2 = (f32[5,20,2,512]{3,2,1,0:T(2,128)S(1)}, f32[5,20,2,512]{3,2,1,0:T(2,128)S(1)}, u32[]{:S(2)}, u32[]{:S(2)}) collective-permute-start(f32[5,20,2,512]{3,2,1,0:T(2,128)S(1)} %pad_maximum_fusion.2), channel_id=1, source_target_pairs={{0,112},{16,96},{32,80},{48,64},{64,48},{80,32},{96,16},{112,0},{1... | collective-permute-start | bytes 1228808 | tf_op jit(solution)/shard_map/ppermute | solution.py:223
  39.2 15.6 %copy-start.5 = (f32[5]{0:T(128)S(1)}, f32[5]{0:T(128)}, u32[]{:S(2)}) copy-start(f32[5]{0:T(128)} %constant.10.clone) | copy-start | bytes 64
  39.2 15.5 %collective-permute-start.3 = (f32[5,20,2,512]{3,2,1,0:T(2,128)S(1)}, f32[5,20,2,512]{3,2,1,0:T(2,128)S(1)}, u32[]{:S(2)}, u32[]{:S(2)}) collective-permute-start(f32[5,20,2,512]{3,2,1,0:T(2,128)S(1)} %pad_maximum_fusion.3), channel_id=1, source_target_pairs={{1,0},{2,1},{3,2},{4,3},{5,4},{6,5},{7,6},{8,7},{9,8},{10,9},{11,1... | collective-permute-start | bytes 1228808 | tf_op jit(solution)/shard_map/ppermute | solution.py:221
  41.4 11.5 %all-to-all-start.1 = ((f32[2,64,384]{2,0,1:T(2,128)}), f32[2,64,384]{2,0,1:T(2,128)S(1)}, u32[]{:S(2)}, u32[]{:S(2)}) async-start(f32[2,64,384]{2,0,1:T(2,128)} %copy.39), calls=%async_computation.1 | async-start | bytes 393216 | tf_op jit(solution)/shard_map/all_to_all | solution.py:596
  47.0 12.9 %collective-permute-start.4 = (f32[5,20,2,512]{3,2,1,0:T(2,128)S(1)}, f32[5,20,2,512]{3,2,1,0:T(2,128)S(1)}, u32[]{:S(2)}, u32[]{:S(2)}) collective-permute-start(f32[5,20,2,512]{3,2,1,0:T(2,128)S(1)} %pad_maximum_fusion.2), channel_id=1, source_target_pairs={{0,1},{1,2},{2,3},{3,4},{4,5},{5,6},{6,7},{7,8},{8,9},{9,10},{10,1... | collective-permute-start | bytes 1228808 | tf_op jit(solution)/shard_map/ppermute | solution.py:222
  88.1 10.4 %all-to-all-start = ((f32[8,8,384]{2,1,0:T(8,128)}), f32[8,8,384]{2,1,0:T(8,128)S(1)}, u32[]{:S(2)}, u32[]{:S(2)}) async-start(f32[8,8,384]{2,1,0:T(8,128)} %bitcast.170), calls=%async_computation | async-start | bytes 196608 | tf_op jit(solution)/shard_map/all_to_all | solution.py:610
  98.5 8.5 %collective-permute-start.6 = (f32[3,1,3072]{2,1,0:T(1,128)S(1)}, f32[3,1,3072]{2,1,0:T(1,128)S(1)}, u32[]{:S(2)}, u32[]{:S(2)}) collective-permute-start(f32[3,1,3072]{2,1,0:T(1,128)S(1)} %get-tuple-element.38), channel_id=1, source_target_pairs={{16,0},{32,16},{48,32},{64,48},{80,64},{96,80},{112,96},{1,112},{1... | collective-permute-start | bytes 110600 | tf_op jit(solution)/shard_map/ppermute | solution.py:480
  101.2 5.7 %collective-permute-start.5 = (f32[3,1,3072]{2,1,0:T(1,128)S(1)}, f32[3,1,3072]{2,1,0:T(1,128)S(1)}, u32[]{:S(2)}, u32[]{:S(2)}) collective-permute-start(f32[3,1,3072]{2,1,0:T(1,128)S(1)} %get-tuple-element.37), channel_id=1, source_target_pairs={{0,16},{16,32},{32,48},{48,64},{64,80},{80,96},{96,112},{112,1},{1... | collective-permute-start | bytes 110600 | tf_op jit(solution)/shard_map/ppermute | solution.py:483
  109.4 7.0 %collective-permute-start.7 = (f32[2]{0:T(128)S(1)}, f32[2]{0:T(128)S(1)}, u32[]{:S(2)}, u32[]{:S(2)}) collective-permute-start(f32[2]{0:T(128)S(1)} %pad_maximum_fusion.28), channel_id=1, source_target_pairs={{0,16},{16,0},{32,48},{48,32},{64,80},{80,64},{96,112},{112,96},{1... | collective-permute-start | bytes 32 | tf_op jit(solution)/shard_map/ppermute | solution.py:466
  109.5 40.9 %collective-permute-start.14 = (f32[1,1,3072]{2,1,0:T(1,128)S(1)}, f32[1,1,3072]{2,1,0:T(1,128)S(1)}, u32[]{:S(2)}, u32[]{:S(2)}) collective-permute-start(f32[1,1,3072]{2,1,0:T(1,128)S(1)} %get-tuple-element.51), channel_id=1, source_target_pairs={{0,16},{16,32},{32,48},{48,64},{64,80},{80,96},{96,112},{112,1},{1... | collective-permute-start | bytes 36872 | tf_op jit(solution)/shard_map/ppermute | solution.py:483
  112.3 38.1 %collective-permute-start.15 = (f32[1,1,3072]{2,1,0:T(1,128)S(1)}, f32[1,1,3072]{2,1,0:T(1,128)S(1)}, u32[]{:S(2)}, u32[]{:S(2)}) collective-permute-start(f32[1,1,3072]{2,1,0:T(1,128)S(1)} %get-tuple-element.52), channel_id=1, source_target_pairs={{16,0},{32,16},{48,32},{64,48},{80,64},{96,80},{112,96},{1,112},{1... | collective-permute-start | bytes 36872 | tf_op jit(solution)/shard_map/ppermute | solution.py:480
  117.8 2.4 collective-permute-start.8
  121.6 6.3 %collective-permute-start.9 = (f32[2]{0:T(128)S(1)}, f32[2]{0:T(128)S(1)}, u32[]{:S(2)}, u32[]{:S(2)}) collective-permute-start(f32[2]{0:T(128)S(1)} %fusion.51), channel_id=1, source_target_pairs={{0,64},{16,80},{32,96},{48,112},{64,0},{80,16},{96,32},{112,48},{1... | collective-permute-start | bytes 32 | tf_op jit(solution)/shard_map/ppermute | solution.py:466
  127.9 3.2 %collective-permute-start.10 = (f32[2]{0:T(128)S(1)}, f32[2]{0:T(128)S(1)}, u32[]{:S(2)}, u32[]{:S(2)}) collective-permute-start(f32[2]{0:T(128)S(1)} %add.187), channel_id=1, source_target_pairs={{0,1},{1,0},{2,3},{3,2},{4,5},{5,4},{6,7},{7,6},{8,9},{9,8},{10,11... | collective-permute-start | bytes 32 | tf_op jit(solution)/shard_map/ppermute | solution.py:466
  131.0 10.0 %collective-permute-start.11 = (f32[2]{0:T(128)S(1)}, f32[2]{0:T(128)S(1)}, u32[]{:S(2)}, u32[]{:S(2)}) collective-permute-start(f32[2]{0:T(128)S(1)} %add.188), channel_id=1, source_target_pairs={{0,2},{1,3},{2,0},{3,1},{4,6},{5,7},{6,4},{7,5},{8,10},{9,11},{10,... | collective-permute-start | bytes 32 | tf_op jit(solution)/shard_map/ppermute | solution.py:466
  141.1 3.3 %collective-permute-start.12 = (f32[2]{0:T(128)S(1)}, f32[2]{0:T(128)S(1)}, u32[]{:S(2)}, u32[]{:S(2)}) collective-permute-start(f32[2]{0:T(128)S(1)} %add.189), channel_id=1, source_target_pairs={{0,4},{1,5},{2,6},{3,7},{4,0},{5,1},{6,2},{7,3},{8,12},{9,13},{10,... | collective-permute-start | bytes 32 | tf_op jit(solution)/shard_map/ppermute | solution.py:466
  144.3 4.0 %collective-permute-start.13 = (f32[2]{0:T(128)S(1)}, f32[2]{0:T(128)S(1)}, u32[]{:S(2)}, u32[]{:S(2)}) collective-permute-start(f32[2]{0:T(128)S(1)} %add.190), channel_id=1, source_target_pairs={{0,8},{1,9},{2,10},{3,11},{4,12},{5,13},{6,14},{7,15},{8,0},{9,1},... | collective-permute-start | bytes 32 | tf_op jit(solution)/shard_map/ppermute | solution.py:466
  153.2 18.6 %collective-permute-start.16 = (f32[3]{0:T(128)S(1)}, f32[3]{0:T(128)S(1)}, u32[]{:S(2)}, u32[]{:S(2)}) collective-permute-start(f32[3]{0:T(128)S(1)} %pad_maximum_fusion.29), channel_id=1, source_target_pairs={{0,16},{16,0},{32,48},{48,32},{64,80},{80,64},{96,112},{112,96},{1... | collective-permute-start | bytes 44 | tf_op jit(solution)/shard_map/ppermute | solution.py:466
  165.4 33.8 %collective-permute-start.23 = (f32[1,1,3072]{2,1,0:T(1,128)S(1)}, f32[1,1,3072]{2,1,0:T(1,128)S(1)}, u32[]{:S(2)}, u32[]{:S(2)}) collective-permute-start(f32[1,1,3072]{2,1,0:T(1,128)S(1)} %get-tuple-element.49), channel_id=1, source_target_pairs={{0,16},{16,32},{32,48},{48,64},{64,80},{80,96},{96,112},{112,1},{1... | collective-permute-start | bytes 36872 | tf_op jit(solution)/shard_map/ppermute | solution.py:483
  167.3 31.9 %collective-permute-start.24 = (f32[1,1,3072]{2,1,0:T(1,128)S(1)}, f32[1,1,3072]{2,1,0:T(1,128)S(1)}, u32[]{:S(2)}, u32[]{:S(2)}) collective-permute-start(f32[1,1,3072]{2,1,0:T(1,128)S(1)} %get-tuple-element.50), channel_id=1, source_target_pairs={{16,0},{32,16},{48,32},{64,48},{80,64},{96,80},{112,96},{1,112},{1... | collective-permute-start | bytes 36872 | tf_op jit(solution)/shard_map/ppermute | solution.py:480
  173.6 2.4 collective-permute-start.17
  177.9 3.9 %collective-permute-start.18 = (f32[3]{0:T(128)S(1)}, f32[3]{0:T(128)S(1)}, u32[]{:S(2)}, u32[]{:S(2)}) collective-permute-start(f32[3]{0:T(128)S(1)} %fusion.50), channel_id=1, source_target_pairs={{0,64},{16,80},{32,96},{48,112},{64,0},{80,16},{96,32},{112,48},{1... | collective-permute-start | bytes 44 | tf_op jit(solution)/shard_map/ppermute | solution.py:466
  181.8 2.4 collective-permute-start.19
  184.3 3.9 %collective-permute-start.20 = (f32[3]{0:T(128)S(1)}, f32[3]{0:T(128)S(1)}, u32[]{:S(2)}, u32[]{:S(2)}) collective-permute-start(f32[3]{0:T(128)S(1)} %add.201), channel_id=1, source_target_pairs={{0,2},{1,3},{2,0},{3,1},{4,6},{5,7},{6,4},{7,5},{8,10},{9,11},{10,... | collective-permute-start | bytes 44 | tf_op jit(solution)/shard_map/ppermute | solution.py:466
  188.2 2.6 %collective-permute-start.21 = (f32[3]{0:T(128)S(1)}, f32[3]{0:T(128)S(1)}, u32[]{:S(2)}, u32[]{:S(2)}) collective-permute-start(f32[3]{0:T(128)S(1)} %add.202), channel_id=1, source_target_pairs={{0,4},{1,5},{2,6},{3,7},{4,0},{5,1},{6,2},{7,3},{8,12},{9,13},{10,... | collective-permute-start | bytes 44 | tf_op jit(solution)/shard_map/ppermute | solution.py:466
  190.8 4.0 %collective-permute-start.22 = (f32[3]{0:T(128)S(1)}, f32[3]{0:T(128)S(1)}, u32[]{:S(2)}, u32[]{:S(2)}) collective-permute-start(f32[3]{0:T(128)S(1)} %add.203), channel_id=1, source_target_pairs={{0,8},{1,9},{2,10},{3,11},{4,12},{5,13},{6,14},{7,15},{8,0},{9,1},... | collective-permute-start | bytes 44 | tf_op jit(solution)/shard_map/ppermute | solution.py:466
  202.4 12.9 %collective-permute-start.25 = (f32[3]{0:T(128)S(1)}, f32[3]{0:T(128)S(1)}, u32[]{:S(2)}, u32[]{:S(2)}) collective-permute-start(f32[3]{0:T(128)S(1)} %pad_maximum_fusion.30), channel_id=1, source_target_pairs={{0,16},{16,0},{32,48},{48,32},{64,80},{80,64},{96,112},{112,96},{1... | collective-permute-start | bytes 44 | tf_op jit(solution)/shard_map/ppermute | solution.py:466
  217.3 2.4 collective-permute-start.26
  221.8 3.9 %collective-permute-start.27 = (f32[3]{0:T(128)S(1)}, f32[3]{0:T(128)S(1)}, u32[]{:S(2)}, u32[]{:S(2)}) collective-permute-start(f32[3]{0:T(128)S(1)} %fusion.49), channel_id=1, source_target_pairs={{0,64},{16,80},{32,96},{48,112},{64,0},{80,16},{96,32},{112,48},{1... | collective-permute-start | bytes 44 | tf_op jit(solution)/shard_map/ppermute | solution.py:466
  225.7 2.4 collective-permute-start.28
  228.1 3.9 %collective-permute-start.29 = (f32[3]{0:T(128)S(1)}, f32[3]{0:T(128)S(1)}, u32[]{:S(2)}, u32[]{:S(2)}) collective-permute-start(f32[3]{0:T(128)S(1)} %add.222), channel_id=1, source_target_pairs={{0,2},{1,3},{2,0},{3,1},{4,6},{5,7},{6,4},{7,5},{8,10},{9,11},{10,... | collective-permute-start | bytes 44 | tf_op jit(solution)/shard_map/ppermute | solution.py:466
  232.1 2.6 %collective-permute-start.30 = (f32[3]{0:T(128)S(1)}, f32[3]{0:T(128)S(1)}, u32[]{:S(2)}, u32[]{:S(2)}) collective-permute-start(f32[3]{0:T(128)S(1)} %add.223), channel_id=1, source_target_pairs={{0,4},{1,5},{2,6},{3,7},{4,0},{5,1},{6,2},{7,3},{8,12},{9,13},{10,... | collective-permute-start | bytes 44 | tf_op jit(solution)/shard_map/ppermute | solution.py:466
  234.7 4.0 %collective-permute-start.31 = (f32[3]{0:T(128)S(1)}, f32[3]{0:T(128)S(1)}, u32[]{:S(2)}, u32[]{:S(2)}) collective-permute-start(f32[3]{0:T(128)S(1)} %add.224), channel_id=1, source_target_pairs={{0,8},{1,9},{2,10},{3,11},{4,12},{5,13},{6,14},{7,15},{8,0},{9,1},... | collective-permute-start | bytes 44 | tf_op jit(solution)/shard_map/ppermute | solution.py:466

commit v7 on v5

--- a/solution.py
+++ b/solution.py
@@ -146,13 +146,15 @@
 
     east_speed = field(3)
     north_speed = field(4)
-    east_mean = 0.5 * (east_speed + east(east_speed))
-    north_mean = 0.5 * (north_speed + north(north_speed))
+    east_mean = 0.5 * (east_speed + east(east_speed)) * 0.5
+    north_mean = 0.5 * (north_speed + north(north_speed)) * 0.5
+    east_pair = wet * wet_near[3]
+    north_pair = wet * wet_near[1]
     for t in range(out_ref.shape[0]):
         tracer = field(t)
         lap_two = laplacian(laplacian(tracer))
-        east_flux = east_mean * 0.5 * (tracer + east(tracer)) * wet * wet_near[3]
-        north_flux = north_mean * 0.5 * (tracer + north(tracer)) * wet * wet_near[1]
+        east_flux = east_mean * (tracer + east(tracer)) * east_pair
+        north_flux = north_mean * (tracer + north(tracer)) * north_pair
         divergence = east_flux - west(east_flux) + north_flux - south(north_flux)
         result = wet * (tracer - advection_rate * divergence - biharmonic_rate * lap_two)
         out_ref[t, 0] = result[:row_count, :col_count]

time: 253 us -> 253 us (level)
  no operation moved by 1% of the time
where the time goes in v7:
time: 253 us; the launch traced here: 252 us
  starting transfers between devices  95.1 us (38%)
  waiting for transfers between devices  44.5 us (18%)
  other arithmetic  32.1 us (13%)
  local copies, waits for them, and re-layouts  29.7 us (12%)
  Pallas kernels  26.5 us (10%)
  blocking collectives  14.3 us (6%)
  between operations  9.33 us (4%)
    ppermute x21, starting transfers between devices, butterfly_sum(): lax.ppermute(value, axis, [(i, i ^ bit) for i in range(count)])  59.7 us
    ppermute x21, waiting for transfers between devices, butterfly_sum(): lax.ppermute(value, axis, [(i, i ^ bit) for i in range(count)])  33.2 us
    pallas_call x1, Pallas kernels, assembling_call(): pl.pallas_call(assembling_kernel, grid=(level_count,), in_specs=[pl.Block...  20.7 us
    all_to_all x1, blocking collectives, shards(): lax.all_to_all(strip_solution, 'lon', split_axis=1, concat_axis=0, tiled=...  14.3 us
    add x21, other arithmetic, butterfly_sum(): value + lax.ppermute(value, axis, [(i, i ^ bit) for i in range(count)])  10.5 us
    ppermute x3, starting transfers between devices, neighbour_rows(): lax.ppermute(values[:, -1:, :], axes, [(device(s - 1), device(s)) for s i...  7.32 us
    ppermute x3, starting transfers between devices, neighbour_rows(): lax.ppermute(values[:, 0:1, :], axes, [(device(s + 1), device(s)) for s i...  7.05 us
    rev x3, local copies, waits for them, and re-layouts, strip_assemble(): jnp.flip(surface_field[-1:, :], axis=1)  6.33 us
  transfers between devices with their start and end apart: 34, of which 22 were waited for; matrix products, arithmetic and copies ran while one was open for 11% of the time, Pallas kernels for 0%

profile of v7, /device:TPU:1, one launch (start us, length us, event | category | flops | bytes accessed | tf_op | source)
XLA Modules:
  0.0 251.6 jit_solution(18006201576979337778)
XLA Ops:
  9.0 2.2 fusion.35
  20.3 1.7 fusion.37
  22.1 3.1 %copy.51 = f32[5,20,64,2]{3,2,1,0:T(8,128)} copy(f32[5,20,64,2]{2,3,1,0:T(2,128)} %collective-permute-done) | data formatting | bytes 102400 | tf_op jit(solution)/shard_map/ppermute | solution.py:202
  25.2 2.3 copy.52
  27.6 3.8 %pad_maximum_fusion.cols_ref = f32[5,20,64,128]{3,2,1,0:T(8,128)S(1)} fusion(f32[5,20,64,2]{3,2,1,0:T(8,128)} %copy.52, f32[5,20,64,2]{3,2,1,0:T(8,128)} %copy.51, f32[128]{0:T(128)S(1)} %pad.74.clone), kind=kLoop, calls=%fused_computation | loop fusion | flops 1638400 | bytes 3379712 | tf_op jit(solution)/shard_map/concatenate | solution.py:212
  31.7 1.8 collective-permute-start.2
  36.0 5.6 %all-to-all-start.1 = ((f32[2,64,384]{2,0,1:T(2,128)}), f32[2,64,384]{2,0,1:T(2,128)S(1)}, u32[]{:S(2)}, u32[]{:S(2)}) async-start(f32[2,64,384]{2,0,1:T(2,128)} %copy.53), calls=%async_computation.1 | async-start | bytes 393216 | tf_op jit(solution)/shard_map/all_to_all | solution.py:584
  41.5 4.3 %collective-permute-start.4 = (f32[5,20,2,512]{3,2,1,0:T(2,128)S(1)}, f32[5,20,2,512]{3,2,1,0:T(2,128)S(1)}, u32[]{:S(2)}, u32[]{:S(2)}) collective-permute-start(f32[5,20,2,512]{3,2,1,0:T(2,128)S(1)} %pad_maximum_fusion.2), channel_id=1, source_target_pairs={{0,1},{1,2},{2,3},{3,4},{4,5},{5,6},{6,7},{7,8},{8,9},{9,10},{10,1... | collective-permute-start | bytes 1228808 | tf_op jit(solution)/shard_map/ppermute | solution.py:224
  49.6 4.8 %collective-permute-done.4 = f32[5,20,2,512]{3,2,1,0:T(2,128)S(1)} collective-permute-done((f32[5,20,2,512]{3,2,1,0:T(2,128)S(1)}, f32[5,20,2,512]{3,2,1,0:T(2,128)S(1)}, u32[]{:S(2)}, u32[]{:S(2)}) %collective-permute-start.4) | collective-permute-done | bytes 409632 | tf_op jit(solution)/shard_map/ppermute | solution.py:224
  56.0 20.7 %shard_map.104.values_ref = f32[2,20,64,384]{3,2,1,0:T(8,128)} custom-call(f32[2,20,64,384]{3,2,1,0:T(8,128)} %tracer_ref.1, f32[20,64,384]{2,1,0:T(8,128)} %copy-done, bf16[20,64,384]{2,1,0:T(8,128)(2,1)} %east_ref.1, bf16[20,64,384]{2,1,0:T(8,128)(2,1)} %north_ref.1, f32[5,20,64,128]{3,2,1,0:T(8,128)} %copy-done.1, ...), custom_call_target="tpu_custom_call" | custom-call | tf_op jit(solution)/shard_map/pallas_call | solution.py:241
  76.8 5.8 %shard_map.105 = (f32[2,20,64,384]{3,2,1,0:T(8,128)}, f32[64,384]{1,0:T(8,128)}) custom-call(f32[2,20,64,384]{3,2,1,0:T(8,128)} %shard_map.104.values_ref, f32[20,64,384]{2,1,0:T(8,128)} %copy-done, bf16[20,64,384]{2,1,0:T(8,128)(2,1)} %diff_ref.1, f32[64,384]{1,0:T(8,128)} %forcing_ref.1), custom_call_target="tpu_custom_call" | custom-call | tf_op jit(solution)/shard_map/pallas_call | solution.py:341
  82.6 5.4 %all-to-all-start = ((f32[8,8,384]{2,1,0:T(8,128)}), f32[8,8,384]{2,1,0:T(8,128)S(1)}, u32[]{:S(2)}, u32[]{:S(2)}) async-start(f32[8,8,384]{2,1,0:T(8,128)} %bitcast.167), calls=%async_computation | async-start | bytes 196608 | tf_op jit(solution)/shard_map/all_to_all | solution.py:598
  88.0 5.0 %all-to-all-done = f32[8,8,384]{2,1,0:T(8,128)S(1)} async-done(((f32[8,8,384]{2,1,0:T(8,128)}), f32[8,8,384]{2,1,0:T(8,128)S(1)}, u32[]{:S(2)}, u32[]{:S(2)}) %all-to-all-start) | async-done | bytes 98336 | tf_op jit(solution)/shard_map/all_to_all | solution.py:598
  93.0 2.7 %collective-permute-start.6 = (f32[3,1,3072]{2,1,0:T(1,128)S(1)}, f32[3,1,3072]{2,1,0:T(1,128)S(1)}, u32[]{:S(2)}, u32[]{:S(2)}) collective-permute-start(f32[3,1,3072]{2,1,0:T(1,128)S(1)} %get-tuple-element.38), channel_id=1, source_target_pairs={{16,0},{32,16},{48,32},{64,48},{80,64},{96,80},{112,96},{1,112},{1... | collective-permute-start | bytes 110600 | tf_op jit(solution)/shard_map/ppermute | solution.py:482
  95.7 2.8 %collective-permute-start.5 = (f32[3,1,3072]{2,1,0:T(1,128)S(1)}, f32[3,1,3072]{2,1,0:T(1,128)S(1)}, u32[]{:S(2)}, u32[]{:S(2)}) collective-permute-start(f32[3,1,3072]{2,1,0:T(1,128)S(1)} %get-tuple-element.37), channel_id=1, source_target_pairs={{0,16},{16,32},{32,48},{48,64},{64,80},{80,96},{96,112},{112,1},{1... | collective-permute-start | bytes 110600 | tf_op jit(solution)/shard_map/ppermute | solution.py:485
  99.3 2.1 rev.12
  103.9 2.6 %collective-permute-start.14 = (f32[1,1,3072]{2,1,0:T(1,128)S(1)}, f32[1,1,3072]{2,1,0:T(1,128)S(1)}, u32[]{:S(2)}, u32[]{:S(2)}) collective-permute-start(f32[1,1,3072]{2,1,0:T(1,128)S(1)} %get-tuple-element.49), channel_id=1, source_target_pairs={{0,16},{16,32},{32,48},{48,64},{64,80},{80,96},{96,112},{112,1},{1... | collective-permute-start | bytes 36872 | tf_op jit(solution)/shard_map/ppermute | solution.py:485
  106.5 1.9 collective-permute-start.15
  110.2 2.0 collective-permute-done.8
  113.5 5.3 %collective-permute-start.9 = (f32[2]{0:T(128)S(1)}, f32[2]{0:T(128)S(1)}, u32[]{:S(2)}, u32[]{:S(2)}) collective-permute-start(f32[2]{0:T(128)S(1)} %fusion.50), channel_id=1, source_target_pairs={{0,64},{16,80},{32,96},{48,112},{64,0},{80,16},{96,32},{112,48},{1... | collective-permute-start | bytes 32 | tf_op jit(solution)/shard_map/ppermute | solution.py:468
  119.8 1.6 collective-permute-start.10
  122.4 9.6 %collective-permute-start.11 = (f32[2]{0:T(128)S(1)}, f32[2]{0:T(128)S(1)}, u32[]{:S(2)}, u32[]{:S(2)}) collective-permute-start(f32[2]{0:T(128)S(1)} %add.185), channel_id=1, source_target_pairs={{0,2},{1,3},{2,0},{3,1},{4,6},{5,7},{6,4},{7,5},{8,10},{9,11},{10,... | collective-permute-start | bytes 32 | tf_op jit(solution)/shard_map/ppermute | solution.py:468
  133.0 2.6 %collective-permute-start.12 = (f32[2]{0:T(128)S(1)}, f32[2]{0:T(128)S(1)}, u32[]{:S(2)}, u32[]{:S(2)}) collective-permute-start(f32[2]{0:T(128)S(1)} %add.186), channel_id=1, source_target_pairs={{0,4},{1,5},{2,6},{3,7},{4,0},{5,1},{6,2},{7,3},{8,12},{9,13},{10,... | collective-permute-start | bytes 32 | tf_op jit(solution)/shard_map/ppermute | solution.py:468
  136.5 3.1 %collective-permute-start.13 = (f32[2]{0:T(128)S(1)}, f32[2]{0:T(128)S(1)}, u32[]{:S(2)}, u32[]{:S(2)}) collective-permute-start(f32[2]{0:T(128)S(1)} %add.187), channel_id=1, source_target_pairs={{0,8},{1,9},{2,10},{3,11},{4,12},{5,13},{6,14},{7,15},{8,0},{9,1},... | collective-permute-start | bytes 32 | tf_op jit(solution)/shard_map/ppermute | solution.py:468
  142.5 2.1 rev.13
  145.7 1.9 pad_maximum_fusion.29
  147.6 11.8 %collective-permute-start.16 = (f32[3]{0:T(128)S(1)}, f32[3]{0:T(128)S(1)}, u32[]{:S(2)}, u32[]{:S(2)}) collective-permute-start(f32[3]{0:T(128)S(1)} %pad_maximum_fusion.29), channel_id=1, source_target_pairs={{0,16},{16,0},{32,48},{48,32},{64,80},{80,64},{96,112},{112,96},{1... | collective-permute-start | bytes 44 | tf_op jit(solution)/shard_map/ppermute | solution.py:468
  159.4 1.9 collective-permute-start.23
  161.4 2.4 collective-permute-start.24
  163.8 1.9 fusion.46
  165.7 2.4 collective-permute-done.17
  168.1 1.9 fusion.49
  171.3 2.7 %collective-permute-done.18 = f32[3]{0:T(128)S(1)} collective-permute-done((f32[3]{0:T(128)S(1)}, f32[3]{0:T(128)S(1)}, u32[]{:S(2)}, u32[]{:S(2)}) %collective-permute-start.18) | collective-permute-done | bytes 44 | tf_op jit(solution)/shard_map/ppermute | solution.py:468
  173.9 2.4 collective-permute-done.19
  176.4 2.3 collective-permute-start.20
  180.3 1.8 collective-permute-start.21
  183.1 3.1 %collective-permute-start.22 = (f32[3]{0:T(128)S(1)}, f32[3]{0:T(128)S(1)}, u32[]{:S(2)}, u32[]{:S(2)}) collective-permute-start(f32[3]{0:T(128)S(1)} %add.200), channel_id=1, source_target_pairs={{0,8},{1,9},{2,10},{3,11},{4,12},{5,13},{6,14},{7,15},{8,0},{9,1},... | collective-permute-start | bytes 44 | tf_op jit(solution)/shard_map/ppermute | solution.py:468
  191.5 2.1 rev.14
  194.7 2.0 pad_maximum_fusion.30
  196.7 11.9 %collective-permute-start.25 = (f32[3]{0:T(128)S(1)}, f32[3]{0:T(128)S(1)}, u32[]{:S(2)}, u32[]{:S(2)}) collective-permute-start(f32[3]{0:T(128)S(1)} %pad_maximum_fusion.30), channel_id=1, source_target_pairs={{0,16},{16,0},{32,48},{48,32},{64,80},{80,64},{96,112},{112,96},{1... | collective-permute-start | bytes 44 | tf_op jit(solution)/shard_map/ppermute | solution.py:468
  209.5 2.0 fusion.45
  211.5 2.4 collective-permute-done.26
  213.9 2.0 fusion.48
  215.9 3.9 %collective-permute-done.27 = f32[3]{0:T(128)S(1)} collective-permute-done((f32[3]{0:T(128)S(1)}, f32[3]{0:T(128)S(1)}, u32[]{:S(2)}, u32[]{:S(2)}) %collective-permute-start.27) | collective-permute-done | bytes 44 | tf_op jit(solution)/shard_map/ppermute | solution.py:468
  219.8 2.4 collective-permute-done.28
  222.3 3.9 %collective-permute-done.29 = f32[3]{0:T(128)S(1)} collective-permute-done((f32[3]{0:T(128)S(1)}, f32[3]{0:T(128)S(1)}, u32[]{:S(2)}, u32[]{:S(2)}) %collective-permute-start.29) | collective-permute-done | bytes 44 | tf_op jit(solution)/shard_map/ppermute | solution.py:468
  228.8 3.1 %collective-permute-start.31 = (f32[3]{0:T(128)S(1)}, f32[3]{0:T(128)S(1)}, u32[]{:S(2)}, u32[]{:S(2)}) collective-permute-start(f32[3]{0:T(128)S(1)} %add.220), channel_id=1, source_target_pairs={{0,8},{1,9},{2,10},{3,11},{4,12},{5,13},{6,14},{7,15},{8,0},{9,1},... | collective-permute-start | bytes 44 | tf_op jit(solution)/shard_map/ppermute | solution.py:468
  236.7 14.3 %all_to_all.53 = f32[8,8,384]{2,0,1:T(8,128)S(1)} all-to-all(f32[8,8,384]{2,0,1:T(8,128)S(1)} %bitcast.165), channel_id=1, replica_groups=mesh['lon'=8,'lat'=16] {'lon'}, dimensions={1} | all-to-all | bytes 196608 | tf_op jit(solution)/shard_map/all_to_all | solution.py:600
  (141 shorter events, 50.7 us)
Async XLA Ops:
  2.7 1.3 copy-start.2
  4.0 1.2 copy-start.3
  4.2 2.9 %copy-start.4 = (bf16[20,64,384]{2,1,0:T(8,128)(2,1)S(1)}, bf16[20,64,384]{2,1,0:T(8,128)(2,1)}, u32[]{:S(2)}) copy-start(bf16[20,64,384]{2,1,0:T(8,128)(2,1)} %north_ref.1) | copy-start | bytes 2949124
  11.7 3.9 %copy-start.5 = (f32[1,20,64,2]{3,2,1,0:T(8,128)S(1)}, f32[1,20,64,2]{3,2,1,0:T(8,128)}, u32[]{:S(2)}) copy-start(f32[1,20,64,2]{3,2,1,0:T(8,128)} %get-tuple-element.36) | copy-start | bytes 30724
  12.6 9.5 %collective-permute-start = (f32[5,20,64,2]{2,3,1,0:T(2,128)S(1)}, f32[5,20,64,2]{2,3,1,0:T(2,128)}, u32[]{:S(2)}, u32[]{:S(2)}) collective-permute-start(f32[5,20,64,2]{2,3,1,0:T(2,128)S(1)} %pad_maximum_fusion.17), channel_id=1, source_target_pairs={{0,112},{16,0},{32,16},{48,32},{64,48},{80,64},{96,80},{112,96},{1... | collective-permute-start | bytes 153608 | tf_op jit(solution)/shard_map/ppermute | solution.py:202
  14.2 5.9 %copy-start.6 = (s32[64,384]{1,0:T(8,128)S(1)}, s32[64,384]{1,0:T(8,128)}, u32[]{:S(2)}) copy-start(s32[64,384]{1,0:T(8,128)} %param.13) | copy-start | bytes 294916
  16.4 8.8 %collective-permute-start.1 = (f32[5,20,64,2]{2,3,1,0:T(2,128)S(1)}, f32[5,20,64,2]{2,3,1,0:T(2,128)S(1)}, u32[]{:S(2)}, u32[]{:S(2)}) collective-permute-start(f32[5,20,64,2]{2,3,1,0:T(2,128)S(1)} %pad_maximum_fusion.18), channel_id=1, source_target_pairs={{0,16},{16,32},{32,48},{48,64},{64,80},{80,96},{96,112},{112,0},{1... | collective-permute-start | bytes 153608 | tf_op jit(solution)/shard_map/ppermute | solution.py:207
  20.3 7.3 %copy-start = (f32[20,64,384]{2,1,0:T(8,128)}, f32[20,64,384]{2,1,0:T(8,128)S(1)}, u32[]{:S(2)}) copy-start(f32[20,64,384]{2,1,0:T(8,128)S(1)} %fusion.wet_ref) | copy-start | bytes 5898244
  31.4 3.7 %copy-start.1 = (f32[5,20,64,128]{3,2,1,0:T(8,128)}, f32[5,20,64,128]{3,2,1,0:T(8,128)S(1)}, u32[]{:S(2)}) copy-start(f32[5,20,64,128]{3,2,1,0:T(8,128)S(1)} %pad_maximum_fusion.cols_ref) | copy-start | bytes 9830404
  31.4 3.6 %copy-start.7 = (f32[64,384]{1,0:T(8,128)S(1)}, f32[64,384]{1,0:T(8,128)}, u32[]{:S(2)}) copy-start(f32[64,384]{1,0:T(8,128)} %param.16) | copy-start | bytes 294916
  31.4 3.6 %slice-start = ((f32[20,64,384]{2,1,0:T(8,128)}), f32[1,64,384]{2,1,0:T(8,128)S(1)}, s32[]{:S(2)}) async-start(f32[20,64,384]{2,1,0:T(8,128)} %copy-done), calls=%async_computation.3 | async-start | bytes 196608 | tf_op jit(solution)/shard_map/slice | solution.py:585
  31.7 15.7 %collective-permute-start.2 = (f32[5,20,2,512]{3,2,1,0:T(2,128)S(1)}, f32[5,20,2,512]{3,2,1,0:T(2,128)S(1)}, u32[]{:S(2)}, u32[]{:S(2)}) collective-permute-start(f32[5,20,2,512]{3,2,1,0:T(2,128)S(1)} %pad_maximum_fusion.2), channel_id=1, source_target_pairs={{0,112},{16,96},{32,80},{48,64},{64,48},{80,32},{96,16},{112,0},{1... | collective-permute-start | bytes 1228808 | tf_op jit(solution)/shard_map/ppermute | solution.py:225
  33.6 15.7 %copy-start.8 = (f32[5]{0:T(128)S(1)}, f32[5]{0:T(128)}, u32[]{:S(2)}) copy-start(f32[5]{0:T(128)} %constant.10.clone) | copy-start | bytes 64
  33.8 15.5 %collective-permute-start.3 = (f32[5,20,2,512]{3,2,1,0:T(2,128)S(1)}, f32[5,20,2,512]{3,2,1,0:T(2,128)S(1)}, u32[]{:S(2)}, u32[]{:S(2)}) collective-permute-start(f32[5,20,2,512]{3,2,1,0:T(2,128)S(1)} %pad_maximum_fusion.3), channel_id=1, source_target_pairs={{1,0},{2,1},{3,2},{4,3},{5,4},{6,5},{7,6},{8,7},{9,8},{10,9},{11,1... | collective-permute-start | bytes 1228808 | tf_op jit(solution)/shard_map/ppermute | solution.py:223
  36.0 11.5 %all-to-all-start.1 = ((f32[2,64,384]{2,0,1:T(2,128)}), f32[2,64,384]{2,0,1:T(2,128)S(1)}, u32[]{:S(2)}, u32[]{:S(2)}) async-start(f32[2,64,384]{2,0,1:T(2,128)} %copy.53), calls=%async_computation.1 | async-start | bytes 393216 | tf_op jit(solution)/shard_map/all_to_all | solution.py:584
  41.5 12.9 %collective-permute-start.4 = (f32[5,20,2,512]{3,2,1,0:T(2,128)S(1)}, f32[5,20,2,512]{3,2,1,0:T(2,128)S(1)}, u32[]{:S(2)}, u32[]{:S(2)}) collective-permute-start(f32[5,20,2,512]{3,2,1,0:T(2,128)S(1)} %pad_maximum_fusion.2), channel_id=1, source_target_pairs={{0,1},{1,2},{2,3},{3,4},{4,5},{5,6},{6,7},{7,8},{8,9},{9,10},{10,1... | collective-permute-start | bytes 1228808 | tf_op jit(solution)/shard_map/ppermute | solution.py:224
  82.6 10.4 %all-to-all-start = ((f32[8,8,384]{2,1,0:T(8,128)}), f32[8,8,384]{2,1,0:T(8,128)S(1)}, u32[]{:S(2)}, u32[]{:S(2)}) async-start(f32[8,8,384]{2,1,0:T(8,128)} %bitcast.167), calls=%async_computation | async-start | bytes 196608 | tf_op jit(solution)/shard_map/all_to_all | solution.py:598
  93.0 8.5 %collective-permute-start.6 = (f32[3,1,3072]{2,1,0:T(1,128)S(1)}, f32[3,1,3072]{2,1,0:T(1,128)S(1)}, u32[]{:S(2)}, u32[]{:S(2)}) collective-permute-start(f32[3,1,3072]{2,1,0:T(1,128)S(1)} %get-tuple-element.38), channel_id=1, source_target_pairs={{16,0},{32,16},{48,32},{64,48},{80,64},{96,80},{112,96},{1,112},{1... | collective-permute-start | bytes 110600 | tf_op jit(solution)/shard_map/ppermute | solution.py:482
  95.7 5.7 %collective-permute-start.5 = (f32[3,1,3072]{2,1,0:T(1,128)S(1)}, f32[3,1,3072]{2,1,0:T(1,128)S(1)}, u32[]{:S(2)}, u32[]{:S(2)}) collective-permute-start(f32[3,1,3072]{2,1,0:T(1,128)S(1)} %get-tuple-element.37), channel_id=1, source_target_pairs={{0,16},{16,32},{32,48},{48,64},{64,80},{80,96},{96,112},{112,1},{1... | collective-permute-start | bytes 110600 | tf_op jit(solution)/shard_map/ppermute | solution.py:485
  103.8 4.6 %collective-permute-start.7 = (f32[2]{0:T(128)S(1)}, f32[2]{0:T(128)S(1)}, u32[]{:S(2)}, u32[]{:S(2)}) collective-permute-start(f32[2]{0:T(128)S(1)} %pad_maximum_fusion.28), channel_id=1, source_target_pairs={{0,16},{16,0},{32,48},{48,32},{64,80},{80,64},{96,112},{112,96},{1... | collective-permute-start | bytes 32 | tf_op jit(solution)/shard_map/ppermute | solution.py:468
  103.9 40.7 %collective-permute-start.14 = (f32[1,1,3072]{2,1,0:T(1,128)S(1)}, f32[1,1,3072]{2,1,0:T(1,128)S(1)}, u32[]{:S(2)}, u32[]{:S(2)}) collective-permute-start(f32[1,1,3072]{2,1,0:T(1,128)S(1)} %get-tuple-element.49), channel_id=1, source_target_pairs={{0,16},{16,32},{32,48},{48,64},{64,80},{80,96},{96,112},{112,1},{1... | collective-permute-start | bytes 36872 | tf_op jit(solution)/shard_map/ppermute | solution.py:485
  106.5 38.2 %collective-permute-start.15 = (f32[1,1,3072]{2,1,0:T(1,128)S(1)}, f32[1,1,3072]{2,1,0:T(1,128)S(1)}, u32[]{:S(2)}, u32[]{:S(2)}) collective-permute-start(f32[1,1,3072]{2,1,0:T(1,128)S(1)} %get-tuple-element.50), channel_id=1, source_target_pairs={{16,0},{32,16},{48,32},{64,48},{80,64},{96,80},{112,96},{1,112},{1... | collective-permute-start | bytes 36872 | tf_op jit(solution)/shard_map/ppermute | solution.py:482
  109.7 2.4 collective-permute-start.8
  113.5 6.2 %collective-permute-start.9 = (f32[2]{0:T(128)S(1)}, f32[2]{0:T(128)S(1)}, u32[]{:S(2)}, u32[]{:S(2)}) collective-permute-start(f32[2]{0:T(128)S(1)} %fusion.50), channel_id=1, source_target_pairs={{0,64},{16,80},{32,96},{48,112},{64,0},{80,16},{96,32},{112,48},{1... | collective-permute-start | bytes 32 | tf_op jit(solution)/shard_map/ppermute | solution.py:468
  119.8 2.6 %collective-permute-start.10 = (f32[2]{0:T(128)S(1)}, f32[2]{0:T(128)S(1)}, u32[]{:S(2)}, u32[]{:S(2)}) collective-permute-start(f32[2]{0:T(128)S(1)} %add.184), channel_id=1, source_target_pairs={{0,1},{1,0},{2,3},{3,2},{4,5},{5,4},{6,7},{7,6},{8,9},{9,8},{10,11... | collective-permute-start | bytes 32 | tf_op jit(solution)/shard_map/ppermute | solution.py:468
  122.4 10.6 %collective-permute-start.11 = (f32[2]{0:T(128)S(1)}, f32[2]{0:T(128)S(1)}, u32[]{:S(2)}, u32[]{:S(2)}) collective-permute-start(f32[2]{0:T(128)S(1)} %add.185), channel_id=1, source_target_pairs={{0,2},{1,3},{2,0},{3,1},{4,6},{5,7},{6,4},{7,5},{8,10},{9,11},{10,... | collective-permute-start | bytes 32 | tf_op jit(solution)/shard_map/ppermute | solution.py:468
  133.0 3.5 %collective-permute-start.12 = (f32[2]{0:T(128)S(1)}, f32[2]{0:T(128)S(1)}, u32[]{:S(2)}, u32[]{:S(2)}) collective-permute-start(f32[2]{0:T(128)S(1)} %add.186), channel_id=1, source_target_pairs={{0,4},{1,5},{2,6},{3,7},{4,0},{5,1},{6,2},{7,3},{8,12},{9,13},{10,... | collective-permute-start | bytes 32 | tf_op jit(solution)/shard_map/ppermute | solution.py:468
  136.5 4.0 %collective-permute-start.13 = (f32[2]{0:T(128)S(1)}, f32[2]{0:T(128)S(1)}, u32[]{:S(2)}, u32[]{:S(2)}) collective-permute-start(f32[2]{0:T(128)S(1)} %add.187), channel_id=1, source_target_pairs={{0,8},{1,9},{2,10},{3,11},{4,12},{5,13},{6,14},{7,15},{8,0},{9,1},... | collective-permute-start | bytes 32 | tf_op jit(solution)/shard_map/ppermute | solution.py:468
  147.6 16.2 %collective-permute-start.16 = (f32[3]{0:T(128)S(1)}, f32[3]{0:T(128)S(1)}, u32[]{:S(2)}, u32[]{:S(2)}) collective-permute-start(f32[3]{0:T(128)S(1)} %pad_maximum_fusion.29), channel_id=1, source_target_pairs={{0,16},{16,0},{32,48},{48,32},{64,80},{80,64},{96,112},{112,96},{1... | collective-permute-start | bytes 44 | tf_op jit(solution)/shard_map/ppermute | solution.py:468
  159.4 34.2 %collective-permute-start.23 = (f32[1,1,3072]{2,1,0:T(1,128)S(1)}, f32[1,1,3072]{2,1,0:T(1,128)S(1)}, u32[]{:S(2)}, u32[]{:S(2)}) collective-permute-start(f32[1,1,3072]{2,1,0:T(1,128)S(1)} %get-tuple-element.47), channel_id=1, source_target_pairs={{0,16},{16,32},{32,48},{48,64},{64,80},{80,96},{96,112},{112,1},{1... | collective-permute-start | bytes 36872 | tf_op jit(solution)/shard_map/ppermute | solution.py:485
  161.4 32.3 %collective-permute-start.24 = (f32[1,1,3072]{2,1,0:T(1,128)S(1)}, f32[1,1,3072]{2,1,0:T(1,128)S(1)}, u32[]{:S(2)}, u32[]{:S(2)}) collective-permute-start(f32[1,1,3072]{2,1,0:T(1,128)S(1)} %get-tuple-element.48), channel_id=1, source_target_pairs={{16,0},{32,16},{48,32},{64,48},{80,64},{96,80},{112,96},{1,112},{1... | collective-permute-start | bytes 36872 | tf_op jit(solution)/shard_map/ppermute | solution.py:482
  165.7 2.4 collective-permute-start.17
  170.0 3.9 %collective-permute-start.18 = (f32[3]{0:T(128)S(1)}, f32[3]{0:T(128)S(1)}, u32[]{:S(2)}, u32[]{:S(2)}) collective-permute-start(f32[3]{0:T(128)S(1)} %fusion.49), channel_id=1, source_target_pairs={{0,64},{16,80},{32,96},{48,112},{64,0},{80,16},{96,32},{112,48},{1... | collective-permute-start | bytes 44 | tf_op jit(solution)/shard_map/ppermute | solution.py:468
  173.9 2.4 collective-permute-start.19
  176.4 3.9 %collective-permute-start.20 = (f32[3]{0:T(128)S(1)}, f32[3]{0:T(128)S(1)}, u32[]{:S(2)}, u32[]{:S(2)}) collective-permute-start(f32[3]{0:T(128)S(1)} %add.198), channel_id=1, source_target_pairs={{0,2},{1,3},{2,0},{3,1},{4,6},{5,7},{6,4},{7,5},{8,10},{9,11},{10,... | collective-permute-start | bytes 44 | tf_op jit(solution)/shard_map/ppermute | solution.py:468
  180.3 2.8 %collective-permute-start.21 = (f32[3]{0:T(128)S(1)}, f32[3]{0:T(128)S(1)}, u32[]{:S(2)}, u32[]{:S(2)}) collective-permute-start(f32[3]{0:T(128)S(1)} %add.199), channel_id=1, source_target_pairs={{0,4},{1,5},{2,6},{3,7},{4,0},{5,1},{6,2},{7,3},{8,12},{9,13},{10,... | collective-permute-start | bytes 44 | tf_op jit(solution)/shard_map/ppermute | solution.py:468
  183.1 4.0 %collective-permute-start.22 = (f32[3]{0:T(128)S(1)}, f32[3]{0:T(128)S(1)}, u32[]{:S(2)}, u32[]{:S(2)}) collective-permute-start(f32[3]{0:T(128)S(1)} %add.200), channel_id=1, source_target_pairs={{0,8},{1,9},{2,10},{3,11},{4,12},{5,13},{6,14},{7,15},{8,0},{9,1},... | collective-permute-start | bytes 44 | tf_op jit(solution)/shard_map/ppermute | solution.py:468
  196.7 12.7 %collective-permute-start.25 = (f32[3]{0:T(128)S(1)}, f32[3]{0:T(128)S(1)}, u32[]{:S(2)}, u32[]{:S(2)}) collective-permute-start(f32[3]{0:T(128)S(1)} %pad_maximum_fusion.30), channel_id=1, source_target_pairs={{0,16},{16,0},{32,48},{48,32},{64,80},{80,64},{96,112},{112,96},{1... | collective-permute-start | bytes 44 | tf_op jit(solution)/shard_map/ppermute | solution.py:468
  211.5 2.4 collective-permute-start.26
  215.9 3.9 %collective-permute-start.27 = (f32[3]{0:T(128)S(1)}, f32[3]{0:T(128)S(1)}, u32[]{:S(2)}, u32[]{:S(2)}) collective-permute-start(f32[3]{0:T(128)S(1)} %fusion.48), channel_id=1, source_target_pairs={{0,64},{16,80},{32,96},{48,112},{64,0},{80,16},{96,32},{112,48},{1... | collective-permute-start | bytes 44 | tf_op jit(solution)/shard_map/ppermute | solution.py:468
  219.8 2.4 collective-permute-start.28
  222.3 3.9 %collective-permute-start.29 = (f32[3]{0:T(128)S(1)}, f32[3]{0:T(128)S(1)}, u32[]{:S(2)}, u32[]{:S(2)}) collective-permute-start(f32[3]{0:T(128)S(1)} %add.218), channel_id=1, source_target_pairs={{0,2},{1,3},{2,0},{3,1},{4,6},{5,7},{6,4},{7,5},{8,10},{9,11},{10,... | collective-permute-start | bytes 44 | tf_op jit(solution)/shard_map/ppermute | solution.py:468
  226.2 2.6 %collective-permute-start.30 = (f32[3]{0:T(128)S(1)}, f32[3]{0:T(128)S(1)}, u32[]{:S(2)}, u32[]{:S(2)}) collective-permute-start(f32[3]{0:T(128)S(1)} %add.219), channel_id=1, source_target_pairs={{0,4},{1,5},{2,6},{3,7},{4,0},{5,1},{6,2},{7,3},{8,12},{9,13},{10,... | collective-permute-start | bytes 44 | tf_op jit(solution)/shard_map/ppermute | solution.py:468
  228.8 4.0 %collective-permute-start.31 = (f32[3]{0:T(128)S(1)}, f32[3]{0:T(128)S(1)}, u32[]{:S(2)}, u32[]{:S(2)}) collective-permute-start(f32[3]{0:T(128)S(1)} %add.220), channel_id=1, source_target_pairs={{0,8},{1,9},{2,10},{3,11},{4,12},{5,13},{6,14},{7,15},{8,0},{9,1},... | collective-permute-start | bytes 44 | tf_op jit(solution)/shard_map/ppermute | solution.py:468

commit v8 on v5

--- a/solution.py
+++ b/solution.py
@@ -335,7 +335,7 @@
 
 def vertical_mix(values, wet_mask, diffusivity, forcing):
     tracer_count, level_count, row_count, col_count = values.shape
-    rows = 16 if row_count % 16 == 0 else row_count
+    rows = 32 if row_count % 32 == 0 else row_count
     return pl.pallas_call(
         mix_kernel,
         grid=(row_count // rows,),

time: 253 us -> 252 us (level)
  no operation moved by 1% of the time
where the time goes in v8:
time: 252 us; the launch traced here: 251 us
  starting transfers between devices  95.1 us (38%)
  waiting for transfers between devices  44.5 us (18%)
  other arithmetic  32.1 us (13%)
  local copies, waits for them, and re-layouts  29.7 us (12%)
  Pallas kernels  25.8 us (10%)
  blocking collectives  14.3 us (6%)
  between operations  9.33 us (4%)
    ppermute x21, starting transfers between devices, butterfly_sum(): lax.ppermute(value, axis, [(i, i ^ bit) for i in range(count)])  59.7 us
    ppermute x21, waiting for transfers between devices, butterfly_sum(): lax.ppermute(value, axis, [(i, i ^ bit) for i in range(count)])  33.2 us
    pallas_call x1, Pallas kernels, assembling_call(): pl.pallas_call(assembling_kernel, grid=(level_count,), in_specs=[pl.Block...  20.7 us
    all_to_all x1, blocking collectives, shards(): lax.all_to_all(strip_solution, 'lon', split_axis=1, concat_axis=0, tiled=...  14.3 us
    add x21, other arithmetic, butterfly_sum(): value + lax.ppermute(value, axis, [(i, i ^ bit) for i in range(count)])  10.5 us
    ppermute x3, starting transfers between devices, neighbour_rows(): lax.ppermute(values[:, -1:, :], axes, [(device(s - 1), device(s)) for s i...  7.32 us
    ppermute x3, starting transfers between devices, neighbour_rows(): lax.ppermute(values[:, 0:1, :], axes, [(device(s + 1), device(s)) for s i...  7.05 us
    rev x3, local copies, waits for them, and re-layouts, strip_assemble(): jnp.flip(surface_field[-1:, :], axis=1)  6.33 us
  transfers between devices with their start and end apart: 34, of which 22 were waited for; matrix products, arithmetic and copies ran while one was open for 11% of the time, Pallas kernels for 0%

profile of v8, /device:TPU:1, one launch (start us, length us, event | category | flops | bytes accessed | tf_op | source)
XLA Modules:
  0.0 250.9 jit_solution(16600615259367569109)
XLA Ops:
  9.0 2.2 fusion.35
  20.3 1.7 fusion.37
  22.1 3.1 %copy.51 = f32[5,20,64,2]{3,2,1,0:T(8,128)} copy(f32[5,20,64,2]{2,3,1,0:T(2,128)} %collective-permute-done) | data formatting | bytes 102400 | tf_op jit(solution)/shard_map/ppermute | solution.py:200
  25.2 2.3 copy.52
  27.6 3.8 %pad_maximum_fusion.cols_ref = f32[5,20,64,128]{3,2,1,0:T(8,128)S(1)} fusion(f32[5,20,64,2]{3,2,1,0:T(8,128)} %copy.52, f32[5,20,64,2]{3,2,1,0:T(8,128)} %copy.51, f32[128]{0:T(128)S(1)} %pad.74.clone), kind=kLoop, calls=%fused_computation | loop fusion | flops 1638400 | bytes 3379712 | tf_op jit(solution)/shard_map/concatenate | solution.py:210
  31.7 1.8 collective-permute-start.2
  36.0 5.6 %all-to-all-start.1 = ((f32[2,64,384]{2,0,1:T(2,128)}), f32[2,64,384]{2,0,1:T(2,128)S(1)}, u32[]{:S(2)}, u32[]{:S(2)}) async-start(f32[2,64,384]{2,0,1:T(2,128)} %copy.53), calls=%async_computation.1 | async-start | bytes 393216 | tf_op jit(solution)/shard_map/all_to_all | solution.py:582
  41.5 4.3 %collective-permute-start.4 = (f32[5,20,2,512]{3,2,1,0:T(2,128)S(1)}, f32[5,20,2,512]{3,2,1,0:T(2,128)S(1)}, u32[]{:S(2)}, u32[]{:S(2)}) collective-permute-start(f32[5,20,2,512]{3,2,1,0:T(2,128)S(1)} %pad_maximum_fusion.2), channel_id=1, source_target_pairs={{0,1},{1,2},{2,3},{3,4},{4,5},{5,6},{6,7},{7,8},{8,9},{9,10},{10,1... | collective-permute-start | bytes 1228808 | tf_op jit(solution)/shard_map/ppermute | solution.py:222
  49.6 4.8 %collective-permute-done.4 = f32[5,20,2,512]{3,2,1,0:T(2,128)S(1)} collective-permute-done((f32[5,20,2,512]{3,2,1,0:T(2,128)S(1)}, f32[5,20,2,512]{3,2,1,0:T(2,128)S(1)}, u32[]{:S(2)}, u32[]{:S(2)}) %collective-permute-start.4) | collective-permute-done | bytes 409632 | tf_op jit(solution)/shard_map/ppermute | solution.py:222
  56.0 20.7 %shard_map.104.values_ref = f32[2,20,64,384]{3,2,1,0:T(8,128)} custom-call(f32[2,20,64,384]{3,2,1,0:T(8,128)} %tracer_ref.1, f32[20,64,384]{2,1,0:T(8,128)} %copy-done, bf16[20,64,384]{2,1,0:T(8,128)(2,1)} %east_ref.1, bf16[20,64,384]{2,1,0:T(8,128)(2,1)} %north_ref.1, f32[5,20,64,128]{3,2,1,0:T(8,128)} %copy-done.1, ...), custom_call_target="tpu_custom_call" | custom-call | tf_op jit(solution)/shard_map/pallas_call | solution.py:239
  76.8 5.1 %shard_map.105 = (f32[2,20,64,384]{3,2,1,0:T(8,128)}, f32[64,384]{1,0:T(8,128)}) custom-call(f32[2,20,64,384]{3,2,1,0:T(8,128)} %shard_map.104.values_ref, f32[20,64,384]{2,1,0:T(8,128)} %copy-done, bf16[20,64,384]{2,1,0:T(8,128)(2,1)} %diff_ref.1, f32[64,384]{1,0:T(8,128)} %forcing_ref.1), custom_call_target="tpu_custom_call" | custom-call | tf_op jit(solution)/shard_map/pallas_call | solution.py:339
  81.8 5.4 %all-to-all-start = ((f32[8,8,384]{2,1,0:T(8,128)}), f32[8,8,384]{2,1,0:T(8,128)S(1)}, u32[]{:S(2)}, u32[]{:S(2)}) async-start(f32[8,8,384]{2,1,0:T(8,128)} %bitcast.167), calls=%async_computation | async-start | bytes 196608 | tf_op jit(solution)/shard_map/all_to_all | solution.py:596
  87.3 5.0 %all-to-all-done = f32[8,8,384]{2,1,0:T(8,128)S(1)} async-done(((f32[8,8,384]{2,1,0:T(8,128)}), f32[8,8,384]{2,1,0:T(8,128)S(1)}, u32[]{:S(2)}, u32[]{:S(2)}) %all-to-all-start) | async-done | bytes 98336 | tf_op jit(solution)/shard_map/all_to_all | solution.py:596
  92.3 2.7 %collective-permute-start.6 = (f32[3,1,3072]{2,1,0:T(1,128)S(1)}, f32[3,1,3072]{2,1,0:T(1,128)S(1)}, u32[]{:S(2)}, u32[]{:S(2)}) collective-permute-start(f32[3,1,3072]{2,1,0:T(1,128)S(1)} %get-tuple-element.38), channel_id=1, source_target_pairs={{16,0},{32,16},{48,32},{64,48},{80,64},{96,80},{112,96},{1,112},{1... | collective-permute-start | bytes 110600 | tf_op jit(solution)/shard_map/ppermute | solution.py:480
  95.0 2.8 %collective-permute-start.5 = (f32[3,1,3072]{2,1,0:T(1,128)S(1)}, f32[3,1,3072]{2,1,0:T(1,128)S(1)}, u32[]{:S(2)}, u32[]{:S(2)}) collective-permute-start(f32[3,1,3072]{2,1,0:T(1,128)S(1)} %get-tuple-element.37), channel_id=1, source_target_pairs={{0,16},{16,32},{32,48},{48,64},{64,80},{80,96},{96,112},{112,1},{1... | collective-permute-start | bytes 110600 | tf_op jit(solution)/shard_map/ppermute | solution.py:483
  98.6 2.1 rev.12
  103.1 2.6 %collective-permute-start.14 = (f32[1,1,3072]{2,1,0:T(1,128)S(1)}, f32[1,1,3072]{2,1,0:T(1,128)S(1)}, u32[]{:S(2)}, u32[]{:S(2)}) collective-permute-start(f32[1,1,3072]{2,1,0:T(1,128)S(1)} %get-tuple-element.49), channel_id=1, source_target_pairs={{0,16},{16,32},{32,48},{48,64},{64,80},{80,96},{96,112},{112,1},{1... | collective-permute-start | bytes 36872 | tf_op jit(solution)/shard_map/ppermute | solution.py:483
  105.7 1.9 collective-permute-start.15
  109.5 2.0 collective-permute-done.8
  112.8 5.3 %collective-permute-start.9 = (f32[2]{0:T(128)S(1)}, f32[2]{0:T(128)S(1)}, u32[]{:S(2)}, u32[]{:S(2)}) collective-permute-start(f32[2]{0:T(128)S(1)} %fusion.50), channel_id=1, source_target_pairs={{0,64},{16,80},{32,96},{48,112},{64,0},{80,16},{96,32},{112,48},{1... | collective-permute-start | bytes 32 | tf_op jit(solution)/shard_map/ppermute | solution.py:466
  119.0 1.6 collective-permute-start.10
  121.6 9.6 %collective-permute-start.11 = (f32[2]{0:T(128)S(1)}, f32[2]{0:T(128)S(1)}, u32[]{:S(2)}, u32[]{:S(2)}) collective-permute-start(f32[2]{0:T(128)S(1)} %add.185), channel_id=1, source_target_pairs={{0,2},{1,3},{2,0},{3,1},{4,6},{5,7},{6,4},{7,5},{8,10},{9,11},{10,... | collective-permute-start | bytes 32 | tf_op jit(solution)/shard_map/ppermute | solution.py:466
  132.2 2.6 %collective-permute-start.12 = (f32[2]{0:T(128)S(1)}, f32[2]{0:T(128)S(1)}, u32[]{:S(2)}, u32[]{:S(2)}) collective-permute-start(f32[2]{0:T(128)S(1)} %add.186), channel_id=1, source_target_pairs={{0,4},{1,5},{2,6},{3,7},{4,0},{5,1},{6,2},{7,3},{8,12},{9,13},{10,... | collective-permute-start | bytes 32 | tf_op jit(solution)/shard_map/ppermute | solution.py:466
  135.8 3.1 %collective-permute-start.13 = (f32[2]{0:T(128)S(1)}, f32[2]{0:T(128)S(1)}, u32[]{:S(2)}, u32[]{:S(2)}) collective-permute-start(f32[2]{0:T(128)S(1)} %add.187), channel_id=1, source_target_pairs={{0,8},{1,9},{2,10},{3,11},{4,12},{5,13},{6,14},{7,15},{8,0},{9,1},... | collective-permute-start | bytes 32 | tf_op jit(solution)/shard_map/ppermute | solution.py:466
  141.8 2.1 rev.13
  145.0 1.9 pad_maximum_fusion.29
  146.9 11.8 %collective-permute-start.16 = (f32[3]{0:T(128)S(1)}, f32[3]{0:T(128)S(1)}, u32[]{:S(2)}, u32[]{:S(2)}) collective-permute-start(f32[3]{0:T(128)S(1)} %pad_maximum_fusion.29), channel_id=1, source_target_pairs={{0,16},{16,0},{32,48},{48,32},{64,80},{80,64},{96,112},{112,96},{1... | collective-permute-start | bytes 44 | tf_op jit(solution)/shard_map/ppermute | solution.py:466
  158.7 1.9 collective-permute-start.23
  160.6 2.4 collective-permute-start.24
  163.1 1.9 fusion.46
  165.0 2.4 collective-permute-done.17
  167.4 1.9 fusion.49
  170.5 2.7 %collective-permute-done.18 = f32[3]{0:T(128)S(1)} collective-permute-done((f32[3]{0:T(128)S(1)}, f32[3]{0:T(128)S(1)}, u32[]{:S(2)}, u32[]{:S(2)}) %collective-permute-start.18) | collective-permute-done | bytes 44 | tf_op jit(solution)/shard_map/ppermute | solution.py:466
  173.2 2.4 collective-permute-done.19
  175.6 2.3 collective-permute-start.20
  179.6 1.8 collective-permute-start.21
  182.3 3.1 %collective-permute-start.22 = (f32[3]{0:T(128)S(1)}, f32[3]{0:T(128)S(1)}, u32[]{:S(2)}, u32[]{:S(2)}) collective-permute-start(f32[3]{0:T(128)S(1)} %add.200), channel_id=1, source_target_pairs={{0,8},{1,9},{2,10},{3,11},{4,12},{5,13},{6,14},{7,15},{8,0},{9,1},... | collective-permute-start | bytes 44 | tf_op jit(solution)/shard_map/ppermute | solution.py:466
  190.8 2.1 rev.14
  194.0 2.0 pad_maximum_fusion.30
  196.0 11.9 %collective-permute-start.25 = (f32[3]{0:T(128)S(1)}, f32[3]{0:T(128)S(1)}, u32[]{:S(2)}, u32[]{:S(2)}) collective-permute-start(f32[3]{0:T(128)S(1)} %pad_maximum_fusion.30), channel_id=1, source_target_pairs={{0,16},{16,0},{32,48},{48,32},{64,80},{80,64},{96,112},{112,96},{1... | collective-permute-start | bytes 44 | tf_op jit(solution)/shard_map/ppermute | solution.py:466
  208.7 2.0 fusion.45
  210.8 2.4 collective-permute-done.26
  213.2 2.0 fusion.48
  215.2 3.9 %collective-permute-done.27 = f32[3]{0:T(128)S(1)} collective-permute-done((f32[3]{0:T(128)S(1)}, f32[3]{0:T(128)S(1)}, u32[]{:S(2)}, u32[]{:S(2)}) %collective-permute-start.27) | collective-permute-done | bytes 44 | tf_op jit(solution)/shard_map/ppermute | solution.py:466
  219.1 2.4 collective-permute-done.28
  221.5 3.9 %collective-permute-done.29 = f32[3]{0:T(128)S(1)} collective-permute-done((f32[3]{0:T(128)S(1)}, f32[3]{0:T(128)S(1)}, u32[]{:S(2)}, u32[]{:S(2)}) %collective-permute-start.29) | collective-permute-done | bytes 44 | tf_op jit(solution)/shard_map/ppermute | solution.py:466
  228.1 3.1 %collective-permute-start.31 = (f32[3]{0:T(128)S(1)}, f32[3]{0:T(128)S(1)}, u32[]{:S(2)}, u32[]{:S(2)}) collective-permute-start(f32[3]{0:T(128)S(1)} %add.220), channel_id=1, source_target_pairs={{0,8},{1,9},{2,10},{3,11},{4,12},{5,13},{6,14},{7,15},{8,0},{9,1},... | collective-permute-start | bytes 44 | tf_op jit(solution)/shard_map/ppermute | solution.py:466
  235.9 14.3 %all_to_all.53 = f32[8,8,384]{2,0,1:T(8,128)S(1)} all-to-all(f32[8,8,384]{2,0,1:T(8,128)S(1)} %bitcast.165), channel_id=1, replica_groups=mesh['lon'=8,'lat'=16] {'lon'}, dimensions={1} | all-to-all | bytes 196608 | tf_op jit(solution)/shard_map/all_to_all | solution.py:598
  (141 shorter events, 50.7 us)
Async XLA Ops:
  2.7 1.3 copy-start.2
  4.0 1.2 copy-start.3
  4.2 2.9 %copy-start.4 = (bf16[20,64,384]{2,1,0:T(8,128)(2,1)S(1)}, bf16[20,64,384]{2,1,0:T(8,128)(2,1)}, u32[]{:S(2)}) copy-start(bf16[20,64,384]{2,1,0:T(8,128)(2,1)} %north_ref.1) | copy-start | bytes 2949124
  11.7 3.9 %copy-start.5 = (f32[1,20,64,2]{3,2,1,0:T(8,128)S(1)}, f32[1,20,64,2]{3,2,1,0:T(8,128)}, u32[]{:S(2)}) copy-start(f32[1,20,64,2]{3,2,1,0:T(8,128)} %get-tuple-element.36) | copy-start | bytes 30724
  12.6 9.5 %collective-permute-start = (f32[5,20,64,2]{2,3,1,0:T(2,128)S(1)}, f32[5,20,64,2]{2,3,1,0:T(2,128)}, u32[]{:S(2)}, u32[]{:S(2)}) collective-permute-start(f32[5,20,64,2]{2,3,1,0:T(2,128)S(1)} %pad_maximum_fusion.17), channel_id=1, source_target_pairs={{0,112},{16,0},{32,16},{48,32},{64,48},{80,64},{96,80},{112,96},{1... | collective-permute-start | bytes 153608 | tf_op jit(solution)/shard_map/ppermute | solution.py:200
  14.2 5.9 %copy-start.6 = (s32[64,384]{1,0:T(8,128)S(1)}, s32[64,384]{1,0:T(8,128)}, u32[]{:S(2)}) copy-start(s32[64,384]{1,0:T(8,128)} %param.13) | copy-start | bytes 294916
  16.4 8.8 %collective-permute-start.1 = (f32[5,20,64,2]{2,3,1,0:T(2,128)S(1)}, f32[5,20,64,2]{2,3,1,0:T(2,128)S(1)}, u32[]{:S(2)}, u32[]{:S(2)}) collective-permute-start(f32[5,20,64,2]{2,3,1,0:T(2,128)S(1)} %pad_maximum_fusion.18), channel_id=1, source_target_pairs={{0,16},{16,32},{32,48},{48,64},{64,80},{80,96},{96,112},{112,0},{1... | collective-permute-start | bytes 153608 | tf_op jit(solution)/shard_map/ppermute | solution.py:205
  20.3 7.3 %copy-start = (f32[20,64,384]{2,1,0:T(8,128)}, f32[20,64,384]{2,1,0:T(8,128)S(1)}, u32[]{:S(2)}) copy-start(f32[20,64,384]{2,1,0:T(8,128)S(1)} %fusion.wet_ref) | copy-start | bytes 5898244
  31.4 3.7 %copy-start.1 = (f32[5,20,64,128]{3,2,1,0:T(8,128)}, f32[5,20,64,128]{3,2,1,0:T(8,128)S(1)}, u32[]{:S(2)}) copy-start(f32[5,20,64,128]{3,2,1,0:T(8,128)S(1)} %pad_maximum_fusion.cols_ref) | copy-start | bytes 9830404
  31.4 3.6 %copy-start.7 = (f32[64,384]{1,0:T(8,128)S(1)}, f32[64,384]{1,0:T(8,128)}, u32[]{:S(2)}) copy-start(f32[64,384]{1,0:T(8,128)} %param.16) | copy-start | bytes 294916
  31.4 3.6 %slice-start = ((f32[20,64,384]{2,1,0:T(8,128)}), f32[1,64,384]{2,1,0:T(8,128)S(1)}, s32[]{:S(2)}) async-start(f32[20,64,384]{2,1,0:T(8,128)} %copy-done), calls=%async_computation.3 | async-start | bytes 196608 | tf_op jit(solution)/shard_map/slice | solution.py:583
  31.7 15.7 %collective-permute-start.2 = (f32[5,20,2,512]{3,2,1,0:T(2,128)S(1)}, f32[5,20,2,512]{3,2,1,0:T(2,128)S(1)}, u32[]{:S(2)}, u32[]{:S(2)}) collective-permute-start(f32[5,20,2,512]{3,2,1,0:T(2,128)S(1)} %pad_maximum_fusion.2), channel_id=1, source_target_pairs={{0,112},{16,96},{32,80},{48,64},{64,48},{80,32},{96,16},{112,0},{1... | collective-permute-start | bytes 1228808 | tf_op jit(solution)/shard_map/ppermute | solution.py:223
  33.6 15.7 %copy-start.8 = (f32[5]{0:T(128)S(1)}, f32[5]{0:T(128)}, u32[]{:S(2)}) copy-start(f32[5]{0:T(128)} %constant.10.clone) | copy-start | bytes 64
  33.8 15.5 %collective-permute-start.3 = (f32[5,20,2,512]{3,2,1,0:T(2,128)S(1)}, f32[5,20,2,512]{3,2,1,0:T(2,128)S(1)}, u32[]{:S(2)}, u32[]{:S(2)}) collective-permute-start(f32[5,20,2,512]{3,2,1,0:T(2,128)S(1)} %pad_maximum_fusion.3), channel_id=1, source_target_pairs={{1,0},{2,1},{3,2},{4,3},{5,4},{6,5},{7,6},{8,7},{9,8},{10,9},{11,1... | collective-permute-start | bytes 1228808 | tf_op jit(solution)/shard_map/ppermute | solution.py:221
  36.0 11.5 %all-to-all-start.1 = ((f32[2,64,384]{2,0,1:T(2,128)}), f32[2,64,384]{2,0,1:T(2,128)S(1)}, u32[]{:S(2)}, u32[]{:S(2)}) async-start(f32[2,64,384]{2,0,1:T(2,128)} %copy.53), calls=%async_computation.1 | async-start | bytes 393216 | tf_op jit(solution)/shard_map/all_to_all | solution.py:582
  41.5 12.9 %collective-permute-start.4 = (f32[5,20,2,512]{3,2,1,0:T(2,128)S(1)}, f32[5,20,2,512]{3,2,1,0:T(2,128)S(1)}, u32[]{:S(2)}, u32[]{:S(2)}) collective-permute-start(f32[5,20,2,512]{3,2,1,0:T(2,128)S(1)} %pad_maximum_fusion.2), channel_id=1, source_target_pairs={{0,1},{1,2},{2,3},{3,4},{4,5},{5,6},{6,7},{7,8},{8,9},{9,10},{10,1... | collective-permute-start | bytes 1228808 | tf_op jit(solution)/shard_map/ppermute | solution.py:222
  81.8 10.4 %all-to-all-start = ((f32[8,8,384]{2,1,0:T(8,128)}), f32[8,8,384]{2,1,0:T(8,128)S(1)}, u32[]{:S(2)}, u32[]{:S(2)}) async-start(f32[8,8,384]{2,1,0:T(8,128)} %bitcast.167), calls=%async_computation | async-start | bytes 196608 | tf_op jit(solution)/shard_map/all_to_all | solution.py:596
  92.3 8.5 %collective-permute-start.6 = (f32[3,1,3072]{2,1,0:T(1,128)S(1)}, f32[3,1,3072]{2,1,0:T(1,128)S(1)}, u32[]{:S(2)}, u32[]{:S(2)}) collective-permute-start(f32[3,1,3072]{2,1,0:T(1,128)S(1)} %get-tuple-element.38), channel_id=1, source_target_pairs={{16,0},{32,16},{48,32},{64,48},{80,64},{96,80},{112,96},{1,112},{1... | collective-permute-start | bytes 110600 | tf_op jit(solution)/shard_map/ppermute | solution.py:480
  95.0 5.7 %collective-permute-start.5 = (f32[3,1,3072]{2,1,0:T(1,128)S(1)}, f32[3,1,3072]{2,1,0:T(1,128)S(1)}, u32[]{:S(2)}, u32[]{:S(2)}) collective-permute-start(f32[3,1,3072]{2,1,0:T(1,128)S(1)} %get-tuple-element.37), channel_id=1, source_target_pairs={{0,16},{16,32},{32,48},{48,64},{64,80},{80,96},{96,112},{112,1},{1... | collective-permute-start | bytes 110600 | tf_op jit(solution)/shard_map/ppermute | solution.py:483
  103.1 4.6 %collective-permute-start.7 = (f32[2]{0:T(128)S(1)}, f32[2]{0:T(128)S(1)}, u32[]{:S(2)}, u32[]{:S(2)}) collective-permute-start(f32[2]{0:T(128)S(1)} %pad_maximum_fusion.28), channel_id=1, source_target_pairs={{0,16},{16,0},{32,48},{48,32},{64,80},{80,64},{96,112},{112,96},{1... | collective-permute-start | bytes 32 | tf_op jit(solution)/shard_map/ppermute | solution.py:466
  103.1 40.7 %collective-permute-start.14 = (f32[1,1,3072]{2,1,0:T(1,128)S(1)}, f32[1,1,3072]{2,1,0:T(1,128)S(1)}, u32[]{:S(2)}, u32[]{:S(2)}) collective-permute-start(f32[1,1,3072]{2,1,0:T(1,128)S(1)} %get-tuple-element.49), channel_id=1, source_target_pairs={{0,16},{16,32},{32,48},{48,64},{64,80},{80,96},{96,112},{112,1},{1... | collective-permute-start | bytes 36872 | tf_op jit(solution)/shard_map/ppermute | solution.py:483
  105.7 38.2 %collective-permute-start.15 = (f32[1,1,3072]{2,1,0:T(1,128)S(1)}, f32[1,1,3072]{2,1,0:T(1,128)S(1)}, u32[]{:S(2)}, u32[]{:S(2)}) collective-permute-start(f32[1,1,3072]{2,1,0:T(1,128)S(1)} %get-tuple-element.50), channel_id=1, source_target_pairs={{16,0},{32,16},{48,32},{64,48},{80,64},{96,80},{112,96},{1,112},{1... | collective-permute-start | bytes 36872 | tf_op jit(solution)/shard_map/ppermute | solution.py:480
  109.0 2.4 collective-permute-start.8
  112.8 6.2 %collective-permute-start.9 = (f32[2]{0:T(128)S(1)}, f32[2]{0:T(128)S(1)}, u32[]{:S(2)}, u32[]{:S(2)}) collective-permute-start(f32[2]{0:T(128)S(1)} %fusion.50), channel_id=1, source_target_pairs={{0,64},{16,80},{32,96},{48,112},{64,0},{80,16},{96,32},{112,48},{1... | collective-permute-start | bytes 32 | tf_op jit(solution)/shard_map/ppermute | solution.py:466
  119.0 2.6 %collective-permute-start.10 = (f32[2]{0:T(128)S(1)}, f32[2]{0:T(128)S(1)}, u32[]{:S(2)}, u32[]{:S(2)}) collective-permute-start(f32[2]{0:T(128)S(1)} %add.184), channel_id=1, source_target_pairs={{0,1},{1,0},{2,3},{3,2},{4,5},{5,4},{6,7},{7,6},{8,9},{9,8},{10,11... | collective-permute-start | bytes 32 | tf_op jit(solution)/shard_map/ppermute | solution.py:466
  121.6 10.6 %collective-permute-start.11 = (f32[2]{0:T(128)S(1)}, f32[2]{0:T(128)S(1)}, u32[]{:S(2)}, u32[]{:S(2)}) collective-permute-start(f32[2]{0:T(128)S(1)} %add.185), channel_id=1, source_target_pairs={{0,2},{1,3},{2,0},{3,1},{4,6},{5,7},{6,4},{7,5},{8,10},{9,11},{10,... | collective-permute-start | bytes 32 | tf_op jit(solution)/shard_map/ppermute | solution.py:466
  132.2 3.5 %collective-permute-start.12 = (f32[2]{0:T(128)S(1)}, f32[2]{0:T(128)S(1)}, u32[]{:S(2)}, u32[]{:S(2)}) collective-permute-start(f32[2]{0:T(128)S(1)} %add.186), channel_id=1, source_target_pairs={{0,4},{1,5},{2,6},{3,7},{4,0},{5,1},{6,2},{7,3},{8,12},{9,13},{10,... | collective-permute-start | bytes 32 | tf_op jit(solution)/shard_map/ppermute | solution.py:466
  135.8 4.0 %collective-permute-start.13 = (f32[2]{0:T(128)S(1)}, f32[2]{0:T(128)S(1)}, u32[]{:S(2)}, u32[]{:S(2)}) collective-permute-start(f32[2]{0:T(128)S(1)} %add.187), channel_id=1, source_target_pairs={{0,8},{1,9},{2,10},{3,11},{4,12},{5,13},{6,14},{7,15},{8,0},{9,1},... | collective-permute-start | bytes 32 | tf_op jit(solution)/shard_map/ppermute | solution.py:466
  146.9 16.2 %collective-permute-start.16 = (f32[3]{0:T(128)S(1)}, f32[3]{0:T(128)S(1)}, u32[]{:S(2)}, u32[]{:S(2)}) collective-permute-start(f32[3]{0:T(128)S(1)} %pad_maximum_fusion.29), channel_id=1, source_target_pairs={{0,16},{16,0},{32,48},{48,32},{64,80},{80,64},{96,112},{112,96},{1... | collective-permute-start | bytes 44 | tf_op jit(solution)/shard_map/ppermute | solution.py:466
  158.7 34.2 %collective-permute-start.23 = (f32[1,1,3072]{2,1,0:T(1,128)S(1)}, f32[1,1,3072]{2,1,0:T(1,128)S(1)}, u32[]{:S(2)}, u32[]{:S(2)}) collective-permute-start(f32[1,1,3072]{2,1,0:T(1,128)S(1)} %get-tuple-element.47), channel_id=1, source_target_pairs={{0,16},{16,32},{32,48},{48,64},{64,80},{80,96},{96,112},{112,1},{1... | collective-permute-start | bytes 36872 | tf_op jit(solution)/shard_map/ppermute | solution.py:483
  160.6 32.3 %collective-permute-start.24 = (f32[1,1,3072]{2,1,0:T(1,128)S(1)}, f32[1,1,3072]{2,1,0:T(1,128)S(1)}, u32[]{:S(2)}, u32[]{:S(2)}) collective-permute-start(f32[1,1,3072]{2,1,0:T(1,128)S(1)} %get-tuple-element.48), channel_id=1, source_target_pairs={{16,0},{32,16},{48,32},{64,48},{80,64},{96,80},{112,96},{1,112},{1... | collective-permute-start | bytes 36872 | tf_op jit(solution)/shard_map/ppermute | solution.py:480
  164.9 2.4 collective-permute-start.17
  169.3 3.9 %collective-permute-start.18 = (f32[3]{0:T(128)S(1)}, f32[3]{0:T(128)S(1)}, u32[]{:S(2)}, u32[]{:S(2)}) collective-permute-start(f32[3]{0:T(128)S(1)} %fusion.49), channel_id=1, source_target_pairs={{0,64},{16,80},{32,96},{48,112},{64,0},{80,16},{96,32},{112,48},{1... | collective-permute-start | bytes 44 | tf_op jit(solution)/shard_map/ppermute | solution.py:466
  173.2 2.4 collective-permute-start.19
  175.6 3.9 %collective-permute-start.20 = (f32[3]{0:T(128)S(1)}, f32[3]{0:T(128)S(1)}, u32[]{:S(2)}, u32[]{:S(2)}) collective-permute-start(f32[3]{0:T(128)S(1)} %add.198), channel_id=1, source_target_pairs={{0,2},{1,3},{2,0},{3,1},{4,6},{5,7},{6,4},{7,5},{8,10},{9,11},{10,... | collective-permute-start | bytes 44 | tf_op jit(solution)/shard_map/ppermute | solution.py:466
  179.6 2.8 %collective-permute-start.21 = (f32[3]{0:T(128)S(1)}, f32[3]{0:T(128)S(1)}, u32[]{:S(2)}, u32[]{:S(2)}) collective-permute-start(f32[3]{0:T(128)S(1)} %add.199), channel_id=1, source_target_pairs={{0,4},{1,5},{2,6},{3,7},{4,0},{5,1},{6,2},{7,3},{8,12},{9,13},{10,... | collective-permute-start | bytes 44 | tf_op jit(solution)/shard_map/ppermute | solution.py:466
  182.3 4.0 %collective-permute-start.22 = (f32[3]{0:T(128)S(1)}, f32[3]{0:T(128)S(1)}, u32[]{:S(2)}, u32[]{:S(2)}) collective-permute-start(f32[3]{0:T(128)S(1)} %add.200), channel_id=1, source_target_pairs={{0,8},{1,9},{2,10},{3,11},{4,12},{5,13},{6,14},{7,15},{8,0},{9,1},... | collective-permute-start | bytes 44 | tf_op jit(solution)/shard_map/ppermute | solution.py:466
  196.0 12.7 %collective-permute-start.25 = (f32[3]{0:T(128)S(1)}, f32[3]{0:T(128)S(1)}, u32[]{:S(2)}, u32[]{:S(2)}) collective-permute-start(f32[3]{0:T(128)S(1)} %pad_maximum_fusion.30), channel_id=1, source_target_pairs={{0,16},{16,0},{32,48},{48,32},{64,80},{80,64},{96,112},{112,96},{1... | collective-permute-start | bytes 44 | tf_op jit(solution)/shard_map/ppermute | solution.py:466
  210.7 2.4 collective-permute-start.26
  215.2 3.9 %collective-permute-start.27 = (f32[3]{0:T(128)S(1)}, f32[3]{0:T(128)S(1)}, u32[]{:S(2)}, u32[]{:S(2)}) collective-permute-start(f32[3]{0:T(128)S(1)} %fusion.48), channel_id=1, source_target_pairs={{0,64},{16,80},{32,96},{48,112},{64,0},{80,16},{96,32},{112,48},{1... | collective-permute-start | bytes 44 | tf_op jit(solution)/shard_map/ppermute | solution.py:466
  219.1 2.4 collective-permute-start.28
  221.5 3.9 %collective-permute-start.29 = (f32[3]{0:T(128)S(1)}, f32[3]{0:T(128)S(1)}, u32[]{:S(2)}, u32[]{:S(2)}) collective-permute-start(f32[3]{0:T(128)S(1)} %add.218), channel_id=1, source_target_pairs={{0,2},{1,3},{2,0},{3,1},{4,6},{5,7},{6,4},{7,5},{8,10},{9,11},{10,... | collective-permute-start | bytes 44 | tf_op jit(solution)/shard_map/ppermute | solution.py:466
  225.5 2.6 %collective-permute-start.30 = (f32[3]{0:T(128)S(1)}, f32[3]{0:T(128)S(1)}, u32[]{:S(2)}, u32[]{:S(2)}) collective-permute-start(f32[3]{0:T(128)S(1)} %add.219), channel_id=1, source_target_pairs={{0,4},{1,5},{2,6},{3,7},{4,0},{5,1},{6,2},{7,3},{8,12},{9,13},{10,... | collective-permute-start | bytes 44 | tf_op jit(solution)/shard_map/ppermute | solution.py:466
  228.1 4.0 %collective-permute-start.31 = (f32[3]{0:T(128)S(1)}, f32[3]{0:T(128)S(1)}, u32[]{:S(2)}, u32[]{:S(2)}) collective-permute-start(f32[3]{0:T(128)S(1)} %add.220), channel_id=1, source_target_pairs={{0,8},{1,9},{2,10},{3,11},{4,12},{5,13},{6,14},{7,15},{8,0},{9,1},... | collective-permute-start | bytes 44 | tf_op jit(solution)/shard_map/ppermute | solution.py:466
